TPU v7x, 256 devices: a whole 4x4x8 slice. The times are simulated.
256 devices in a mesh: pipe: 16 (over y, z_hi), expert: 16 (over z_lo, x, core).
Axes of the slice: x: 4, y: 4, z: 8 (z_hi: 4, z_lo: 2; z = z_hi * 2 + z_lo), core: 2. Of those that a mesh axis runs over, the one named last changes fastest.
Arguments:
- up_in: bfloat16 [16, 1024, 2560], P('pipe', 'expert'), may hold values from -6 to 6
- down_in: bfloat16 [16, 1024, 2560], P('pipe', 'expert'), may hold values from -6 to 6
- up_ids: int32 [16, 1024, 6], P('pipe', 'expert'), may hold values from 0 to 15, all different within a row; in each aligned block of 64 rows (0 to 63, 64 to 127, ..., all dimensions but the last counted through in order) at most 32 rows name the same one
- down_ids: int32 [16, 1024, 6], P('pipe', 'expert'), may hold values from 0 to 15, all different within a row; in each aligned block of 64 rows (0 to 63, 64 to 127, ..., all dimensions but the last counted through in order) at most 32 rows name the same one
- norm_gain: float32 [16, 2560], P('pipe'), may hold values from 0.1 to 1.9
- router: bfloat16 [16, 2560, 16], P('pipe'), may hold values from -0.25 to 0.25
- w_up: bfloat16 [16, 16, 2560, 1152], P('pipe', 'expert'), may hold values from -0.125 to 0.125
- w_down: bfloat16 [16, 16, 1152, 2560], P('pipe', 'expert'), may hold values from -0.375 to 0.375
Outputs:
- up_out: bfloat16 [16, 1024, 2560], P('pipe', 'expert')
- down_out: bfloat16 [16, 1024, 2560], P('pipe', 'expert')
Inputs may be any that keep to these rules, and one draw needn't show every extreme that they name: `up_ids`: each token names 6 different experts. Within the tokens of one device (aligned blocks of 64 tokens of one section) no expert is named more than 32 times, and in every draw some expert is named exactly 32 times in some block. `down_ids`: as for up_ids.
All inputs are finite; a program needn't handle non-finite values.
Results may differ from a plain program's by a relative error of at most 0.0061.
Values may be sent and summed in bfloat16 or wider, within the bound.
No kernel may reach another device: no remote copies, remote signals or barrier semaphores. Data moves between devices by JAX's collectives and lax.ppermute only.
A program may use at most 128 MiB of HBM per device.

v0:
```python
import jax
import jax.numpy as jnp
from jax import lax
from jax.sharding import PartitionSpec as P

CAP = 32


def shifted(block, axis, distance):
    devices = range(lax.axis_size(axis))
    route = [((i - distance) % len(devices), i) for i in devices]
    return lax.ppermute(block, axis, route)


def layer_route(x, ids, gain, table, owners_count):
    tokens_here = x.shape[0]
    experts = table.shape[1]
    width = x.shape[1]
    choose = ids.shape[1]
    xf = x.astype(jnp.float32)
    normed = (xf * lax.rsqrt(jnp.mean(xf * xf, axis=-1, keepdims=True) + 1e-06) * gain).astype(
        jnp.bfloat16
    )
    logits = jnp.dot(normed, table, preferred_element_type=jnp.float32)
    onehot = (ids[:, :, None] == jnp.arange(experts, dtype=jnp.int32)[None, None, :]).astype(
        jnp.int32
    )
    chosen = jnp.take_along_axis(logits, ids, axis=1)
    score = jax.nn.sigmoid(chosen)
    gates = score / jnp.sum(score, axis=-1, keepdims=True)
    flat = onehot.reshape(tokens_here * choose, experts)
    before = jnp.cumsum(flat, axis=0) - flat
    slot = jnp.sum(before * flat, axis=-1)
    target = ids.reshape(-1) * CAP + slot
    token_of = jnp.arange(tokens_here * choose, dtype=jnp.int32) // choose + 1
    source_row = jnp.zeros((experts * CAP,), jnp.int32).at[target].set(token_of)
    padded = jnp.concatenate([jnp.zeros((1, width), jnp.bfloat16), normed], axis=0)
    send = jnp.take(padded, source_row, axis=0)
    send = send.reshape(owners_count, experts // owners_count, CAP, width)
    return (send, target, gates)


def apply_experts(rows, up_w, down_w):
    up_h = jnp.einsum("slcd,ldf->slcf", rows, up_w, preferred_element_type=jnp.float32)
    hidden = jax.nn.silu(up_h).astype(jnp.bfloat16)
    return jnp.einsum("slcf,lfd->slcd", hidden, down_w, preferred_element_type=jnp.float32).astype(
        jnp.bfloat16
    )


def finish(x, gates, returned, target):
    tokens_here, choose = gates.shape
    width = x.shape[1]
    picked = jnp.take(returned.reshape(-1, width), target, axis=0)
    picked = picked.reshape(tokens_here, choose, width).astype(jnp.float32)
    combined = jnp.sum(gates[:, :, None] * picked, axis=1)
    return (x.astype(jnp.float32) + 2.5 * combined).astype(jnp.bfloat16)


def per_device(up_in, down_in, up_ids, down_ids, norm_gain, router, w_up, w_down):
    owners_count = lax.axis_size("expert")
    gain = norm_gain[0]
    table = router[0]
    up_w = w_up[0]
    down_w = w_down[0]
    send_up, target_up, gates_up = layer_route(up_in[0], up_ids[0], gain, table, owners_count)
    send_down, target_down, gates_down = layer_route(
        down_in[0], down_ids[0], gain, table, owners_count
    )

    def run_single(rows):
        return lax.all_to_all(
            apply_experts(rows, up_w, down_w), "expert", split_axis=0, concat_axis=0, tiled=True
        )

    def dispatch_single(send):
        return run_single(lax.all_to_all(send, "expert", split_axis=0, concat_axis=0, tiled=True))

    back_up = dispatch_single(send_up)
    back_down = dispatch_single(send_down)
    layer_up = finish(up_in[0], gates_up, back_up, target_up)
    layer_down = finish(down_in[0], gates_down, back_down, target_down)
    up_out = shifted(layer_up[None], "pipe", 1)
    down_out = shifted(layer_down[None], "pipe", -1)
    return (up_out, down_out)


def solution(mesh):
    placed = (
        P("pipe", "expert", None),
        P("pipe", "expert", None),
        P("pipe", "expert", None),
        P("pipe", "expert", None),
        P("pipe", None),
        P("pipe", None, None),
        P("pipe", "expert", None, None),
        P("pipe", "expert", None, None),
    )
    return jax.shard_map(
        per_device,
        mesh=mesh,
        in_specs=placed,
        out_specs=(P("pipe", "expert", None), P("pipe", "expert", None)),
        check_vma=False,
    )
```

profile of v0, /device:TPU:6, one launch (start us, length us, event | category | flops | bytes accessed | tf_op | source)
XLA Modules:
  0.0 233.1 jit_solution(5851529569297065728)
XLA Ops:
  0.6 0.8 copy.48
  1.7 0.7 broadcast_multiply_fusion
  2.4 0.9 reduce-window.16
  3.3 0.2 slice_reduce_fusion
  3.9 2.9 %scatter_custom_fusion.1 = s32[512]{0:T(512)S(1)} fusion(s32[384]{0:T(512)S(1)} %fusion.91, s32[384]{0:T(512)S(1)} %fusion.86, s32[]{:T(128)} %constant.48.clone.1), kind=kCustom, calls=%fused_computation.125 | custom fusion | bytes 2052 | tf_op jit(solution)/shard_map/scatter | solution.py:36
  6.9 1.1 fusion.50
  8.0 1.1 fusion.53
  9.2 0.7 reduce
  10.0 1.3 fusion.52
  11.3 2.6 %gather_fusion.4 = bf16[512,2560]{1,0:T(8,128)(2,1)S(1)} fusion(bf16[65,2560]{1,0:T(8,128)(2,1)S(1)} %concatenate.7, s32[1024]{0:T(1024)S(1)} %pad_clamp_fusion.1), kind=kCustom, calls=%fused_computation.4.clone | custom fusion | bytes 5244928 | tf_op jit(solution)/shard_map/jit(_take)/gather | solution.py:38
  14.0 1.8 broadcast_select_fusion
  15.8 6.6 %all-to-all-start.2 = ((bf16[16,1,32,2560]{3,2,1,0:T(8,128)(2,1)}), bf16[16,1,32,2560]{3,2,1,0:T(8,128)(2,1)}, u32[]{:S(2)}, u32[]{:S(2)}) async-start(bf16[16,1,32,2560]{3,2,1,0:T(8,128)(2,1)} %bitcast.29), calls=%async_computation.2 | async-start | bytes 5242880 | tf_op jit(solution)/shard_map/all_to_all | solution.py:77
  22.7 0.9 reduce-window.14
  23.6 0.2 slice_reduce_fusion.1
  24.2 2.9 %scatter_custom_fusion = s32[512]{0:T(512)S(1)} fusion(s32[384]{0:T(512)S(1)} %fusion.90, s32[384]{0:T(512)S(1)} %fusion.86, s32[]{:T(128)} %constant.48.clone.1), kind=kCustom, calls=%fused_computation.127 | custom fusion | bytes 2052 | tf_op jit(solution)/shard_map/scatter | solution.py:36
  27.3 2.6 %gather_fusion.1 = bf16[512,2560]{1,0:T(8,128)(2,1)S(1)} fusion(bf16[65,2560]{1,0:T(8,128)(2,1)S(1)} %concatenate.6, s32[1024]{0:T(1024)S(1)} %pad_clamp_fusion.3), kind=kCustom, calls=%fused_computation.1.clone | custom fusion | bytes 5244928 | tf_op jit(solution)/shard_map/jit(_take)/gather | solution.py:38
  29.9 1.8 broadcast_select_fusion.1
  31.7 28.4 %all-to-all-done.2 = bf16[16,1,32,2560]{3,2,1,0:T(8,128)(2,1)} async-done(((bf16[16,1,32,2560]{3,2,1,0:T(8,128)(2,1)}), bf16[16,1,32,2560]{3,2,1,0:T(8,128)(2,1)}, u32[]{:S(2)}, u32[]{:S(2)}) %all-to-all-start.2) | async-done | bytes 2621472 | tf_op jit(solution)/shard_map/all_to_all | solution.py:77
  60.1 4.5 %all-to-all-start = ((bf16[16,1,32,2560]{3,2,1,0:T(8,128)(2,1)}), bf16[16,1,32,2560]{3,2,1,0:T(8,128)(2,1)S(1)}, u32[]{:S(2)}, u32[]{:S(2)}) async-start(bf16[16,1,32,2560]{3,2,1,0:T(8,128)(2,1)} %bitcast.6), calls=%async_computation | async-start | bytes 5242880 | tf_op jit(solution)/shard_map/all_to_all | solution.py:77
  64.6 7.2 %fusion.32 = bf16[16,32,1152]{2,1,0:T(8,128)(2,1)S(1)} fusion(bf16[1,1,2560,1152]{3,2,1,0:T(8,128)(2,1)} %param.20, bf16[16,1,32,2560]{3,2,1,0:T(8,128)(2,1)} %all-to-all-done.2), kind=kOutput, calls=%fused_computation.29 | convolution fusion | flops 3022848000 | bytes 9699328 | tf_op jit(solution)/shard_map/slcd,ldf->slcf/dot_general | solution.py:44
  71.8 7.5 %fusion.14 = bf16[16,1,32,2560]{3,2,1,0:T(8,128)(2,1)} fusion(bf16[16,32,1152]{2,1,0:T(8,128)(2,1)S(1)} %fusion.32, bf16[1,1,1152,2560]{3,2,1,0:T(8,128)(2,1)} %param.21), kind=kOutput, calls=%fused_computation.20 | convolution fusion | flops 3021209600 | bytes 9699328 | tf_op jit(solution)/shard_map/slcf,lfd->slcd/dot_general | solution.py:46
  79.3 22.9 %all-to-all-done = bf16[16,1,32,2560]{3,2,1,0:T(8,128)(2,1)S(1)} async-done(((bf16[16,1,32,2560]{3,2,1,0:T(8,128)(2,1)}), bf16[16,1,32,2560]{3,2,1,0:T(8,128)(2,1)S(1)}, u32[]{:S(2)}, u32[]{:S(2)}) %all-to-all-start) | async-done | bytes 2621472 | tf_op jit(solution)/shard_map/all_to_all | solution.py:77
  102.3 1.5 copy-done.4
  103.8 4.9 %all-to-all-start.3 = ((bf16[16,1,32,2560]{3,2,1,0:T(8,128)(2,1)}), bf16[16,1,32,2560]{3,2,1,0:T(8,128)(2,1)S(1)}, u32[]{:S(2)}, u32[]{:S(2)}) async-start(bf16[16,1,32,2560]{3,2,1,0:T(8,128)(2,1)} %fusion.14), calls=%async_computation.3 | async-start | bytes 5242880 | tf_op jit(solution)/shard_map/all_to_all | solution.py:72
  108.6 7.2 %fusion.41 = bf16[16,32,1152]{2,1,0:T(8,128)(2,1)S(1)} fusion(bf16[1,1,2560,1152]{3,2,1,0:T(8,128)(2,1)} %param.20, bf16[16,1,32,2560]{3,2,1,0:T(8,128)(2,1)} %copy-done.4), kind=kOutput, calls=%fused_computation.31 | convolution fusion | flops 3022848000 | bytes 9699328 | tf_op jit(solution)/shard_map/slcd,ldf->slcf/dot_general | solution.py:44
  115.8 7.6 %fusion.17 = bf16[16,1,32,2560]{3,2,1,0:T(8,128)(2,1)} fusion(bf16[16,32,1152]{2,1,0:T(8,128)(2,1)S(1)} %fusion.41, bf16[1,1,1152,2560]{3,2,1,0:T(8,128)(2,1)} %param.21), kind=kOutput, calls=%fused_computation.21 | convolution fusion | flops 3021209600 | bytes 9699328 | tf_op jit(solution)/shard_map/slcf,lfd->slcd/dot_general | solution.py:46
  123.4 22.9 %all-to-all-done.3 = bf16[16,1,32,2560]{3,2,1,0:T(8,128)(2,1)S(1)} async-done(((bf16[16,1,32,2560]{3,2,1,0:T(8,128)(2,1)}), bf16[16,1,32,2560]{3,2,1,0:T(8,128)(2,1)S(1)}, u32[]{:S(2)}, u32[]{:S(2)}) %all-to-all-start.3) | async-done | bytes 2621472 | tf_op jit(solution)/shard_map/all_to_all | solution.py:72
  146.3 1.5 copy-done.1
  147.8 4.9 %all-to-all-start.1 = ((bf16[16,1,32,2560]{3,2,1,0:T(8,128)(2,1)}), bf16[16,1,32,2560]{3,2,1,0:T(8,128)(2,1)S(1)}, u32[]{:S(2)}, u32[]{:S(2)}) async-start(bf16[16,1,32,2560]{3,2,1,0:T(8,128)(2,1)} %fusion.17), calls=%async_computation.1 | async-start | bytes 5242880 | tf_op jit(solution)/shard_map/all_to_all | solution.py:72
  152.9 0.3 fusion.63
  153.2 3.0 %gather_fusion.3 = f32[384]{0:T(512)S(1)} fusion(f32[64,16]{0,1:T(8,128)S(1)} %fusion.63, s32[384]{0:T(512)S(1)} %reshape.333), kind=kCustom, calls=%fused_computation.3.clone | custom fusion | bytes 6144 | tf_op jit(solution)/shard_map/jit(take_along_axis)/gather | solution.py:28
  156.8 0.3 fusion.66
  157.1 3.0 %gather_fusion = f32[384]{0:T(512)S(1)} fusion(f32[64,16]{0,1:T(8,128)S(1)} %fusion.66, s32[384]{0:T(512)S(1)} %reshape.324), kind=kCustom, calls=%fused_computation.clone | custom fusion | bytes 6144 | tf_op jit(solution)/shard_map/jit(take_along_axis)/gather | solution.py:28
  160.5 7.9 %gather_fusion.5 = bf16[384,2560]{1,0:T(8,128)(2,1)} fusion(bf16[512,2560]{1,0:T(8,128)(2,1)} %bitcast.206, s32[1024]{0:T(1024)S(1)} %pad_clamp_fusion), kind=kCustom, calls=%fused_computation.5.clone | custom fusion | bytes 3933696 | tf_op jit(solution)/shard_map/jit(_take)/gather | solution.py:54
  168.4 3.8 %select_convert_fusion = f32[384,2560]{1,0:T(8,128)} fusion(bf16[384,2560]{1,0:T(8,128)(2,1)} %gather_fusion.5, pred[384]{0:T(512)(128)(4,1)S(1)} %get-tuple-element.4), kind=kLoop, calls=%fused_computation.32 | loop fusion | flops 1966080 | bytes 5898624 | tf_op jit(solution)/shard_map/convert_element_type | solution.py:55
  172.3 5.1 %reshape.248 = f32[64,6,2560]{2,1,0:T(8,128)} reshape(f32[384,2560]{1,0:T(8,128)} %select_convert_fusion) | data formatting | bytes 7864320 | tf_op jit(solution)/shard_map/convert_element_type | solution.py:55
  177.3 4.4 %multiply_reduce_fusion = f32[64,2560]{1,0:T(8,128)S(1)} fusion(f32[64,6,2560]{2,1,0:T(8,128)} %reshape.248, f32[64,6]{1,0:T(8,128)S(1)} %copy.47), kind=kLoop, calls=%fused_computation.16 | loop fusion | flops 1802240 | bytes 4589056 | tf_op jit(solution)/shard_map/reduce_sum | solution.py:56
  181.8 0.8 fusion.61
  182.6 7.9 %collective-permute-start.1 = (bf16[1,64,2560]{2,1,0:T(8,128)(2,1)}, bf16[1,64,2560]{2,1,0:T(8,128)(2,1)S(1)}, u32[]{:S(2)}, u32[]{:S(2)}) collective-permute-start(bf16[1,64,2560]{2,1,0:T(8,128)(2,1)} %fusion.61), channel_id=1, source_target_pairs={{16,0},{32,16},{48,32},{64,48},{80,64},{96,80},{112,96},{128,112},... | collective-permute-start | bytes 983048 | tf_op jit(solution)/shard_map/ppermute | solution.py:12
  190.5 6.8 %all-to-all-done.1 = bf16[16,1,32,2560]{3,2,1,0:T(8,128)(2,1)S(1)} async-done(((bf16[16,1,32,2560]{3,2,1,0:T(8,128)(2,1)}), bf16[16,1,32,2560]{3,2,1,0:T(8,128)(2,1)S(1)}, u32[]{:S(2)}, u32[]{:S(2)}) %all-to-all-start.1) | async-done | bytes 2621472 | tf_op jit(solution)/shard_map/all_to_all | solution.py:72
  197.3 3.3 %gather_fusion.2 = bf16[384,2560]{1,0:T(8,128)(2,1)} fusion(bf16[512,2560]{1,0:T(8,128)(2,1)S(1)} %bitcast.205, s32[1024]{0:T(1024)S(1)} %pad_clamp_fusion.2), kind=kCustom, calls=%fused_computation.2.clone | custom fusion | bytes 3933696 | tf_op jit(solution)/shard_map/jit(_take)/gather | solution.py:54
  200.6 3.8 %select_convert_fusion.1 = f32[384,2560]{1,0:T(8,128)} fusion(bf16[384,2560]{1,0:T(8,128)(2,1)} %gather_fusion.2, pred[384]{0:T(512)(128)(4,1)S(1)} %get-tuple-element.7), kind=kLoop, calls=%fused_computation.33 | loop fusion | flops 1966080 | bytes 5898624 | tf_op jit(solution)/shard_map/convert_element_type | solution.py:55
  204.4 5.1 %reshape.246 = f32[64,6,2560]{2,1,0:T(8,128)} reshape(f32[384,2560]{1,0:T(8,128)} %select_convert_fusion.1) | data formatting | bytes 7864320 | tf_op jit(solution)/shard_map/convert_element_type | solution.py:55
  209.5 4.4 %multiply_reduce_fusion.1 = f32[64,2560]{1,0:T(8,128)S(1)} fusion(f32[64,6,2560]{2,1,0:T(8,128)} %reshape.246, f32[64,6]{1,0:T(8,128)S(1)} %copy.38), kind=kLoop, calls=%fused_computation.17 | loop fusion | flops 1802240 | bytes 4589056 | tf_op jit(solution)/shard_map/reduce_sum | solution.py:56
  214.0 3.4 %collective-permute-start = (bf16[1,64,2560]{2,1,0:T(8,128)(2,1)S(1)}, bf16[1,64,2560]{2,1,0:T(8,128)(2,1)S(1)}, u32[]{:S(2)}, u32[]{:S(2)}) collective-permute-start(bf16[1,64,2560]{2,1,0:T(8,128)(2,1)S(1)} %fusion.58), channel_id=1, source_target_pairs={{240,0},{0,16},{16,32},{32,48},{48,64},{64,80},{80,96},{96,112},{1... | collective-permute-start | bytes 983048 | tf_op jit(solution)/shard_map/ppermute | solution.py:12
  217.4 14.2 %collective-permute-done = bf16[1,64,2560]{2,1,0:T(8,128)(2,1)S(1)} collective-permute-done((bf16[1,64,2560]{2,1,0:T(8,128)(2,1)S(1)}, bf16[1,64,2560]{2,1,0:T(8,128)(2,1)S(1)}, u32[]{:S(2)}, u32[]{:S(2)}) %collective-permute-start) | collective-permute-done | bytes 327712 | tf_op jit(solution)/shard_map/ppermute | solution.py:12
  231.6 0.7 copy.80
  232.3 0.7 copy.81
  (62 shorter events, 3.0 us)
Async XLA Ops:
  0.6 152.3 %copy-start = (bf16[1,2560,16]{1,2,0:T(8,128)(2,1)S(1)}, bf16[1,2560,16]{1,2,0:T(8,128)(2,1)}, u32[]{:S(2)}) copy-start(bf16[1,2560,16]{1,2,0:T(8,128)(2,1)} %param.19) | copy-start | bytes 245764
  15.8 6.6 %copy-start.6 = (s32[1,64,6]{1,0,2:T(1,128)S(1)}, s32[1,64,6]{1,0,2:T(1,128)}, u32[]{:S(2)}) copy-start(s32[1,64,6]{1,0,2:T(1,128)} %param.16) | copy-start | bytes 4612
  15.8 44.3 %all-to-all-start.2 = ((bf16[16,1,32,2560]{3,2,1,0:T(8,128)(2,1)}), bf16[16,1,32,2560]{3,2,1,0:T(8,128)(2,1)}, u32[]{:S(2)}, u32[]{:S(2)}) async-start(bf16[16,1,32,2560]{3,2,1,0:T(8,128)(2,1)} %bitcast.29), calls=%async_computation.2 | async-start | bytes 5242880 | tf_op jit(solution)/shard_map/all_to_all | solution.py:77
  60.1 42.2 %all-to-all-start = ((bf16[16,1,32,2560]{3,2,1,0:T(8,128)(2,1)}), bf16[16,1,32,2560]{3,2,1,0:T(8,128)(2,1)S(1)}, u32[]{:S(2)}, u32[]{:S(2)}) async-start(bf16[16,1,32,2560]{3,2,1,0:T(8,128)(2,1)} %bitcast.6), calls=%async_computation | async-start | bytes 5242880 | tf_op jit(solution)/shard_map/all_to_all | solution.py:77
  102.3 1.5 copy-start.4
  103.8 42.5 %all-to-all-start.3 = ((bf16[16,1,32,2560]{3,2,1,0:T(8,128)(2,1)}), bf16[16,1,32,2560]{3,2,1,0:T(8,128)(2,1)S(1)}, u32[]{:S(2)}, u32[]{:S(2)}) async-start(bf16[16,1,32,2560]{3,2,1,0:T(8,128)(2,1)} %fusion.14), calls=%async_computation.3 | async-start | bytes 5242880 | tf_op jit(solution)/shard_map/all_to_all | solution.py:72
  123.4 29.2 %copy-start.5 = (s32[1,64,6]{1,0,2:T(1,128)S(1)}, s32[1,64,6]{1,0,2:T(1,128)}, u32[]{:S(2)}) copy-start(s32[1,64,6]{1,0,2:T(1,128)} %param.17) | copy-start | bytes 4612
  123.4 29.5 %copy-start.2 = (bf16[1,64,2560]{2,1,0:T(8,128)(2,1)S(1)}, bf16[1,64,2560]{2,1,0:T(8,128)(2,1)}, u32[]{:S(2)}) copy-start(bf16[1,64,2560]{2,1,0:T(8,128)(2,1)} %param.15) | copy-start | bytes 983044
  146.3 1.5 copy-start.1
  147.8 49.5 %all-to-all-start.1 = ((bf16[16,1,32,2560]{3,2,1,0:T(8,128)(2,1)}), bf16[16,1,32,2560]{3,2,1,0:T(8,128)(2,1)S(1)}, u32[]{:S(2)}, u32[]{:S(2)}) async-start(bf16[16,1,32,2560]{3,2,1,0:T(8,128)(2,1)} %fusion.17), calls=%async_computation.1 | async-start | bytes 5242880 | tf_op jit(solution)/shard_map/all_to_all | solution.py:72
  153.2 3.6 %copy-start.3 = (bf16[1,64,2560]{2,1,0:T(8,128)(2,1)S(1)}, bf16[1,64,2560]{2,1,0:T(8,128)(2,1)}, u32[]{:S(2)}) copy-start(bf16[1,64,2560]{2,1,0:T(8,128)(2,1)} %param.14) | copy-start | bytes 983044
  182.6 34.8 %collective-permute-start.1 = (bf16[1,64,2560]{2,1,0:T(8,128)(2,1)}, bf16[1,64,2560]{2,1,0:T(8,128)(2,1)S(1)}, u32[]{:S(2)}, u32[]{:S(2)}) collective-permute-start(bf16[1,64,2560]{2,1,0:T(8,128)(2,1)} %fusion.61), channel_id=1, source_target_pairs={{16,0},{32,16},{48,32},{64,48},{80,64},{96,80},{112,96},{128,112},... | collective-permute-start | bytes 983048 | tf_op jit(solution)/shard_map/ppermute | solution.py:12
  214.0 17.6 %collective-permute-start = (bf16[1,64,2560]{2,1,0:T(8,128)(2,1)S(1)}, bf16[1,64,2560]{2,1,0:T(8,128)(2,1)S(1)}, u32[]{:S(2)}, u32[]{:S(2)}) collective-permute-start(bf16[1,64,2560]{2,1,0:T(8,128)(2,1)S(1)} %fusion.58), channel_id=1, source_target_pairs={{240,0},{0,16},{16,32},{32,48},{48,64},{64,80},{80,96},{96,112},{1... | collective-permute-start | bytes 983048 | tf_op jit(solution)/shard_map/ppermute | solution.py:12
where the time goes:
time: 234 us; the launch traced here: 233 us
  waiting for transfers between devices  95.2 us (41%)
  local copies, waits for them, and re-layouts  46.5 us (20%)
  starting transfers between devices  32 us (14%)
  matrix products  30 us (13%)
  other arithmetic  28.4 us (12%)
    all_to_all x2, waiting for transfers between devices, dispatch_single(): lax.all_to_all(send, 'expert', split_axis=0, concat_axis=0, tiled=True)  51.3 us
    all_to_all x2, waiting for transfers between devices, run_single(): lax.all_to_all(apply_experts(rows, up_w, down_w), 'expert', split_axis=0,...  29.7 us
    dot_general x2, matrix products, apply_experts(): jnp.einsum('slcf,lfd->slcd', hidden, down_w, preferred_element_type=jnp.f...  15.1 us
    dot_general x2, matrix products, apply_experts(): jnp.einsum('slcd,ldf->slcf', rows, up_w, preferred_element_type=jnp.float32)  14.3 us
    ppermute x2, waiting for transfers between devices, shifted(): return lax.ppermute(block, axis, route)  14.2 us
    gather x2, local copies, waits for them, and re-layouts, finish(): picked = jnp.take(returned.reshape(-1, width), target, axis=0)  11.2 us
    ppermute x2, starting transfers between devices, shifted(): return lax.ppermute(block, axis, route)  11.2 us
    all_to_all x2, starting transfers between devices, dispatch_single(): lax.all_to_all(send, 'expert', split_axis=0, concat_axis=0, tiled=True)  11.1 us
  transfers between devices with their start and end apart: 6, of which 5 were waited for; matrix products, arithmetic and copies ran while one was open for 37% of the time, Pallas kernels for 0%

commit v1 on v0

v1 whole, which is shorter than its diff:
```python
import jax
import jax.numpy as jnp
from jax import lax
from jax.sharding import PartitionSpec as P

CAP = 32


def shifted(block, axis, distance):
    devices = range(lax.axis_size(axis))
    route = [((i - distance) % len(devices), i) for i in devices]
    return lax.ppermute(block, axis, route)


def layer_route(x, ids, gain, table):
    tokens_here = x.shape[0]
    experts = table.shape[1]
    choose = ids.shape[1]
    xf = x.astype(jnp.float32)
    normed = (xf * lax.rsqrt(jnp.mean(xf * xf, axis=-1, keepdims=True) + 1e-06) * gain).astype(
        jnp.bfloat16
    )
    logits = jnp.dot(normed, table, preferred_element_type=jnp.float32)
    chosen = jnp.take_along_axis(logits, ids, axis=1)
    score = jax.nn.sigmoid(chosen)
    gates = score / jnp.sum(score, axis=-1, keepdims=True)
    onehot = (ids[:, :, None] == jnp.arange(experts, dtype=jnp.int32)[None, None, :]).astype(
        jnp.int32
    )
    flat = onehot.reshape(tokens_here * choose, experts)
    before = jnp.cumsum(flat, axis=0) - flat
    slot = jnp.sum(before * flat, axis=-1).reshape(tokens_here, choose)
    target = ids * CAP + slot
    rows = jnp.arange(experts * CAP, dtype=jnp.int32)
    hit = target[:, :, None] == rows[None, None, :]
    place = jnp.any(hit, axis=1).astype(jnp.bfloat16)
    send = lax.dot_general(
        place, normed, (((0,), (0,)), ((), ())), preferred_element_type=jnp.float32
    ).astype(jnp.bfloat16)
    weight = jnp.sum(jnp.where(hit, gates[:, :, None], 0.0), axis=1)
    weight_hi = weight.astype(jnp.bfloat16)
    weight_lo = (weight - weight_hi.astype(jnp.float32)).astype(jnp.bfloat16)
    return (send, weight_hi, weight_lo)


def apply_experts(rows, up_w, down_w):
    up_h = jnp.dot(rows, up_w, preferred_element_type=jnp.float32)
    hidden = jax.nn.silu(up_h).astype(jnp.bfloat16)
    return jnp.dot(hidden, down_w, preferred_element_type=jnp.float32).astype(jnp.bfloat16)


def finish(x, weight_hi, weight_lo, returned):
    combined = jnp.dot(weight_hi, returned, preferred_element_type=jnp.float32) + jnp.dot(
        weight_lo, returned, preferred_element_type=jnp.float32
    )
    return (x.astype(jnp.float32) + 2.5 * combined).astype(jnp.bfloat16)


def exchange(block):
    return lax.all_to_all(block, "expert", split_axis=0, concat_axis=0, tiled=True)


def per_device(up_in, down_in, up_ids, down_ids, norm_gain, router, w_up, w_down):
    gain = norm_gain[0]
    table = router[0]
    up_w = w_up[0, 0]
    down_w = w_down[0, 0]
    send_up, hi_up, lo_up = layer_route(up_in[0], up_ids[0], gain, table)
    send_down, hi_down, lo_down = layer_route(down_in[0], down_ids[0], gain, table)
    rows_up = exchange(send_up)
    rows_down = exchange(send_down)
    back_up = exchange(apply_experts(rows_up, up_w, down_w))
    back_down = exchange(apply_experts(rows_down, up_w, down_w))
    layer_up = finish(up_in[0], hi_up, lo_up, back_up)
    up_out = shifted(layer_up[None], "pipe", 1)
    layer_down = finish(down_in[0], hi_down, lo_down, back_down)
    down_out = shifted(layer_down[None], "pipe", -1)
    return (up_out, down_out)


def solution(mesh):
    placed = (
        P("pipe", "expert", None),
        P("pipe", "expert", None),
        P("pipe", "expert", None),
        P("pipe", "expert", None),
        P("pipe", None),
        P("pipe", None, None),
        P("pipe", "expert", None, None),
        P("pipe", "expert", None, None),
    )
    return jax.shard_map(
        per_device,
        mesh=mesh,
        in_specs=placed,
        out_specs=(P("pipe", "expert", None), P("pipe", "expert", None)),
        check_vma=False,
    )
```

time: 234 us -> 208 us (0.89)
  local copies, waits for them, and re-layouts: 46.5 us -> 12.2 us
  other arithmetic: 28.4 us -> 5.62 us
  waiting for transfers between devices: 95.2 us -> 117 us
  matrix products: 30 us -> 39.8 us
    all_to_all x4, waiting for transfers between devices: 81 us -> 102 us  [exchange(): lax.all_to_all(block, 'expert', split_axis=0, concat_axis=0, tiled=True)]
    gather x4 -> x0, local copies, waits for them, and re-layouts: 16.5 us -> none  [the longest x2 11.2 us: finish(): picked = jnp.take(returned.reshape(-1, width), target, axis=0)]
    convert_element_type x2 -> x0, local copies, waits for them, and re-layouts: 10.1 us -> none  [finish(): picked = picked.reshape(tokens_here, choose, width).astype(jnp.float32)]
    dot_general x4 -> x8, matrix products: 29.5 us -> 39.3 us  [the longest x2 28.4 us: apply_experts(): jnp.dot(hidden, down_w, preferred_element_type=jnp.float32)]
    convert_element_type x5 -> x0, other arithmetic: 9.82 us -> none  [the longest x2 7.64 us: finish(): picked = picked.reshape(tokens_here, choose, width).astype(jnp.float32)]
    reduce_sum x4, other arithmetic: 9.08 us -> 0.54 us  [the longest x2 0.35 us: layer_route(): weight = jnp.sum(jnp.where(hit, gates[:, :, None], 0.0), axis=1)]
    scatter x2 -> x0, local copies, waits for them, and re-layouts: 5.83 us -> none  [layer_route(): source_row = jnp.zeros((experts * CAP,), jnp.int32).at[target].set(token_of)]
    select_n x6 -> x0, other arithmetic: 3.7 us -> none  [the longest x4 3.65 us: layer_route(): send = jnp.take(padded, source_row, axis=0)]
  transfers between devices with their start and end apart: 6 -> 6, of which waited for: 5 -> 6; matrix products, arithmetic and copies ran while one was open for 37% -> 22% of each run, Pallas kernels for 0% -> 0%
where the time goes in v1:
time: 208 us; the launch traced here: 207 us
  waiting for transfers between devices  117 us (56%)
  matrix products  39.8 us (19%)
  starting transfers between devices  32.1 us (15%)
  local copies, waits for them, and re-layouts  12.2 us (6%)
  other arithmetic  5.62 us (3%)
    all_to_all x4, waiting for transfers between devices, exchange(): lax.all_to_all(block, 'expert', split_axis=0, concat_axis=0, tiled=True)  102 us
    dot_general x2, matrix products, apply_experts(): jnp.dot(hidden, down_w, preferred_element_type=jnp.float32)  28.4 us
    all_to_all x4, starting transfers between devices, exchange(): lax.all_to_all(block, 'expert', split_axis=0, concat_axis=0, tiled=True)  20.9 us
    ppermute x2, waiting for transfers between devices, shifted(): return lax.ppermute(block, axis, route)  14.5 us
    ppermute x2, starting transfers between devices, shifted(): return lax.ppermute(block, axis, route)  11.2 us
    gather x10, local copies, waits for them, and re-layouts, layer_route(): chosen = jnp.take_along_axis(logits, ids, axis=1)  6.85 us
    dot_general x2, matrix products, layer_route(): lax.dot_general(place, normed, (((0,), (0,)), ((), ())), preferred_elemen...  5.85 us
  transfers between devices with their start and end apart: 6, of which 6 were waited for; matrix products, arithmetic and copies ran while one was open for 22% of the time, Pallas kernels for 0%

profile of v1, /device:TPU:6, one launch (start us, length us, event | category | flops | bytes accessed | tf_op | source)
XLA Modules:
  0.0 207.5 jit_solution(17033683474460195873)
XLA Ops:
  0.6 0.8 copy.34
  1.5 0.1 eq.78
  1.6 0.1 eq.82
  1.7 0.9 reduce-window.14
  2.6 0.2 slice_reduce_fusion.1
  3.0 0.1 reshape.135
  3.2 0.7 fusion.79
  3.9 0.2 fusion.31
  4.1 1.1 fusion.36
  5.2 0.7 reduce.1
  6.0 3.4 %convolution_convert_fusion.1 = bf16[512,2560]{1,0:T(8,128)(2,1)} fusion(pred[64,512]{1,0:T(8,128)(4,1)S(1)} %fusion.31, bf16[1,64,2560]{2,1,0:T(8,128)(2,1)} %param.10, f32[2560]{0:T(1024)S(1)} %reduce.1, f32[64]{0:T(128)S(1)} %add_rsqrt_fusion.1), kind=kOutput, calls=%fused_computation.13 | convolution fusion | flops 169738240 | bytes 2992384 | tf_op jit(solution)/shard_map/dot_general | solution.py:37
  9.4 6.3 %all-to-all-start = ((bf16[16,32,2560]{2,1,0:T(8,128)(2,1)}), bf16[16,32,2560]{2,1,0:T(8,128)(2,1)S(1)}, u32[]{:S(2)}, u32[]{:S(2)}) async-start(bf16[16,32,2560]{2,1,0:T(8,128)(2,1)} %bitcast.5), calls=%async_computation | async-start | bytes 5242880 | tf_op jit(solution)/shard_map/all_to_all | solution.py:60
  15.8 0.1 eq.89
  15.9 0.1 eq.93
  16.1 0.9 reduce-window.16
  16.9 0.2 slice_reduce_fusion
  17.3 0.1 reshape.137
  17.5 0.2 fusion.30
  17.7 0.2 fusion.41
  17.9 2.4 %convolution_convert_fusion = bf16[512,2560]{1,0:T(8,128)(2,1)} fusion(pred[64,512]{1,0:T(8,128)(4,1)S(1)} %fusion.30, bf16[1,64,2560]{2,1,0:T(8,128)(2,1)S(1)} %copy-done.4, f32[64]{0:T(128)S(1)} %add_rsqrt_fusion, f32[2560]{0:T(1024)S(1)} %reduce.1), kind=kOutput, calls=%fused_computation.12 | convolution fusion | flops 169738240 | bytes 2992384 | tf_op jit(solution)/shard_map/dot_general | solution.py:37
  20.3 33.0 %all-to-all-done = bf16[16,32,2560]{2,1,0:T(8,128)(2,1)S(1)} async-done(((bf16[16,32,2560]{2,1,0:T(8,128)(2,1)}), bf16[16,32,2560]{2,1,0:T(8,128)(2,1)S(1)}, u32[]{:S(2)}, u32[]{:S(2)}) %all-to-all-start) | async-done | bytes 2621472 | tf_op jit(solution)/shard_map/all_to_all | solution.py:60
  53.3 4.9 %all-to-all-start.2 = ((bf16[16,32,2560]{2,1,0:T(8,128)(2,1)}), bf16[16,32,2560]{2,1,0:T(8,128)(2,1)}, u32[]{:S(2)}, u32[]{:S(2)}) async-start(bf16[16,32,2560]{2,1,0:T(8,128)(2,1)} %bitcast.16), calls=%async_computation.2 | async-start | bytes 5242880 | tf_op jit(solution)/shard_map/all_to_all | solution.py:60
  58.2 13.8 %fusion.8 = bf16[512,2560]{1,0:T(8,128)(2,1)} fusion(bf16[1,1,1152,2560]{3,2,1,0:T(8,128)(2,1)} %param.17, bf16[512,2560]{1,0:T(8,128)(2,1)S(1)} %bitcast.162, bf16[1,1,2560,1152]{3,2,1,0:T(8,128)(2,1)} %param.16), kind=kOutput, calls=%fused_computation.10 | convolution fusion | flops 6044057600 | bytes 17039360 | tf_op jit(solution)/shard_map/dot_general | solution.py:49
  72.0 23.9 %all-to-all-done.2 = bf16[16,32,2560]{2,1,0:T(8,128)(2,1)} async-done(((bf16[16,32,2560]{2,1,0:T(8,128)(2,1)}), bf16[16,32,2560]{2,1,0:T(8,128)(2,1)}, u32[]{:S(2)}, u32[]{:S(2)}) %all-to-all-start.2) | async-done | bytes 2621472 | tf_op jit(solution)/shard_map/all_to_all | solution.py:60
  95.9 4.9 %all-to-all-start.1 = ((bf16[16,32,2560]{2,1,0:T(8,128)(2,1)}), bf16[16,32,2560]{2,1,0:T(8,128)(2,1)S(1)}, u32[]{:S(2)}, u32[]{:S(2)}) async-start(bf16[16,32,2560]{2,1,0:T(8,128)(2,1)} %bitcast.163), calls=%async_computation.1 | async-start | bytes 5242880 | tf_op jit(solution)/shard_map/all_to_all | solution.py:60
  100.7 14.6 %fusion.11 = bf16[512,2560]{1,0:T(8,128)(2,1)} fusion(bf16[1,1,1152,2560]{3,2,1,0:T(8,128)(2,1)} %param.17, bf16[512,2560]{1,0:T(8,128)(2,1)} %bitcast.17, bf16[1,1,2560,1152]{3,2,1,0:T(8,128)(2,1)} %param.16), kind=kOutput, calls=%fused_computation.11 | convolution fusion | flops 6044057600 | bytes 17039360 | tf_op jit(solution)/shard_map/dot_general | solution.py:49
  115.3 23.0 %all-to-all-done.1 = bf16[16,32,2560]{2,1,0:T(8,128)(2,1)S(1)} async-done(((bf16[16,32,2560]{2,1,0:T(8,128)(2,1)}), bf16[16,32,2560]{2,1,0:T(8,128)(2,1)S(1)}, u32[]{:S(2)}, u32[]{:S(2)}) %all-to-all-start.1) | async-done | bytes 2621472 | tf_op jit(solution)/shard_map/all_to_all | solution.py:60
  138.4 1.5 copy-done.1
  139.9 4.9 %all-to-all-start.3 = ((bf16[16,32,2560]{2,1,0:T(8,128)(2,1)}), bf16[16,32,2560]{2,1,0:T(8,128)(2,1)S(1)}, u32[]{:S(2)}, u32[]{:S(2)}) async-start(bf16[16,32,2560]{2,1,0:T(8,128)(2,1)} %bitcast.161), calls=%async_computation.3 | async-start | bytes 5242880 | tf_op jit(solution)/shard_map/all_to_all | solution.py:60
  144.9 0.1 reshape.164
  145.0 0.3 fusion.51
  145.3 3.0 %gather_fusion = f32[384]{0:T(512)S(1)} fusion(f32[64,16]{0,1:T(8,128)S(1)} %fusion.51, s32[384]{0:T(512)S(1)} %reshape.164), kind=kCustom, calls=%fused_computation.clone | custom fusion | bytes 6144 | tf_op jit(solution)/shard_map/jit(take_along_axis)/gather | solution.py:24
  148.6 0.1 reshape.169
  148.8 0.3 fusion.47
  149.0 3.0 %gather_fusion.1 = f32[384]{0:T(512)S(1)} fusion(f32[64,16]{0,1:T(8,128)S(1)} %fusion.47, s32[384]{0:T(512)S(1)} %reshape.169), kind=kCustom, calls=%fused_computation.1.clone | custom fusion | bytes 6144 | tf_op jit(solution)/shard_map/jit(take_along_axis)/gather | solution.py:24
  152.3 0.2 select_reduce_fusion.1
  152.5 0.2 select_reduce_fusion
  152.7 2.5 %fusion.68 = f32[64,2560]{1,0:T(8,128)S(1)} fusion(bf16[512,2560]{1,0:T(8,128)(2,1)} %bitcast.159, f32[64,512]{1,0:T(8,128)S(1)} %select_reduce_fusion.1), kind=kOutput, calls=%fused_computation.70 | convolution fusion | flops 167804928 | bytes 3407872 | tf_op jit(solution)/shard_map/dot_general | solution.py:53
  155.3 1.3 fusion.20
  156.6 3.3 %collective-permute-start = (bf16[1,64,2560]{2,1,0:T(8,128)(2,1)}, bf16[1,64,2560]{2,1,0:T(8,128)(2,1)S(1)}, u32[]{:S(2)}, u32[]{:S(2)}) collective-permute-start(bf16[1,64,2560]{2,1,0:T(8,128)(2,1)} %fusion.20), channel_id=1, source_target_pairs={{240,0},{0,16},{16,32},{32,48},{48,64},{64,80},{80,96},{96,112},{1... | collective-permute-start | bytes 983048 | tf_op jit(solution)/shard_map/ppermute | solution.py:12
  159.9 22.5 %all-to-all-done.3 = bf16[16,32,2560]{2,1,0:T(8,128)(2,1)S(1)} async-done(((bf16[16,32,2560]{2,1,0:T(8,128)(2,1)}), bf16[16,32,2560]{2,1,0:T(8,128)(2,1)S(1)}, u32[]{:S(2)}, u32[]{:S(2)}) %all-to-all-start.3) | async-done | bytes 2621472 | tf_op jit(solution)/shard_map/all_to_all | solution.py:60
  182.4 0.6 fusion.65
  183.0 0.6 fusion.21
  183.6 7.9 %collective-permute-start.1 = (bf16[1,64,2560]{2,1,0:T(8,128)(2,1)S(1)}, bf16[1,64,2560]{2,1,0:T(8,128)(2,1)S(1)}, u32[]{:S(2)}, u32[]{:S(2)}) collective-permute-start(bf16[1,64,2560]{2,1,0:T(8,128)(2,1)S(1)} %fusion.21), channel_id=1, source_target_pairs={{16,0},{32,16},{48,32},{64,48},{80,64},{96,80},{112,96},{128,112},... | collective-permute-start | bytes 983048 | tf_op jit(solution)/shard_map/ppermute | solution.py:12
  191.5 5.3 %collective-permute-done = bf16[1,64,2560]{2,1,0:T(8,128)(2,1)S(1)} collective-permute-done((bf16[1,64,2560]{2,1,0:T(8,128)(2,1)}, bf16[1,64,2560]{2,1,0:T(8,128)(2,1)S(1)}, u32[]{:S(2)}, u32[]{:S(2)}) %collective-permute-start) | collective-permute-done | bytes 327712 | tf_op jit(solution)/shard_map/ppermute | solution.py:12
  196.8 9.3 %collective-permute-done.1 = bf16[1,64,2560]{2,1,0:T(8,128)(2,1)S(1)} collective-permute-done((bf16[1,64,2560]{2,1,0:T(8,128)(2,1)S(1)}, bf16[1,64,2560]{2,1,0:T(8,128)(2,1)S(1)}, u32[]{:S(2)}, u32[]{:S(2)}) %collective-permute-start.1) | collective-permute-done | bytes 327712 | tf_op jit(solution)/shard_map/ppermute | solution.py:12
  206.0 0.7 copy.78
  206.7 0.7 copy.79
  (37 shorter events, 1.3 us)
Async XLA Ops:
  0.6 144.4 %copy-start = (bf16[1,2560,16]{1,2,0:T(8,128)(2,1)S(1)}, bf16[1,2560,16]{1,2,0:T(8,128)(2,1)}, u32[]{:S(2)}) copy-start(bf16[1,2560,16]{1,2,0:T(8,128)(2,1)} %param.15) | copy-start | bytes 245764
  9.4 6.3 %copy-start.6 = (s32[1,64,6]{1,0,2:T(1,128)S(1)}, s32[1,64,6]{1,0,2:T(1,128)}, u32[]{:S(2)}) copy-start(s32[1,64,6]{1,0,2:T(1,128)} %param.13) | copy-start | bytes 4612
  9.4 8.3 %copy-start.4 = (bf16[1,64,2560]{2,1,0:T(8,128)(2,1)S(1)}, bf16[1,64,2560]{2,1,0:T(8,128)(2,1)}, u32[]{:S(2)}) copy-start(bf16[1,64,2560]{2,1,0:T(8,128)(2,1)} %param.11) | copy-start | bytes 983044
  9.4 43.9 %all-to-all-start = ((bf16[16,32,2560]{2,1,0:T(8,128)(2,1)}), bf16[16,32,2560]{2,1,0:T(8,128)(2,1)S(1)}, u32[]{:S(2)}, u32[]{:S(2)}) async-start(bf16[16,32,2560]{2,1,0:T(8,128)(2,1)} %bitcast.5), calls=%async_computation | async-start | bytes 5242880 | tf_op jit(solution)/shard_map/all_to_all | solution.py:60
  53.3 42.6 %all-to-all-start.2 = ((bf16[16,32,2560]{2,1,0:T(8,128)(2,1)}), bf16[16,32,2560]{2,1,0:T(8,128)(2,1)}, u32[]{:S(2)}, u32[]{:S(2)}) async-start(bf16[16,32,2560]{2,1,0:T(8,128)(2,1)} %bitcast.16), calls=%async_computation.2 | async-start | bytes 5242880 | tf_op jit(solution)/shard_map/all_to_all | solution.py:60
  95.9 42.5 %all-to-all-start.1 = ((bf16[16,32,2560]{2,1,0:T(8,128)(2,1)}), bf16[16,32,2560]{2,1,0:T(8,128)(2,1)S(1)}, u32[]{:S(2)}, u32[]{:S(2)}) async-start(bf16[16,32,2560]{2,1,0:T(8,128)(2,1)} %bitcast.163), calls=%async_computation.1 | async-start | bytes 5242880 | tf_op jit(solution)/shard_map/all_to_all | solution.py:60
  138.4 1.5 copy-start.1
  138.4 6.4 %copy-start.5 = (s32[1,64,6]{1,0,2:T(1,128)S(1)}, s32[1,64,6]{1,0,2:T(1,128)}, u32[]{:S(2)}) copy-start(s32[1,64,6]{1,0,2:T(1,128)} %param.12) | copy-start | bytes 4612
  138.4 6.7 %copy-start.3 = (bf16[1,64,2560]{2,1,0:T(8,128)(2,1)S(1)}, bf16[1,64,2560]{2,1,0:T(8,128)(2,1)}, u32[]{:S(2)}) copy-start(bf16[1,64,2560]{2,1,0:T(8,128)(2,1)} %param.10) | copy-start | bytes 983044
  139.9 42.5 %all-to-all-start.3 = ((bf16[16,32,2560]{2,1,0:T(8,128)(2,1)}), bf16[16,32,2560]{2,1,0:T(8,128)(2,1)S(1)}, u32[]{:S(2)}, u32[]{:S(2)}) async-start(bf16[16,32,2560]{2,1,0:T(8,128)(2,1)} %bitcast.161), calls=%async_computation.3 | async-start | bytes 5242880 | tf_op jit(solution)/shard_map/all_to_all | solution.py:60
  152.2 3.0 %copy-start.2 = (bf16[16,32,2560]{2,1,0:T(8,128)(2,1)S(1)}, bf16[16,32,2560]{2,1,0:T(8,128)(2,1)}, u32[]{:S(2)}) copy-start(bf16[16,32,2560]{2,1,0:T(8,128)(2,1)} %copy-done.1) | copy-start | bytes 7864324
  156.6 40.2 %collective-permute-start = (bf16[1,64,2560]{2,1,0:T(8,128)(2,1)}, bf16[1,64,2560]{2,1,0:T(8,128)(2,1)S(1)}, u32[]{:S(2)}, u32[]{:S(2)}) collective-permute-start(bf16[1,64,2560]{2,1,0:T(8,128)(2,1)} %fusion.20), channel_id=1, source_target_pairs={{240,0},{0,16},{16,32},{32,48},{48,64},{64,80},{80,96},{96,112},{1... | collective-permute-start | bytes 983048 | tf_op jit(solution)/shard_map/ppermute | solution.py:12
  183.6 22.5 %collective-permute-start.1 = (bf16[1,64,2560]{2,1,0:T(8,128)(2,1)S(1)}, bf16[1,64,2560]{2,1,0:T(8,128)(2,1)S(1)}, u32[]{:S(2)}, u32[]{:S(2)}) collective-permute-start(bf16[1,64,2560]{2,1,0:T(8,128)(2,1)S(1)} %fusion.21), channel_id=1, source_target_pairs={{16,0},{32,16},{48,32},{64,48},{80,64},{96,80},{112,96},{128,112},... | collective-permute-start | bytes 983048 | tf_op jit(solution)/shard_map/ppermute | solution.py:12

commit v2 on v1

--- a/solution.py
+++ b/solution.py
@@ -20,13 +20,13 @@
     normed = (xf * lax.rsqrt(jnp.mean(xf * xf, axis=-1, keepdims=True) + 1e-06) * gain).astype(
         jnp.bfloat16
     )
+    normed = lax.optimization_barrier(normed)
     logits = jnp.dot(normed, table, preferred_element_type=jnp.float32)
-    chosen = jnp.take_along_axis(logits, ids, axis=1)
+    picks = ids[:, :, None] == jnp.arange(experts, dtype=jnp.int32)[None, None, :]
+    chosen = jnp.sum(jnp.where(picks, logits[:, None, :], 0.0), axis=-1)
     score = jax.nn.sigmoid(chosen)
     gates = score / jnp.sum(score, axis=-1, keepdims=True)
-    onehot = (ids[:, :, None] == jnp.arange(experts, dtype=jnp.int32)[None, None, :]).astype(
-        jnp.int32
-    )
+    onehot = picks.astype(jnp.int32)
     flat = onehot.reshape(tokens_here * choose, experts)
     before = jnp.cumsum(flat, axis=0) - flat
     slot = jnp.sum(before * flat, axis=-1).reshape(tokens_here, choose)
@@ -70,9 +70,11 @@
     rows_up = exchange(send_up)
     rows_down = exchange(send_down)
     back_up = exchange(apply_experts(rows_up, up_w, down_w))
-    back_down = exchange(apply_experts(rows_down, up_w, down_w))
+    out_down = apply_experts(rows_down, up_w, down_w)
     layer_up = finish(up_in[0], hi_up, lo_up, back_up)
+    layer_up, out_down = lax.optimization_barrier((layer_up, out_down))
     up_out = shifted(layer_up[None], "pipe", 1)
+    back_down = exchange(out_down)
     layer_down = finish(down_in[0], hi_down, lo_down, back_down)
     down_out = shifted(layer_down[None], "pipe", -1)
     return (up_out, down_out)

time: 208 us -> 210 us (level)
  waiting for transfers between devices: 117 us -> 128 us
  local copies, waits for them, and re-layouts: 12.2 us -> 4.78 us
  matrix products: 39.8 us -> 36.6 us
    all_to_all x4, waiting for transfers between devices: 102 us -> 113 us  [exchange(): lax.all_to_all(block, 'expert', split_axis=0, concat_axis=0, tiled=True)]
    gather x10 -> x0, local copies, waits for them, and re-layouts: 6.85 us -> none  [layer_route(): chosen = jnp.take_along_axis(logits, ids, axis=1)]
  transfers between devices with their start and end apart: 6 -> 6, of which waited for: 6 -> 6; matrix products, arithmetic and copies ran while one was open for 22% -> 17% of each run, Pallas kernels for 0% -> 0%
where the time goes in v2:
time: 210 us
  waiting for transfers between devices  128 us (61%)
  matrix products  36.6 us (17%)
  starting transfers between devices  32.3 us (15%)
  other arithmetic  7.24 us (3%)
  local copies, waits for them, and re-layouts  4.78 us (2%)
    all_to_all x4, waiting for transfers between devices, exchange(): lax.all_to_all(block, 'expert', split_axis=0, concat_axis=0, tiled=True)  113 us
    dot_general x2, matrix products, apply_experts(): jnp.dot(hidden, down_w, preferred_element_type=jnp.float32)  28.4 us
    all_to_all x4, starting transfers between devices, exchange(): lax.all_to_all(block, 'expert', split_axis=0, concat_axis=0, tiled=True)  21 us
    ppermute x2, waiting for transfers between devices, shifted(): return lax.ppermute(block, axis, route)  14.5 us
    ppermute x2, starting transfers between devices, shifted(): return lax.ppermute(block, axis, route)  11.3 us
    dot_general x2, matrix products, layer_route(): lax.dot_general(place, normed, (((0,), (0,)), ((), ())), preferred_elemen...  4.8 us
  transfers between devices with their start and end apart: 6, of which 6 were waited for; matrix products, arithmetic and copies ran while one was open for 17% of the time, Pallas kernels for 0%

profile of v2, /device:TPU:6, one launch (start us, length us, event | category | flops | bytes accessed | tf_op | source)
XLA Modules:
  0.0 209.6 jit_solution(7826244716021159859)
XLA Ops:
  0.6 0.8 copy.26
  1.5 0.1 eq.94
  1.6 0.1 eq.90
  1.7 0.9 reduce-window.14
  2.6 0.2 slice_reduce_fusion.1
  2.9 0.1 fusion.54
  3.0 0.1 reshape.141
  3.1 0.1 copy.30
  3.2 1.1 fusion.31
  4.4 1.1 fusion.34
  5.5 0.7 reduce.1
  6.3 1.3 fusion.36
  7.6 0.2 fusion.26
  7.7 2.4 %convolution_convert_fusion.1 = bf16[512,2560]{1,0:T(8,128)(2,1)} fusion(pred[64,512]{1,0:T(8,128)(4,1)S(1)} %fusion.26, bf16[64,2560]{1,0:T(8,128)(2,1)S(1)} %get-tuple-element.7), kind=kOutput, calls=%fused_computation.11 | convolution fusion | flops 169082880 | bytes 2981888 | tf_op jit(solution)/shard_map/dot_general | solution.py:37
  10.1 6.3 %all-to-all-start = ((bf16[16,32,2560]{2,1,0:T(8,128)(2,1)}), bf16[16,32,2560]{2,1,0:T(8,128)(2,1)S(1)}, u32[]{:S(2)}, u32[]{:S(2)}) async-start(bf16[16,32,2560]{2,1,0:T(8,128)(2,1)} %bitcast.6), calls=%async_computation | async-start | bytes 5242880 | tf_op jit(solution)/shard_map/all_to_all | solution.py:60
  16.4 0.1 copy.32
  16.5 0.1 eq.108
  16.7 0.1 eq.104
  16.8 0.9 reduce-window.16
  17.7 0.2 slice_reduce_fusion
  17.9 0.1 fusion.51
  18.0 0.1 reshape.143
  18.2 0.1 copy.36
  18.3 0.2 fusion.25
  18.4 2.4 %convolution_convert_fusion = bf16[512,2560]{1,0:T(8,128)(2,1)} fusion(pred[64,512]{1,0:T(8,128)(4,1)S(1)} %fusion.25, bf16[64,2560]{1,0:T(8,128)(2,1)S(1)} %get-tuple-element.6), kind=kOutput, calls=%fused_computation.10 | convolution fusion | flops 169082880 | bytes 2981888 | tf_op jit(solution)/shard_map/dot_general | solution.py:37
  20.8 33.2 %all-to-all-done = bf16[16,32,2560]{2,1,0:T(8,128)(2,1)S(1)} async-done(((bf16[16,32,2560]{2,1,0:T(8,128)(2,1)}), bf16[16,32,2560]{2,1,0:T(8,128)(2,1)S(1)}, u32[]{:S(2)}, u32[]{:S(2)}) %all-to-all-start) | async-done | bytes 2621472 | tf_op jit(solution)/shard_map/all_to_all | solution.py:60
  54.0 4.9 %all-to-all-start.2 = ((bf16[16,32,2560]{2,1,0:T(8,128)(2,1)}), bf16[16,32,2560]{2,1,0:T(8,128)(2,1)}, u32[]{:S(2)}, u32[]{:S(2)}) async-start(bf16[16,32,2560]{2,1,0:T(8,128)(2,1)} %bitcast.16), calls=%async_computation.2 | async-start | bytes 5242880 | tf_op jit(solution)/shard_map/all_to_all | solution.py:60
  58.9 13.9 %fusion.8 = bf16[512,2560]{1,0:T(8,128)(2,1)} fusion(bf16[1,1,1152,2560]{3,2,1,0:T(8,128)(2,1)} %param.15, bf16[512,2560]{1,0:T(8,128)(2,1)S(1)} %bitcast.118, bf16[1,1,2560,1152]{3,2,1,0:T(8,128)(2,1)} %param.14), kind=kOutput, calls=%fused_computation.8 | convolution fusion | flops 6044057600 | bytes 17039360 | tf_op jit(solution)/shard_map/dot_general | solution.py:49
  72.8 23.9 %all-to-all-done.2 = bf16[16,32,2560]{2,1,0:T(8,128)(2,1)} async-done(((bf16[16,32,2560]{2,1,0:T(8,128)(2,1)}), bf16[16,32,2560]{2,1,0:T(8,128)(2,1)}, u32[]{:S(2)}, u32[]{:S(2)}) %all-to-all-start.2) | async-done | bytes 2621472 | tf_op jit(solution)/shard_map/all_to_all | solution.py:60
  96.6 5.0 %all-to-all-start.1 = ((bf16[16,32,2560]{2,1,0:T(8,128)(2,1)}), bf16[16,32,2560]{2,1,0:T(8,128)(2,1)S(1)}, u32[]{:S(2)}, u32[]{:S(2)}) async-start(bf16[16,32,2560]{2,1,0:T(8,128)(2,1)} %bitcast.120), calls=%async_computation.1 | async-start | bytes 5242880 | tf_op jit(solution)/shard_map/all_to_all | solution.py:60
  101.6 0.2 fusion.39
  101.9 0.2 select_reduce_fusion.1
  102.1 14.6 %fusion.11 = bf16[512,2560]{1,0:T(8,128)(2,1)} fusion(bf16[1,1,1152,2560]{3,2,1,0:T(8,128)(2,1)} %param.15, bf16[512,2560]{1,0:T(8,128)(2,1)} %bitcast.17, bf16[1,1,2560,1152]{3,2,1,0:T(8,128)(2,1)} %param.14), kind=kOutput, calls=%fused_computation.9 | convolution fusion | flops 6044057600 | bytes 17039360 | tf_op jit(solution)/shard_map/dot_general | solution.py:49
  116.7 22.6 %all-to-all-done.1 = bf16[16,32,2560]{2,1,0:T(8,128)(2,1)S(1)} async-done(((bf16[16,32,2560]{2,1,0:T(8,128)(2,1)}), bf16[16,32,2560]{2,1,0:T(8,128)(2,1)S(1)}, u32[]{:S(2)}, u32[]{:S(2)}) %all-to-all-start.1) | async-done | bytes 2621472 | tf_op jit(solution)/shard_map/all_to_all | solution.py:60
  139.2 0.6 fusion.47
  139.8 1.3 fusion.19
  141.1 4.9 %all-to-all-start.3 = ((bf16[16,32,2560]{2,1,0:T(8,128)(2,1)}), bf16[16,32,2560]{2,1,0:T(8,128)(2,1)S(1)}, u32[]{:S(2)}, u32[]{:S(2)}) async-start(bf16[16,32,2560]{2,1,0:T(8,128)(2,1)} %bitcast.119), calls=%async_computation.3 | async-start | bytes 5242880 | tf_op jit(solution)/shard_map/all_to_all | solution.py:60
  146.0 0.2 fusion.37
  146.3 0.2 select_reduce_fusion
  146.5 3.3 %collective-permute-start = (bf16[1,64,2560]{2,1,0:T(8,128)(2,1)}, bf16[1,64,2560]{2,1,0:T(8,128)(2,1)}, u32[]{:S(2)}, u32[]{:S(2)}) collective-permute-start(bf16[1,64,2560]{2,1,0:T(8,128)(2,1)} %bitcast.121), channel_id=1, source_target_pairs={{240,0},{0,16},{16,32},{32,48},{48,64},{64,80},{80,96},{96,112},{1... | collective-permute-start | bytes 983048 | tf_op jit(solution)/shard_map/ppermute | solution.py:12
  149.8 33.8 %all-to-all-done.3 = bf16[16,32,2560]{2,1,0:T(8,128)(2,1)S(1)} async-done(((bf16[16,32,2560]{2,1,0:T(8,128)(2,1)}), bf16[16,32,2560]{2,1,0:T(8,128)(2,1)S(1)}, u32[]{:S(2)}, u32[]{:S(2)}) %all-to-all-start.3) | async-done | bytes 2621472 | tf_op jit(solution)/shard_map/all_to_all | solution.py:60
  183.6 0.6 fusion.44
  184.2 0.6 fusion.20
  184.8 7.9 %collective-permute-start.1 = (bf16[1,64,2560]{2,1,0:T(8,128)(2,1)S(1)}, bf16[1,64,2560]{2,1,0:T(8,128)(2,1)S(1)}, u32[]{:S(2)}, u32[]{:S(2)}) collective-permute-start(bf16[1,64,2560]{2,1,0:T(8,128)(2,1)S(1)} %fusion.20), channel_id=1, source_target_pairs={{16,0},{32,16},{48,32},{64,48},{80,64},{96,80},{112,96},{128,112},... | collective-permute-start | bytes 983048 | tf_op jit(solution)/shard_map/ppermute | solution.py:12
  192.7 4.7 %collective-permute-done = bf16[1,64,2560]{2,1,0:T(8,128)(2,1)} collective-permute-done((bf16[1,64,2560]{2,1,0:T(8,128)(2,1)}, bf16[1,64,2560]{2,1,0:T(8,128)(2,1)}, u32[]{:S(2)}, u32[]{:S(2)}) %collective-permute-start) | collective-permute-done | bytes 327712 | tf_op jit(solution)/shard_map/ppermute | solution.py:12
  197.4 9.8 %collective-permute-done.1 = bf16[1,64,2560]{2,1,0:T(8,128)(2,1)S(1)} collective-permute-done((bf16[1,64,2560]{2,1,0:T(8,128)(2,1)S(1)}, bf16[1,64,2560]{2,1,0:T(8,128)(2,1)S(1)}, u32[]{:S(2)}, u32[]{:S(2)}) %collective-permute-start.1) | collective-permute-done | bytes 327712 | tf_op jit(solution)/shard_map/ppermute | solution.py:12
  207.2 1.7 copy.50
  208.9 0.7 copy.51
  (25 shorter events, 0.3 us)
Async XLA Ops:
  0.6 101.0 %copy-start = (bf16[1,2560,16]{1,2,0:T(8,128)(2,1)S(1)}, bf16[1,2560,16]{1,2,0:T(8,128)(2,1)}, u32[]{:S(2)}) copy-start(bf16[1,2560,16]{1,2,0:T(8,128)(2,1)} %param.13) | copy-start | bytes 245764
  10.1 6.3 %copy-start.4 = (s32[1,64,6]{1,0,2:T(1,128)S(1)}, s32[1,64,6]{1,0,2:T(1,128)}, u32[]{:S(2)}) copy-start(s32[1,64,6]{1,0,2:T(1,128)} %param.11) | copy-start | bytes 4612
  10.1 43.9 %all-to-all-start = ((bf16[16,32,2560]{2,1,0:T(8,128)(2,1)}), bf16[16,32,2560]{2,1,0:T(8,128)(2,1)S(1)}, u32[]{:S(2)}, u32[]{:S(2)}) async-start(bf16[16,32,2560]{2,1,0:T(8,128)(2,1)} %bitcast.6), calls=%async_computation | async-start | bytes 5242880 | tf_op jit(solution)/shard_map/all_to_all | solution.py:60
  54.0 42.6 %all-to-all-start.2 = ((bf16[16,32,2560]{2,1,0:T(8,128)(2,1)}), bf16[16,32,2560]{2,1,0:T(8,128)(2,1)}, u32[]{:S(2)}, u32[]{:S(2)}) async-start(bf16[16,32,2560]{2,1,0:T(8,128)(2,1)} %bitcast.16), calls=%async_computation.2 | async-start | bytes 5242880 | tf_op jit(solution)/shard_map/all_to_all | solution.py:60
  96.6 5.0 %copy-start.3 = (s32[1,64,6]{1,0,2:T(1,128)S(1)}, s32[1,64,6]{1,0,2:T(1,128)}, u32[]{:S(2)}) copy-start(s32[1,64,6]{1,0,2:T(1,128)} %param.10) | copy-start | bytes 4612
  96.6 42.6 %all-to-all-start.1 = ((bf16[16,32,2560]{2,1,0:T(8,128)(2,1)}), bf16[16,32,2560]{2,1,0:T(8,128)(2,1)S(1)}, u32[]{:S(2)}, u32[]{:S(2)}) async-start(bf16[16,32,2560]{2,1,0:T(8,128)(2,1)} %bitcast.120), calls=%async_computation.1 | async-start | bytes 5242880 | tf_op jit(solution)/shard_map/all_to_all | solution.py:60
  116.7 23.1 %copy-start.1 = (bf16[1,64,2560]{2,1,0:T(8,128)(2,1)S(1)}, bf16[1,64,2560]{2,1,0:T(8,128)(2,1)}, u32[]{:S(2)}) copy-start(bf16[1,64,2560]{2,1,0:T(8,128)(2,1)} %param.8) | copy-start | bytes 983044
  141.1 42.5 %all-to-all-start.3 = ((bf16[16,32,2560]{2,1,0:T(8,128)(2,1)}), bf16[16,32,2560]{2,1,0:T(8,128)(2,1)S(1)}, u32[]{:S(2)}, u32[]{:S(2)}) async-start(bf16[16,32,2560]{2,1,0:T(8,128)(2,1)} %bitcast.119), calls=%async_computation.3 | async-start | bytes 5242880 | tf_op jit(solution)/shard_map/all_to_all | solution.py:60
  146.0 38.2 %copy-start.2 = (bf16[1,64,2560]{2,1,0:T(8,128)(2,1)S(1)}, bf16[1,64,2560]{2,1,0:T(8,128)(2,1)}, u32[]{:S(2)}) copy-start(bf16[1,64,2560]{2,1,0:T(8,128)(2,1)} %param.9) | copy-start | bytes 983044
  146.5 50.9 %collective-permute-start = (bf16[1,64,2560]{2,1,0:T(8,128)(2,1)}, bf16[1,64,2560]{2,1,0:T(8,128)(2,1)}, u32[]{:S(2)}, u32[]{:S(2)}) collective-permute-start(bf16[1,64,2560]{2,1,0:T(8,128)(2,1)} %bitcast.121), channel_id=1, source_target_pairs={{240,0},{0,16},{16,32},{32,48},{48,64},{64,80},{80,96},{96,112},{1... | collective-permute-start | bytes 983048 | tf_op jit(solution)/shard_map/ppermute | solution.py:12
  184.8 22.4 %collective-permute-start.1 = (bf16[1,64,2560]{2,1,0:T(8,128)(2,1)S(1)}, bf16[1,64,2560]{2,1,0:T(8,128)(2,1)S(1)}, u32[]{:S(2)}, u32[]{:S(2)}) collective-permute-start(bf16[1,64,2560]{2,1,0:T(8,128)(2,1)S(1)} %fusion.20), channel_id=1, source_target_pairs={{16,0},{32,16},{48,32},{64,48},{80,64},{96,80},{112,96},{128,112},... | collective-permute-start | bytes 983048 | tf_op jit(solution)/shard_map/ppermute | solution.py:12

commit v3 on v2

--- a/solution.py
+++ b/solution.py
@@ -70,11 +70,10 @@
     rows_up = exchange(send_up)
     rows_down = exchange(send_down)
     back_up = exchange(apply_experts(rows_up, up_w, down_w))
-    out_down = apply_experts(rows_down, up_w, down_w)
+    back_down = exchange(apply_experts(rows_down, up_w, down_w))
     layer_up = finish(up_in[0], hi_up, lo_up, back_up)
-    layer_up, out_down = lax.optimization_barrier((layer_up, out_down))
+    layer_up, back_down = lax.optimization_barrier((layer_up, back_down))
     up_out = shifted(layer_up[None], "pipe", 1)
-    back_down = exchange(out_down)
     layer_down = finish(down_in[0], hi_down, lo_down, back_down)
     down_out = shifted(layer_down[None], "pipe", -1)
     return (up_out, down_out)

time: 210 us -> 216 us (1.029)
  waiting for transfers between devices: 128 us -> 134 us
  matrix products: 36.6 us -> 40.2 us
  starting transfers between devices: 32.3 us -> 28.9 us
    ppermute x2, waiting for transfers between devices: 14.5 us -> 19.1 us  [shifted(): return lax.ppermute(block, axis, route)]
    ppermute x2, starting transfers between devices: 11.3 us -> 7.93 us  [shifted(): return lax.ppermute(block, axis, route)]
where the time goes in v3:
time: 216 us; the launch traced here: 215 us
  waiting for transfers between devices  134 us (62%)
  matrix products  40.2 us (19%)
  starting transfers between devices  28.9 us (13%)
  other arithmetic  7.23 us (3%)
  local copies, waits for them, and re-layouts  3.79 us (2%)
    all_to_all x4, waiting for transfers between devices, exchange(): lax.all_to_all(block, 'expert', split_axis=0, concat_axis=0, tiled=True)  115 us
    dot_general x2, matrix products, apply_experts(): jnp.dot(hidden, down_w, preferred_element_type=jnp.float32)  28.5 us
    all_to_all x4, starting transfers between devices, exchange(): lax.all_to_all(block, 'expert', split_axis=0, concat_axis=0, tiled=True)  21 us
    ppermute x2, waiting for transfers between devices, shifted(): return lax.ppermute(block, axis, route)  19.1 us
    ppermute x2, starting transfers between devices, shifted(): return lax.ppermute(block, axis, route)  7.93 us
    dot_general x2, matrix products, layer_route(): lax.dot_general(place, normed, (((0,), (0,)), ((), ())), preferred_elemen...  4.8 us
  transfers between devices with their start and end apart: 6, of which 6 were waited for; matrix products, arithmetic and copies ran while one was open for 17% of the time, Pallas kernels for 0%

profile of v3, /device:TPU:6, one launch (start us, length us, event | category | flops | bytes accessed | tf_op | source)
XLA Modules:
  0.0 215.1 jit_solution(13677104824112090806)
XLA Ops:
  0.6 0.0 copy-start
  0.6 0.8 copy.26
  1.5 0.1 eq.94
  1.6 0.1 eq.90
  1.7 0.9 reduce-window.14
  2.6 0.2 slice_reduce_fusion.1
  2.9 0.1 fusion.54
  3.0 0.1 reshape.141
  3.1 0.1 copy.30
  3.2 1.1 fusion.31
  4.4 1.1 fusion.34
  5.5 0.7 reduce.1
  6.3 1.3 fusion.36
  7.6 0.2 fusion.26
  7.7 2.4 %convolution_convert_fusion.1 = bf16[512,2560]{1,0:T(8,128)(2,1)} fusion(pred[64,512]{1,0:T(8,128)(4,1)S(1)} %fusion.26, bf16[64,2560]{1,0:T(8,128)(2,1)S(1)} %get-tuple-element.7), kind=kOutput, calls=%fused_computation.11 | convolution fusion | flops 169082880 | bytes 2981888 | tf_op jit(solution)/shard_map/dot_general | solution.py:37
  10.1 6.3 %all-to-all-start = ((bf16[16,32,2560]{2,1,0:T(8,128)(2,1)}), bf16[16,32,2560]{2,1,0:T(8,128)(2,1)S(1)}, u32[]{:S(2)}, u32[]{:S(2)}) async-start(bf16[16,32,2560]{2,1,0:T(8,128)(2,1)} %bitcast.6), calls=%async_computation | async-start | bytes 5242880 | tf_op jit(solution)/shard_map/all_to_all | solution.py:60
  16.4 0.1 copy.32
  16.5 0.1 eq.108
  16.7 0.1 eq.104
  16.8 0.9 reduce-window.16
  17.7 0.2 slice_reduce_fusion
  17.9 0.1 fusion.51
  18.0 0.1 reshape.143
  18.2 0.1 copy.36
  18.3 0.2 fusion.25
  18.4 2.4 %convolution_convert_fusion = bf16[512,2560]{1,0:T(8,128)(2,1)} fusion(pred[64,512]{1,0:T(8,128)(4,1)S(1)} %fusion.25, bf16[64,2560]{1,0:T(8,128)(2,1)S(1)} %get-tuple-element.6), kind=kOutput, calls=%fused_computation.10 | convolution fusion | flops 169082880 | bytes 2981888 | tf_op jit(solution)/shard_map/dot_general | solution.py:37
  20.8 33.2 %all-to-all-done = bf16[16,32,2560]{2,1,0:T(8,128)(2,1)S(1)} async-done(((bf16[16,32,2560]{2,1,0:T(8,128)(2,1)}), bf16[16,32,2560]{2,1,0:T(8,128)(2,1)S(1)}, u32[]{:S(2)}, u32[]{:S(2)}) %all-to-all-start) | async-done | bytes 2621472 | tf_op jit(solution)/shard_map/all_to_all | solution.py:60
  54.0 4.9 %all-to-all-start.2 = ((bf16[16,32,2560]{2,1,0:T(8,128)(2,1)}), bf16[16,32,2560]{2,1,0:T(8,128)(2,1)}, u32[]{:S(2)}, u32[]{:S(2)}) async-start(bf16[16,32,2560]{2,1,0:T(8,128)(2,1)} %bitcast.16), calls=%async_computation.2 | async-start | bytes 5242880 | tf_op jit(solution)/shard_map/all_to_all | solution.py:60
  58.9 13.9 %fusion.8 = bf16[512,2560]{1,0:T(8,128)(2,1)} fusion(bf16[1,1,1152,2560]{3,2,1,0:T(8,128)(2,1)} %param.15, bf16[512,2560]{1,0:T(8,128)(2,1)S(1)} %bitcast.117, bf16[1,1,2560,1152]{3,2,1,0:T(8,128)(2,1)} %param.14), kind=kOutput, calls=%fused_computation.8 | convolution fusion | flops 6044057600 | bytes 17039360 | tf_op jit(solution)/shard_map/dot_general | solution.py:49
  72.8 23.8 %all-to-all-done.2 = bf16[16,32,2560]{2,1,0:T(8,128)(2,1)} async-done(((bf16[16,32,2560]{2,1,0:T(8,128)(2,1)}), bf16[16,32,2560]{2,1,0:T(8,128)(2,1)}, u32[]{:S(2)}, u32[]{:S(2)}) %all-to-all-start.2) | async-done | bytes 2621472 | tf_op jit(solution)/shard_map/all_to_all | solution.py:60
  96.6 4.9 %all-to-all-start.1 = ((bf16[16,32,2560]{2,1,0:T(8,128)(2,1)}), bf16[16,32,2560]{2,1,0:T(8,128)(2,1)S(1)}, u32[]{:S(2)}, u32[]{:S(2)}) async-start(bf16[16,32,2560]{2,1,0:T(8,128)(2,1)} %bitcast.118), calls=%async_computation.1 | async-start | bytes 5242880 | tf_op jit(solution)/shard_map/all_to_all | solution.py:60
  101.5 14.6 %fusion.11 = bf16[512,2560]{1,0:T(8,128)(2,1)} fusion(bf16[1,1,1152,2560]{3,2,1,0:T(8,128)(2,1)} %param.15, bf16[512,2560]{1,0:T(8,128)(2,1)} %bitcast.17, bf16[1,1,2560,1152]{3,2,1,0:T(8,128)(2,1)} %param.14), kind=kOutput, calls=%fused_computation.9 | convolution fusion | flops 6044057600 | bytes 17039360 | tf_op jit(solution)/shard_map/dot_general | solution.py:49
  116.1 23.0 %all-to-all-done.1 = bf16[16,32,2560]{2,1,0:T(8,128)(2,1)S(1)} async-done(((bf16[16,32,2560]{2,1,0:T(8,128)(2,1)}), bf16[16,32,2560]{2,1,0:T(8,128)(2,1)S(1)}, u32[]{:S(2)}, u32[]{:S(2)}) %all-to-all-start.1) | async-done | bytes 2621472 | tf_op jit(solution)/shard_map/all_to_all | solution.py:60
  139.1 5.0 %all-to-all-start.3 = ((bf16[16,32,2560]{2,1,0:T(8,128)(2,1)}), bf16[16,32,2560]{2,1,0:T(8,128)(2,1)}, u32[]{:S(2)}, u32[]{:S(2)}) async-start(bf16[16,32,2560]{2,1,0:T(8,128)(2,1)} %bitcast.116), calls=%async_computation.3 | async-start | bytes 5242880 | tf_op jit(solution)/shard_map/all_to_all | solution.py:60
  144.2 0.2 fusion.39
  144.4 0.2 fusion.37
  144.7 0.2 select_reduce_fusion.1
  144.9 0.2 select_reduce_fusion
  145.1 0.6 fusion.47
  145.6 1.3 fusion.19
  147.0 34.9 %all-to-all-done.3 = bf16[16,32,2560]{2,1,0:T(8,128)(2,1)} async-done(((bf16[16,32,2560]{2,1,0:T(8,128)(2,1)}), bf16[16,32,2560]{2,1,0:T(8,128)(2,1)}, u32[]{:S(2)}, u32[]{:S(2)}) %all-to-all-start.3) | async-done | bytes 2621472 | tf_op jit(solution)/shard_map/all_to_all | solution.py:60
  181.8 2.3 %fusion.44 = f32[64,2560]{1,0:T(8,128)S(1)} fusion(bf16[512,2560]{1,0:T(8,128)(2,1)} %bitcast.19, f32[64,512]{1,0:T(8,128)S(1)} %select_reduce_fusion), kind=kOutput, calls=%fused_computation.54 | convolution fusion | flops 167804928 | bytes 3407872 | tf_op jit(solution)/shard_map/dot_general | solution.py:53
  184.2 2.4 %fusion.20 = bf16[1,64,2560]{2,1,0:T(8,128)(2,1)S(1)} fusion(f32[64,2560]{1,0:T(8,128)S(1)} %fusion.44, bf16[512,2560]{1,0:T(8,128)(2,1)} %bitcast.19, bf16[1,64,2560]{2,1,0:T(8,128)(2,1)S(1)} %copy-done.2, f32[64,512]{1,0:T(8,128)S(1)} %select_reduce_fusion), kind=kOutput, calls=%fused_computation.20 | convolution fusion | flops 168722432 | bytes 4063232 | tf_op jit(solution)/shard_map/dot_general | solution.py:53
  186.6 7.9 %collective-permute-start.1 = (bf16[1,64,2560]{2,1,0:T(8,128)(2,1)S(1)}, bf16[1,64,2560]{2,1,0:T(8,128)(2,1)S(1)}, u32[]{:S(2)}, u32[]{:S(2)}) collective-permute-start(bf16[1,64,2560]{2,1,0:T(8,128)(2,1)S(1)} %fusion.20), channel_id=1, source_target_pairs={{16,0},{32,16},{48,32},{64,48},{80,64},{96,80},{112,96},{128,112},... | collective-permute-start | bytes 983048 | tf_op jit(solution)/shard_map/ppermute | solution.py:12
  194.5 14.5 %collective-permute-done.1 = bf16[1,64,2560]{2,1,0:T(8,128)(2,1)S(1)} collective-permute-done((bf16[1,64,2560]{2,1,0:T(8,128)(2,1)S(1)}, bf16[1,64,2560]{2,1,0:T(8,128)(2,1)S(1)}, u32[]{:S(2)}, u32[]{:S(2)}) %collective-permute-start.1) | collective-permute-done | bytes 327712 | tf_op jit(solution)/shard_map/ppermute | solution.py:12
  209.0 4.6 %collective-permute-done = bf16[1,64,2560]{2,1,0:T(8,128)(2,1)S(1)} collective-permute-done((bf16[1,64,2560]{2,1,0:T(8,128)(2,1)S(1)}, bf16[1,64,2560]{2,1,0:T(8,128)(2,1)S(1)}, u32[]{:S(2)}, u32[]{:S(2)}) %collective-permute-start) | collective-permute-done | bytes 327712 | tf_op jit(solution)/shard_map/ppermute | solution.py:12
  213.6 0.7 copy.50
  214.3 0.7 copy.51
  (27 shorter events, 0.3 us)
Async XLA Ops:
  0.6 143.5 %copy-start = (bf16[1,2560,16]{1,2,0:T(8,128)(2,1)S(1)}, bf16[1,2560,16]{1,2,0:T(8,128)(2,1)}, u32[]{:S(2)}) copy-start(bf16[1,2560,16]{1,2,0:T(8,128)(2,1)} %param.13) | copy-start | bytes 245764
  10.1 6.3 %copy-start.5 = (s32[1,64,6]{1,0,2:T(1,128)S(1)}, s32[1,64,6]{1,0,2:T(1,128)}, u32[]{:S(2)}) copy-start(s32[1,64,6]{1,0,2:T(1,128)} %param.11) | copy-start | bytes 4612
  10.1 43.9 %all-to-all-start = ((bf16[16,32,2560]{2,1,0:T(8,128)(2,1)}), bf16[16,32,2560]{2,1,0:T(8,128)(2,1)S(1)}, u32[]{:S(2)}, u32[]{:S(2)}) async-start(bf16[16,32,2560]{2,1,0:T(8,128)(2,1)} %bitcast.6), calls=%async_computation | async-start | bytes 5242880 | tf_op jit(solution)/shard_map/all_to_all | solution.py:60
  54.0 42.6 %all-to-all-start.2 = ((bf16[16,32,2560]{2,1,0:T(8,128)(2,1)}), bf16[16,32,2560]{2,1,0:T(8,128)(2,1)}, u32[]{:S(2)}, u32[]{:S(2)}) async-start(bf16[16,32,2560]{2,1,0:T(8,128)(2,1)} %bitcast.16), calls=%async_computation.2 | async-start | bytes 5242880 | tf_op jit(solution)/shard_map/all_to_all | solution.py:60
  96.6 42.5 %all-to-all-start.1 = ((bf16[16,32,2560]{2,1,0:T(8,128)(2,1)}), bf16[16,32,2560]{2,1,0:T(8,128)(2,1)S(1)}, u32[]{:S(2)}, u32[]{:S(2)}) async-start(bf16[16,32,2560]{2,1,0:T(8,128)(2,1)} %bitcast.118), calls=%async_computation.1 | async-start | bytes 5242880 | tf_op jit(solution)/shard_map/all_to_all | solution.py:60
  139.1 5.0 %copy-start.4 = (s32[1,64,6]{1,0,2:T(1,128)S(1)}, s32[1,64,6]{1,0,2:T(1,128)}, u32[]{:S(2)}) copy-start(s32[1,64,6]{1,0,2:T(1,128)} %param.10) | copy-start | bytes 4612
  139.1 42.7 %all-to-all-start.3 = ((bf16[16,32,2560]{2,1,0:T(8,128)(2,1)}), bf16[16,32,2560]{2,1,0:T(8,128)(2,1)}, u32[]{:S(2)}, u32[]{:S(2)}) async-start(bf16[16,32,2560]{2,1,0:T(8,128)(2,1)} %bitcast.116), calls=%async_computation.3 | async-start | bytes 5242880 | tf_op jit(solution)/shard_map/all_to_all | solution.py:60
  144.1 1.5 copy-start.1
  146.9 37.2 %copy-start.2 = (bf16[1,64,2560]{2,1,0:T(8,128)(2,1)S(1)}, bf16[1,64,2560]{2,1,0:T(8,128)(2,1)}, u32[]{:S(2)}) copy-start(bf16[1,64,2560]{2,1,0:T(8,128)(2,1)} %param.9) | copy-start | bytes 983044
  184.2 10.3 %copy-start.3 = (bf16[64,2560]{1,0:T(8,128)(2,1)S(1)}, bf16[64,2560]{1,0:T(8,128)(2,1)}, u32[]{:S(2)}) copy-start(bf16[64,2560]{1,0:T(8,128)(2,1)} %fusion.19) | copy-start | bytes 983044
  186.6 22.4 %collective-permute-start.1 = (bf16[1,64,2560]{2,1,0:T(8,128)(2,1)S(1)}, bf16[1,64,2560]{2,1,0:T(8,128)(2,1)S(1)}, u32[]{:S(2)}, u32[]{:S(2)}) collective-permute-start(bf16[1,64,2560]{2,1,0:T(8,128)(2,1)S(1)} %fusion.20), channel_id=1, source_target_pairs={{16,0},{32,16},{48,32},{64,48},{80,64},{96,80},{112,96},{128,112},... | collective-permute-start | bytes 983048 | tf_op jit(solution)/shard_map/ppermute | solution.py:12
  194.5 19.1 %collective-permute-start = (bf16[1,64,2560]{2,1,0:T(8,128)(2,1)S(1)}, bf16[1,64,2560]{2,1,0:T(8,128)(2,1)S(1)}, u32[]{:S(2)}, u32[]{:S(2)}) collective-permute-start(bf16[1,64,2560]{2,1,0:T(8,128)(2,1)S(1)} %bitcast.119), channel_id=1, source_target_pairs={{240,0},{0,16},{16,32},{32,48},{48,64},{64,80},{80,96},{96,112},{1... | collective-permute-start | bytes 983048 | tf_op jit(solution)/shard_map/ppermute | solution.py:12

commit v4 on v3

--- a/solution.py
+++ b/solution.py
@@ -66,15 +66,15 @@
     up_w = w_up[0, 0]
     down_w = w_down[0, 0]
     send_up, hi_up, lo_up = layer_route(up_in[0], up_ids[0], gain, table)
-    send_down, hi_down, lo_down = layer_route(down_in[0], down_ids[0], gain, table)
+    send_up, x_down, ids_down = lax.optimization_barrier((send_up, down_in[0], down_ids[0]))
+    send_down, hi_down, lo_down = layer_route(x_down, ids_down, gain, table)
     rows_up = exchange(send_up)
     rows_down = exchange(send_down)
     back_up = exchange(apply_experts(rows_up, up_w, down_w))
     back_down = exchange(apply_experts(rows_down, up_w, down_w))
     layer_up = finish(up_in[0], hi_up, lo_up, back_up)
-    layer_up, back_down = lax.optimization_barrier((layer_up, back_down))
     up_out = shifted(layer_up[None], "pipe", 1)
-    layer_down = finish(down_in[0], hi_down, lo_down, back_down)
+    layer_down = finish(x_down, hi_down, lo_down, back_down)
     down_out = shifted(layer_down[None], "pipe", -1)
     return (up_out, down_out)
 

time: 216 us -> 211 us (0.977)
  waiting for transfers between devices: 134 us -> 123 us
  local copies, waits for them, and re-layouts: 3.79 us -> 8.53 us
  starting transfers between devices: 28.9 us -> 32 us
    all_to_all x4, waiting for transfers between devices: 115 us -> 109 us  [exchange(): lax.all_to_all(block, 'expert', split_axis=0, concat_axis=0, tiled=True)]
    unnamed x16 -> x20, local copies, waits for them, and re-layouts: 2.39 us -> 7.06 us
    ppermute x2, waiting for transfers between devices: 19.1 us -> 14.5 us  [shifted(): return lax.ppermute(block, axis, route)]
    ppermute x2, starting transfers between devices: 7.93 us -> 11.2 us  [shifted(): return lax.ppermute(block, axis, route)]
  transfers between devices with their start and end apart: 6 -> 6, of which waited for: 6 -> 6; matrix products, arithmetic and copies ran while one was open for 17% -> 19% of each run, Pallas kernels for 0% -> 0%
where the time goes in v4:
time: 211 us; the launch traced here: 210 us
  waiting for transfers between devices  123 us (58%)
  matrix products  39.1 us (19%)
  starting transfers between devices  32 us (15%)
  local copies, waits for them, and re-layouts  8.53 us (4%)
  other arithmetic  6.23 us (3%)
    all_to_all x4, waiting for transfers between devices, exchange(): lax.all_to_all(block, 'expert', split_axis=0, concat_axis=0, tiled=True)  109 us
    dot_general x2, matrix products, apply_experts(): jnp.dot(hidden, down_w, preferred_element_type=jnp.float32)  29.2 us
    all_to_all x4, starting transfers between devices, exchange(): lax.all_to_all(block, 'expert', split_axis=0, concat_axis=0, tiled=True)  20.8 us
    ppermute x2, waiting for transfers between devices, shifted(): return lax.ppermute(block, axis, route)  14.5 us
    ppermute x2, starting transfers between devices, shifted(): return lax.ppermute(block, axis, route)  11.2 us
    unnamed x20, local copies, waits for them, and re-layouts  7.06 us
    dot_general x2, matrix products, layer_route(): lax.dot_general(place, normed, (((0,), (0,)), ((), ())), preferred_elemen...  4.8 us
  transfers between devices with their start and end apart: 6, of which 6 were waited for; matrix products, arithmetic and copies ran while one was open for 19% of the time, Pallas kernels for 0%

profile of v4, /device:TPU:6, one launch (start us, length us, event | category | flops | bytes accessed | tf_op | source)
XLA Modules:
  0.0 210.1 jit_solution(13179297821204563776)
XLA Ops:
  0.6 0.8 copy.24
  1.5 0.1 eq.94
  1.6 0.1 eq.90
  1.7 1.1 fusion.35
  2.9 0.9 reduce-window.14
  3.8 0.2 slice_reduce_fusion.1
  4.0 0.1 fusion.54
  4.1 0.1 reshape.130
  4.4 0.2 fusion.27
  4.5 0.8 copy.30
  5.3 0.7 reduce.1
  6.1 1.1 fusion.37
  7.2 2.4 %convolution_convert_fusion.1 = bf16[512,2560]{1,0:T(8,128)(2,1)} fusion(pred[64,512]{1,0:T(8,128)(4,1)S(1)} %fusion.27, bf16[64,2560]{1,0:T(8,128)(2,1)S(1)} %fusion.37), kind=kOutput, calls=%fused_computation.11 | convolution fusion | flops 169082880 | bytes 2981888 | tf_op jit(solution)/shard_map/dot_general | solution.py:37
  9.6 6.6 %all-to-all-start = ((bf16[16,32,2560]{2,1,0:T(8,128)(2,1)}), bf16[16,32,2560]{2,1,0:T(8,128)(2,1)}, u32[]{:S(2)}, u32[]{:S(2)}) async-start(bf16[16,32,2560]{2,1,0:T(8,128)(2,1)} %bitcast.8), calls=%async_computation | async-start | bytes 5242880 | tf_op jit(solution)/shard_map/all_to_all | solution.py:60
  16.1 0.1 eq.108
  16.3 0.1 eq.104
  16.4 0.9 reduce-window.16
  17.3 0.2 slice_reduce_fusion
  17.7 0.1 reshape.132
  17.9 0.2 fusion.32
  18.1 0.2 fusion.34
  18.2 0.2 fusion.26
  18.4 2.4 %convolution_convert_fusion = bf16[512,2560]{1,0:T(8,128)(2,1)} fusion(pred[64,512]{1,0:T(8,128)(4,1)S(1)} %fusion.26, bf16[64,2560]{1,0:T(8,128)(2,1)S(1)} %fusion.34), kind=kOutput, calls=%fused_computation.10 | convolution fusion | flops 169082880 | bytes 2981888 | tf_op jit(solution)/shard_map/dot_general | solution.py:37
  20.8 33.1 %all-to-all-done = bf16[16,32,2560]{2,1,0:T(8,128)(2,1)} async-done(((bf16[16,32,2560]{2,1,0:T(8,128)(2,1)}), bf16[16,32,2560]{2,1,0:T(8,128)(2,1)}, u32[]{:S(2)}, u32[]{:S(2)}) %all-to-all-start) | async-done | bytes 2621472 | tf_op jit(solution)/shard_map/all_to_all | solution.py:60
  53.9 4.5 %all-to-all-start.2 = ((bf16[16,32,2560]{2,1,0:T(8,128)(2,1)}), bf16[16,32,2560]{2,1,0:T(8,128)(2,1)S(1)}, u32[]{:S(2)}, u32[]{:S(2)}) async-start(bf16[16,32,2560]{2,1,0:T(8,128)(2,1)} %bitcast.16), calls=%async_computation.2 | async-start | bytes 5242880 | tf_op jit(solution)/shard_map/all_to_all | solution.py:60
  58.4 14.6 %fusion.8 = bf16[512,2560]{1,0:T(8,128)(2,1)} fusion(bf16[1,1,1152,2560]{3,2,1,0:T(8,128)(2,1)} %param.15, bf16[512,2560]{1,0:T(8,128)(2,1)} %bitcast.9, bf16[1,1,2560,1152]{3,2,1,0:T(8,128)(2,1)} %param.14), kind=kOutput, calls=%fused_computation.8 | convolution fusion | flops 6044057600 | bytes 17039360 | tf_op jit(solution)/shard_map/dot_general | solution.py:49
  73.0 23.0 %all-to-all-done.2 = bf16[16,32,2560]{2,1,0:T(8,128)(2,1)S(1)} async-done(((bf16[16,32,2560]{2,1,0:T(8,128)(2,1)}), bf16[16,32,2560]{2,1,0:T(8,128)(2,1)S(1)}, u32[]{:S(2)}, u32[]{:S(2)}) %all-to-all-start.2) | async-done | bytes 2621472 | tf_op jit(solution)/shard_map/all_to_all | solution.py:60
  96.1 1.5 copy-done.6
  97.6 4.9 %all-to-all-start.1 = ((bf16[16,32,2560]{2,1,0:T(8,128)(2,1)}), bf16[16,32,2560]{2,1,0:T(8,128)(2,1)S(1)}, u32[]{:S(2)}, u32[]{:S(2)}) async-start(bf16[16,32,2560]{2,1,0:T(8,128)(2,1)} %bitcast.114), calls=%async_computation.1 | async-start | bytes 5242880 | tf_op jit(solution)/shard_map/all_to_all | solution.py:60
  102.4 14.6 %fusion.11 = bf16[512,2560]{1,0:T(8,128)(2,1)} fusion(bf16[1,1,1152,2560]{3,2,1,0:T(8,128)(2,1)} %param.15, bf16[512,2560]{1,0:T(8,128)(2,1)} %bitcast.113, bf16[1,1,2560,1152]{3,2,1,0:T(8,128)(2,1)} %param.14), kind=kOutput, calls=%fused_computation.9 | convolution fusion | flops 6044057600 | bytes 17039360 | tf_op jit(solution)/shard_map/dot_general | solution.py:49
  117.0 23.0 %all-to-all-done.1 = bf16[16,32,2560]{2,1,0:T(8,128)(2,1)S(1)} async-done(((bf16[16,32,2560]{2,1,0:T(8,128)(2,1)}), bf16[16,32,2560]{2,1,0:T(8,128)(2,1)S(1)}, u32[]{:S(2)}, u32[]{:S(2)}) %all-to-all-start.1) | async-done | bytes 2621472 | tf_op jit(solution)/shard_map/all_to_all | solution.py:60
  140.0 1.5 copy-done.1
  141.6 4.9 %all-to-all-start.3 = ((bf16[16,32,2560]{2,1,0:T(8,128)(2,1)}), bf16[16,32,2560]{2,1,0:T(8,128)(2,1)S(1)}, u32[]{:S(2)}, u32[]{:S(2)}) async-start(bf16[16,32,2560]{2,1,0:T(8,128)(2,1)} %bitcast.112), calls=%async_computation.3 | async-start | bytes 5242880 | tf_op jit(solution)/shard_map/all_to_all | solution.py:60
  146.5 0.2 fusion.40
  146.8 0.2 fusion.38
  147.0 0.2 select_reduce_fusion.1
  147.2 0.2 select_reduce_fusion
  147.4 2.3 %fusion.47 = f32[64,2560]{1,0:T(8,128)S(1)} fusion(bf16[512,2560]{1,0:T(8,128)(2,1)} %bitcast.107, f32[64,512]{1,0:T(8,128)S(1)} %select_reduce_fusion.1), kind=kOutput, calls=%fused_computation.57 | convolution fusion | flops 167804928 | bytes 3407872 | tf_op jit(solution)/shard_map/dot_general | solution.py:53
  149.7 1.3 fusion.20
  151.1 3.3 %collective-permute-start = (bf16[1,64,2560]{2,1,0:T(8,128)(2,1)}, bf16[1,64,2560]{2,1,0:T(8,128)(2,1)}, u32[]{:S(2)}, u32[]{:S(2)}) collective-permute-start(bf16[1,64,2560]{2,1,0:T(8,128)(2,1)} %fusion.20), channel_id=1, source_target_pairs={{240,0},{0,16},{16,32},{32,48},{48,64},{64,80},{80,96},{96,112},{1... | collective-permute-start | bytes 983048 | tf_op jit(solution)/shard_map/ppermute | solution.py:12
  154.3 29.7 %all-to-all-done.3 = bf16[16,32,2560]{2,1,0:T(8,128)(2,1)S(1)} async-done(((bf16[16,32,2560]{2,1,0:T(8,128)(2,1)}), bf16[16,32,2560]{2,1,0:T(8,128)(2,1)S(1)}, u32[]{:S(2)}, u32[]{:S(2)}) %all-to-all-start.3) | async-done | bytes 2621472 | tf_op jit(solution)/shard_map/all_to_all | solution.py:60
  184.0 0.6 fusion.44
  184.6 0.6 fusion.21
  185.2 7.9 %collective-permute-start.1 = (bf16[1,64,2560]{2,1,0:T(8,128)(2,1)S(1)}, bf16[1,64,2560]{2,1,0:T(8,128)(2,1)S(1)}, u32[]{:S(2)}, u32[]{:S(2)}) collective-permute-start(bf16[1,64,2560]{2,1,0:T(8,128)(2,1)S(1)} %fusion.21), channel_id=1, source_target_pairs={{16,0},{32,16},{48,32},{64,48},{80,64},{96,80},{112,96},{128,112},... | collective-permute-start | bytes 983048 | tf_op jit(solution)/shard_map/ppermute | solution.py:12
  193.1 4.7 %collective-permute-done = bf16[1,64,2560]{2,1,0:T(8,128)(2,1)} collective-permute-done((bf16[1,64,2560]{2,1,0:T(8,128)(2,1)}, bf16[1,64,2560]{2,1,0:T(8,128)(2,1)}, u32[]{:S(2)}, u32[]{:S(2)}) %collective-permute-start) | collective-permute-done | bytes 327712 | tf_op jit(solution)/shard_map/ppermute | solution.py:12
  197.8 9.8 %collective-permute-done.1 = bf16[1,64,2560]{2,1,0:T(8,128)(2,1)S(1)} collective-permute-done((bf16[1,64,2560]{2,1,0:T(8,128)(2,1)S(1)}, bf16[1,64,2560]{2,1,0:T(8,128)(2,1)S(1)}, u32[]{:S(2)}, u32[]{:S(2)}) %collective-permute-start.1) | collective-permute-done | bytes 327712 | tf_op jit(solution)/shard_map/ppermute | solution.py:12
  207.6 1.7 copy.43
  209.4 0.7 copy.44
  (33 shorter events, 0.6 us)
Async XLA Ops:
  0.6 145.9 %copy-start = (bf16[1,2560,16]{1,2,0:T(8,128)(2,1)S(1)}, bf16[1,2560,16]{1,2,0:T(8,128)(2,1)}, u32[]{:S(2)}) copy-start(bf16[1,2560,16]{1,2,0:T(8,128)(2,1)} %param.13) | copy-start | bytes 245764
  9.6 8.3 %copy-start.4 = (bf16[1,64,2560]{2,1,0:T(8,128)(2,1)S(1)}, bf16[1,64,2560]{2,1,0:T(8,128)(2,1)}, u32[]{:S(2)}) copy-start(bf16[1,64,2560]{2,1,0:T(8,128)(2,1)} %param.9) | copy-start | bytes 983044
  9.6 44.3 %all-to-all-start = ((bf16[16,32,2560]{2,1,0:T(8,128)(2,1)}), bf16[16,32,2560]{2,1,0:T(8,128)(2,1)}, u32[]{:S(2)}, u32[]{:S(2)}) async-start(bf16[16,32,2560]{2,1,0:T(8,128)(2,1)} %bitcast.8), calls=%async_computation | async-start | bytes 5242880 | tf_op jit(solution)/shard_map/all_to_all | solution.py:60
  53.9 42.2 %all-to-all-start.2 = ((bf16[16,32,2560]{2,1,0:T(8,128)(2,1)}), bf16[16,32,2560]{2,1,0:T(8,128)(2,1)S(1)}, u32[]{:S(2)}, u32[]{:S(2)}) async-start(bf16[16,32,2560]{2,1,0:T(8,128)(2,1)} %bitcast.16), calls=%async_computation.2 | async-start | bytes 5242880 | tf_op jit(solution)/shard_map/all_to_all | solution.py:60
  96.1 1.5 copy-start.6
  97.6 42.5 %all-to-all-start.1 = ((bf16[16,32,2560]{2,1,0:T(8,128)(2,1)}), bf16[16,32,2560]{2,1,0:T(8,128)(2,1)S(1)}, u32[]{:S(2)}, u32[]{:S(2)}) async-start(bf16[16,32,2560]{2,1,0:T(8,128)(2,1)} %bitcast.114), calls=%async_computation.1 | async-start | bytes 5242880 | tf_op jit(solution)/shard_map/all_to_all | solution.py:60
  140.0 1.5 copy-start.1
  140.0 6.4 %copy-start.7 = (s32[1,64,6]{1,0,2:T(1,128)S(1)}, s32[1,64,6]{1,0,2:T(1,128)}, u32[]{:S(2)}) copy-start(s32[1,64,6]{1,0,2:T(1,128)} %param.10) | copy-start | bytes 4612
  141.6 42.5 %all-to-all-start.3 = ((bf16[16,32,2560]{2,1,0:T(8,128)(2,1)}), bf16[16,32,2560]{2,1,0:T(8,128)(2,1)S(1)}, u32[]{:S(2)}, u32[]{:S(2)}) async-start(bf16[16,32,2560]{2,1,0:T(8,128)(2,1)} %bitcast.112), calls=%async_computation.3 | async-start | bytes 5242880 | tf_op jit(solution)/shard_map/all_to_all | solution.py:60
  146.5 3.2 %copy-start.2 = (bf16[16,32,2560]{2,1,0:T(8,128)(2,1)S(1)}, bf16[16,32,2560]{2,1,0:T(8,128)(2,1)}, u32[]{:S(2)}) copy-start(bf16[16,32,2560]{2,1,0:T(8,128)(2,1)} %copy-done.1) | copy-start | bytes 7864324
  146.5 3.2 %copy-start.3 = (bf16[1,64,2560]{2,1,0:T(8,128)(2,1)S(1)}, bf16[1,64,2560]{2,1,0:T(8,128)(2,1)}, u32[]{:S(2)}) copy-start(bf16[1,64,2560]{2,1,0:T(8,128)(2,1)} %param.8) | copy-start | bytes 983044
  151.0 33.6 %copy-start.5 = (bf16[1,64,2560]{2,1,0:T(8,128)(2,1)S(1)}, bf16[1,64,2560]{2,1,0:T(8,128)(2,1)}, u32[]{:S(2)}) copy-start(bf16[1,64,2560]{2,1,0:T(8,128)(2,1)} %param.9) | copy-start | bytes 983044
  151.1 46.8 %collective-permute-start = (bf16[1,64,2560]{2,1,0:T(8,128)(2,1)}, bf16[1,64,2560]{2,1,0:T(8,128)(2,1)}, u32[]{:S(2)}, u32[]{:S(2)}) collective-permute-start(bf16[1,64,2560]{2,1,0:T(8,128)(2,1)} %fusion.20), channel_id=1, source_target_pairs={{240,0},{0,16},{16,32},{32,48},{48,64},{64,80},{80,96},{96,112},{1... | collective-permute-start | bytes 983048 | tf_op jit(solution)/shard_map/ppermute | solution.py:12
  185.2 22.4 %collective-permute-start.1 = (bf16[1,64,2560]{2,1,0:T(8,128)(2,1)S(1)}, bf16[1,64,2560]{2,1,0:T(8,128)(2,1)S(1)}, u32[]{:S(2)}, u32[]{:S(2)}) collective-permute-start(bf16[1,64,2560]{2,1,0:T(8,128)(2,1)S(1)} %fusion.21), channel_id=1, source_target_pairs={{16,0},{32,16},{48,32},{64,48},{80,64},{96,80},{112,96},{128,112},... | collective-permute-start | bytes 983048 | tf_op jit(solution)/shard_map/ppermute | solution.py:12

commit v5 on v3

--- a/solution.py
+++ b/solution.py
@@ -67,12 +67,17 @@
     down_w = w_down[0, 0]
     send_up, hi_up, lo_up = layer_route(up_in[0], up_ids[0], gain, table)
     send_down, hi_down, lo_down = layer_route(down_in[0], down_ids[0], gain, table)
-    rows_up = exchange(send_up)
-    rows_down = exchange(send_down)
+    owners = lax.axis_size("expert")
+    width = send_up.shape[-1]
+    both = jnp.stack(
+        [send_up.reshape(owners, -1, width), send_down.reshape(owners, -1, width)], axis=1
+    )
+    arrived = exchange(both.reshape(-1, width)).reshape(owners, 2, -1, width)
+    rows_up = arrived[:, 0].reshape(-1, width)
+    rows_down = arrived[:, 1].reshape(-1, width)
     back_up = exchange(apply_experts(rows_up, up_w, down_w))
     back_down = exchange(apply_experts(rows_down, up_w, down_w))
     layer_up = finish(up_in[0], hi_up, lo_up, back_up)
-    layer_up, back_down = lax.optimization_barrier((layer_up, back_down))
     up_out = shifted(layer_up[None], "pipe", 1)
     layer_down = finish(down_in[0], hi_down, lo_down, back_down)
     down_out = shifted(layer_down[None], "pipe", -1)

time: 216 us -> 210 us (0.972)
  blocking collectives: 0 us -> 65.2 us
  waiting for transfers between devices: 134 us -> 69.9 us
  starting transfers between devices: 28.9 us -> 21.5 us
  local copies, waits for them, and re-layouts: 3.79 us -> 8.86 us
  matrix products: 40.2 us -> 35.3 us
    all_to_all x0 -> x1, blocking collectives: none -> 65.2 us  [exchange(): lax.all_to_all(block, 'expert', split_axis=0, concat_axis=0, tiled=True)]
    all_to_all x4 -> x2, waiting for transfers between devices: 115 us -> 53.2 us  [exchange(): lax.all_to_all(block, 'expert', split_axis=0, concat_axis=0, tiled=True)]
    all_to_all x4 -> x2, starting transfers between devices: 21 us -> 10.3 us  [exchange(): lax.all_to_all(block, 'expert', split_axis=0, concat_axis=0, tiled=True)]
    ppermute x2, starting transfers between devices: 7.93 us -> 11.2 us  [shifted(): return lax.ppermute(block, axis, route)]
    unnamed x16 -> x18, local copies, waits for them, and re-layouts: 2.39 us -> 5.58 us
    dot_general x2, matrix products: 4.8 us -> 1.78 us  [layer_route(): lax.dot_general(place, normed, (((0,), (0,)), ((), ())), preferred_elemen...]
    ppermute x2, waiting for transfers between devices: 19.1 us -> 16.7 us  [shifted(): return lax.ppermute(block, axis, route)]
  transfers between devices with their start and end apart: 6 -> 4, of which waited for: 6 -> 3; matrix products, arithmetic and copies ran while one was open for 17% -> 10% of each run, Pallas kernels for 0% -> 0%
where the time goes in v5:
time: 210 us; the launch traced here: 209 us
  waiting for transfers between devices  69.9 us (33%)
  blocking collectives  65.2 us (31%)
  matrix products  35.3 us (17%)
  starting transfers between devices  21.5 us (10%)
  local copies, waits for them, and re-layouts  8.86 us (4%)
  other arithmetic  7.7 us (4%)
    all_to_all x1, blocking collectives, exchange(): lax.all_to_all(block, 'expert', split_axis=0, concat_axis=0, tiled=True)  65.2 us
    all_to_all x2, waiting for transfers between devices, exchange(): lax.all_to_all(block, 'expert', split_axis=0, concat_axis=0, tiled=True)  53.2 us
    dot_general x2, matrix products, apply_experts(): jnp.dot(hidden, down_w, preferred_element_type=jnp.float32)  28.4 us
    ppermute x2, waiting for transfers between devices, shifted(): return lax.ppermute(block, axis, route)  16.7 us
    ppermute x2, starting transfers between devices, shifted(): return lax.ppermute(block, axis, route)  11.2 us
    all_to_all x2, starting transfers between devices, exchange(): lax.all_to_all(block, 'expert', split_axis=0, concat_axis=0, tiled=True)  10.3 us
    unnamed x18, local copies, waits for them, and re-layouts  5.58 us
  transfers between devices with their start and end apart: 4, of which 3 were waited for; matrix products, arithmetic and copies ran while one was open for 10% of the time, Pallas kernels for 0%

profile of v5, /device:TPU:6, one launch (start us, length us, event | category | flops | bytes accessed | tf_op | source)
XLA Modules:
  0.0 209.4 jit_solution(700177077048493932)
XLA Ops:
  0.6 0.0 copy-start
  0.6 0.8 copy.28
  1.5 0.1 eq.94
  1.6 0.1 eq.90
  1.7 0.8 copy.34
  2.5 0.1 eq.108
  2.6 0.1 eq.104
  2.8 1.1 fusion.32
  3.9 1.1 fusion.35
  5.1 0.9 reduce-window.14
  6.0 0.2 slice_reduce_fusion.1
  6.2 0.1 fusion.55
  6.3 0.1 reshape.145
  6.5 0.1 copy.32
  6.6 0.9 reduce-window.16
  7.4 0.2 slice_reduce_fusion
  7.7 0.1 fusion.52
  7.8 0.1 reshape.147
  7.9 0.1 copy.38
  8.0 0.2 fusion.26
  8.2 0.2 fusion.27
  8.4 0.7 reduce.1
  9.1 1.3 fusion.34
  10.4 0.9 convolution_convert_fusion.1
  11.3 0.9 convolution_convert_fusion
  12.2 0.5 pad_maximum_fusion
  12.7 65.2 %all_to_all.33 = bf16[16,64,2560]{2,1,0:T(8,128)(2,1)S(1)} all-to-all(bf16[16,64,2560]{2,1,0:T(8,128)(2,1)S(1)} %bitcast.126), channel_id=1, replica_groups=mesh['pipe'=16,'expert'=16] {'expert'}, dimensions={0} | all-to-all | bytes 10485760 | tf_op jit(solution)/shard_map/all_to_all | solution.py:60
  77.9 1.9 fusion.60
  79.8 13.8 %fusion.11 = bf16[512,2560]{1,0:T(8,128)(2,1)} fusion(bf16[1,1,1152,2560]{3,2,1,0:T(8,128)(2,1)} %param.15, bf16[512,2560]{1,0:T(8,128)(2,1)S(1)} %bitcast.130, bf16[1,1,2560,1152]{3,2,1,0:T(8,128)(2,1)} %param.14), kind=kOutput, calls=%fused_computation.10 | convolution fusion | flops 6044057600 | bytes 17039360 | tf_op jit(solution)/shard_map/dot_general | solution.py:49
  93.6 5.8 %all-to-all-start.2 = ((bf16[16,32,2560]{2,1,0:T(8,128)(2,1)}), bf16[16,32,2560]{2,1,0:T(8,128)(2,1)S(1)}, u32[]{:S(2)}, u32[]{:S(2)}) async-start(bf16[16,32,2560]{2,1,0:T(8,128)(2,1)} %bitcast.132), calls=%async_computation.2 | async-start | bytes 5242880 | tf_op jit(solution)/shard_map/all_to_all | solution.py:60
  99.4 14.6 %fusion.8 = bf16[512,2560]{1,0:T(8,128)(2,1)} fusion(bf16[1,1,1152,2560]{3,2,1,0:T(8,128)(2,1)} %param.15, bf16[512,2560]{1,0:T(8,128)(2,1)} %bitcast.129, bf16[1,1,2560,1152]{3,2,1,0:T(8,128)(2,1)} %param.14), kind=kOutput, calls=%fused_computation.9 | convolution fusion | flops 6044057600 | bytes 17039360 | tf_op jit(solution)/shard_map/dot_general | solution.py:49
  114.0 23.1 %all-to-all-done.2 = bf16[16,32,2560]{2,1,0:T(8,128)(2,1)S(1)} async-done(((bf16[16,32,2560]{2,1,0:T(8,128)(2,1)}), bf16[16,32,2560]{2,1,0:T(8,128)(2,1)S(1)}, u32[]{:S(2)}, u32[]{:S(2)}) %all-to-all-start.2) | async-done | bytes 2621472 | tf_op jit(solution)/shard_map/all_to_all | solution.py:60
  137.1 1.5 copy-done.1
  138.6 4.5 %all-to-all-start.1 = ((bf16[16,32,2560]{2,1,0:T(8,128)(2,1)}), bf16[16,32,2560]{2,1,0:T(8,128)(2,1)S(1)}, u32[]{:S(2)}, u32[]{:S(2)}) async-start(bf16[16,32,2560]{2,1,0:T(8,128)(2,1)} %bitcast.131), calls=%async_computation.1 | async-start | bytes 5242880 | tf_op jit(solution)/shard_map/all_to_all | solution.py:60
  143.2 0.2 fusion.38
  143.5 0.2 fusion.40
  143.7 0.2 select_reduce_fusion.1
  143.9 0.2 select_reduce_fusion
  144.1 2.3 %fusion.45 = f32[64,2560]{1,0:T(8,128)S(1)} fusion(bf16[512,2560]{1,0:T(8,128)(2,1)} %bitcast.123, f32[64,512]{1,0:T(8,128)S(1)} %select_reduce_fusion), kind=kOutput, calls=%fused_computation.56 | convolution fusion | flops 167804928 | bytes 3407872 | tf_op jit(solution)/shard_map/dot_general | solution.py:53
  146.4 1.3 fusion.21
  147.7 7.9 %collective-permute-start.1 = (bf16[1,64,2560]{2,1,0:T(8,128)(2,1)}, bf16[1,64,2560]{2,1,0:T(8,128)(2,1)}, u32[]{:S(2)}, u32[]{:S(2)}) collective-permute-start(bf16[1,64,2560]{2,1,0:T(8,128)(2,1)} %fusion.21), channel_id=1, source_target_pairs={{16,0},{32,16},{48,32},{64,48},{80,64},{96,80},{112,96},{128,112},... | collective-permute-start | bytes 983048 | tf_op jit(solution)/shard_map/ppermute | solution.py:12
  155.6 30.1 %all-to-all-done.1 = bf16[16,32,2560]{2,1,0:T(8,128)(2,1)S(1)} async-done(((bf16[16,32,2560]{2,1,0:T(8,128)(2,1)}), bf16[16,32,2560]{2,1,0:T(8,128)(2,1)S(1)}, u32[]{:S(2)}, u32[]{:S(2)}) %all-to-all-start.1) | async-done | bytes 2621472 | tf_op jit(solution)/shard_map/all_to_all | solution.py:60
  185.7 0.6 fusion.48
  186.3 0.6 fusion.20
  186.9 3.3 %collective-permute-start = (bf16[1,64,2560]{2,1,0:T(8,128)(2,1)S(1)}, bf16[1,64,2560]{2,1,0:T(8,128)(2,1)S(1)}, u32[]{:S(2)}, u32[]{:S(2)}) collective-permute-start(bf16[1,64,2560]{2,1,0:T(8,128)(2,1)S(1)} %fusion.20), channel_id=1, source_target_pairs={{240,0},{0,16},{16,32},{32,48},{48,64},{64,80},{80,96},{96,112},{1... | collective-permute-start | bytes 983048 | tf_op jit(solution)/shard_map/ppermute | solution.py:12
  190.2 16.7 %collective-permute-done = bf16[1,64,2560]{2,1,0:T(8,128)(2,1)S(1)} collective-permute-done((bf16[1,64,2560]{2,1,0:T(8,128)(2,1)S(1)}, bf16[1,64,2560]{2,1,0:T(8,128)(2,1)S(1)}, u32[]{:S(2)}, u32[]{:S(2)}) %collective-permute-start) | collective-permute-done | bytes 327712 | tf_op jit(solution)/shard_map/ppermute | solution.py:12
  206.9 0.7 copy.54
  207.7 1.7 copy.55
  (28 shorter events, 0.3 us)
Async XLA Ops:
  0.6 142.6 %copy-start = (bf16[1,2560,16]{1,2,0:T(8,128)(2,1)S(1)}, bf16[1,2560,16]{1,2,0:T(8,128)(2,1)}, u32[]{:S(2)}) copy-start(bf16[1,2560,16]{1,2,0:T(8,128)(2,1)} %param.13) | copy-start | bytes 245764
  93.6 43.5 %all-to-all-start.2 = ((bf16[16,32,2560]{2,1,0:T(8,128)(2,1)}), bf16[16,32,2560]{2,1,0:T(8,128)(2,1)S(1)}, u32[]{:S(2)}, u32[]{:S(2)}) async-start(bf16[16,32,2560]{2,1,0:T(8,128)(2,1)} %bitcast.132), calls=%async_computation.2 | async-start | bytes 5242880 | tf_op jit(solution)/shard_map/all_to_all | solution.py:60
  137.1 1.5 copy-start.1
  137.1 6.1 %copy-start.5 = (s32[1,64,6]{1,0,2:T(1,128)S(1)}, s32[1,64,6]{1,0,2:T(1,128)}, u32[]{:S(2)}) copy-start(s32[1,64,6]{1,0,2:T(1,128)} %param.10) | copy-start | bytes 4612
  137.1 6.1 %copy-start.6 = (s32[1,64,6]{1,0,2:T(1,128)S(1)}, s32[1,64,6]{1,0,2:T(1,128)}, u32[]{:S(2)}) copy-start(s32[1,64,6]{1,0,2:T(1,128)} %param.11) | copy-start | bytes 4612
  138.6 47.1 %all-to-all-start.1 = ((bf16[16,32,2560]{2,1,0:T(8,128)(2,1)}), bf16[16,32,2560]{2,1,0:T(8,128)(2,1)S(1)}, u32[]{:S(2)}, u32[]{:S(2)}) async-start(bf16[16,32,2560]{2,1,0:T(8,128)(2,1)} %bitcast.131), calls=%async_computation.1 | async-start | bytes 5242880 | tf_op jit(solution)/shard_map/all_to_all | solution.py:60
  143.1 3.3 %copy-start.2 = (bf16[16,32,2560]{2,1,0:T(8,128)(2,1)S(1)}, bf16[16,32,2560]{2,1,0:T(8,128)(2,1)}, u32[]{:S(2)}) copy-start(bf16[16,32,2560]{2,1,0:T(8,128)(2,1)} %copy-done.1) | copy-start | bytes 7864324
  143.2 3.3 %copy-start.3 = (bf16[1,64,2560]{2,1,0:T(8,128)(2,1)S(1)}, bf16[1,64,2560]{2,1,0:T(8,128)(2,1)}, u32[]{:S(2)}) copy-start(bf16[1,64,2560]{2,1,0:T(8,128)(2,1)} %param.9) | copy-start | bytes 983044
  147.7 38.5 %copy-start.4 = (bf16[1,64,2560]{2,1,0:T(8,128)(2,1)S(1)}, bf16[1,64,2560]{2,1,0:T(8,128)(2,1)}, u32[]{:S(2)}) copy-start(bf16[1,64,2560]{2,1,0:T(8,128)(2,1)} %param.8) | copy-start | bytes 983044
  147.7 42.5 %collective-permute-start.1 = (bf16[1,64,2560]{2,1,0:T(8,128)(2,1)}, bf16[1,64,2560]{2,1,0:T(8,128)(2,1)}, u32[]{:S(2)}, u32[]{:S(2)}) collective-permute-start(bf16[1,64,2560]{2,1,0:T(8,128)(2,1)} %fusion.21), channel_id=1, source_target_pairs={{16,0},{32,16},{48,32},{64,48},{80,64},{96,80},{112,96},{128,112},... | collective-permute-start | bytes 983048 | tf_op jit(solution)/shard_map/ppermute | solution.py:12
  186.9 20.1 %collective-permute-start = (bf16[1,64,2560]{2,1,0:T(8,128)(2,1)S(1)}, bf16[1,64,2560]{2,1,0:T(8,128)(2,1)S(1)}, u32[]{:S(2)}, u32[]{:S(2)}) collective-permute-start(bf16[1,64,2560]{2,1,0:T(8,128)(2,1)S(1)} %fusion.20), channel_id=1, source_target_pairs={{240,0},{0,16},{16,32},{32,48},{48,64},{64,80},{80,96},{96,112},{1... | collective-permute-start | bytes 983048 | tf_op jit(solution)/shard_map/ppermute | solution.py:12

commit v6 on v5

--- a/solution.py
+++ b/solution.py
@@ -72,11 +72,10 @@
     both = jnp.stack(
         [send_up.reshape(owners, -1, width), send_down.reshape(owners, -1, width)], axis=1
     )
-    arrived = exchange(both.reshape(-1, width)).reshape(owners, 2, -1, width)
-    rows_up = arrived[:, 0].reshape(-1, width)
-    rows_down = arrived[:, 1].reshape(-1, width)
-    back_up = exchange(apply_experts(rows_up, up_w, down_w))
-    back_down = exchange(apply_experts(rows_down, up_w, down_w))
+    arrived = exchange(both.reshape(-1, width))
+    back = exchange(apply_experts(arrived, up_w, down_w)).reshape(owners, 2, -1, width)
+    back_up = back[:, 0].reshape(-1, width)
+    back_down = back[:, 1].reshape(-1, width)
     layer_up = finish(up_in[0], hi_up, lo_up, back_up)
     up_out = shifted(layer_up[None], "pipe", 1)
     layer_down = finish(down_in[0], hi_down, lo_down, back_down)

time: 210 us -> 215 us (1.024)
  waiting for transfers between devices: 69.9 us -> 91.1 us
  matrix products: 35.3 us -> 27 us
  starting transfers between devices: 21.5 us -> 14.8 us
    all_to_all x2 -> x1, waiting for transfers between devices: 53.2 us -> 77.1 us  [exchange(): lax.all_to_all(block, 'expert', split_axis=0, concat_axis=0, tiled=True)]
    dot_general x2 -> x1, matrix products: 28.4 us -> 22.5 us  [apply_experts(): jnp.dot(hidden, down_w, preferred_element_type=jnp.float32)]
    all_to_all x2 -> x1, starting transfers between devices: 10.3 us -> 6.75 us  [exchange(): lax.all_to_all(block, 'expert', split_axis=0, concat_axis=0, tiled=True)]
    ppermute x2, starting transfers between devices: 11.2 us -> 8.02 us  [shifted(): return lax.ppermute(block, axis, route)]
    ppermute x2, waiting for transfers between devices: 16.7 us -> 14 us  [shifted(): return lax.ppermute(block, axis, route)]
    unnamed x18 -> x14, local copies, waits for them, and re-layouts: 5.58 us -> 3.06 us
  transfers between devices with their start and end apart: 4 -> 3, of which waited for: 3 -> 3; matrix products, arithmetic and copies ran while one was open for 10% -> 1% of each run, Pallas kernels for 0% -> 0%
where the time goes in v6:
time: 215 us; the launch traced here: 214 us
  waiting for transfers between devices  91.1 us (42%)
  blocking collectives  65.3 us (30%)
  matrix products  27 us (13%)
  starting transfers between devices  14.8 us (7%)
  other arithmetic  7.7 us (4%)
  local copies, waits for them, and re-layouts  7.38 us (3%)
    all_to_all x1, waiting for transfers between devices, exchange(): lax.all_to_all(block, 'expert', split_axis=0, concat_axis=0, tiled=True)  77.1 us
    all_to_all x1, blocking collectives, exchange(): lax.all_to_all(block, 'expert', split_axis=0, concat_axis=0, tiled=True)  65.3 us
    dot_general x1, matrix products, apply_experts(): jnp.dot(hidden, down_w, preferred_element_type=jnp.float32)  22.5 us
    ppermute x2, waiting for transfers between devices, shifted(): return lax.ppermute(block, axis, route)  14 us
    ppermute x2, starting transfers between devices, shifted(): return lax.ppermute(block, axis, route)  8.02 us
    all_to_all x1, starting transfers between devices, exchange(): lax.all_to_all(block, 'expert', split_axis=0, concat_axis=0, tiled=True)  6.75 us
  transfers between devices with their start and end apart: 3, of which 3 were waited for; matrix products, arithmetic and copies ran while one was open for 1% of the time, Pallas kernels for 0%

profile of v6, /device:TPU:6, one launch (start us, length us, event | category | flops | bytes accessed | tf_op | source)
XLA Modules:
  0.0 214.2 jit_solution(6640880489439365151)
XLA Ops:
  0.6 0.0 copy-start
  0.6 0.8 copy.28
  1.5 0.1 eq.94
  1.6 0.1 eq.90
  1.7 0.8 copy.34
  2.5 0.1 eq.108
  2.6 0.1 eq.104
  2.8 1.1 fusion.22
  3.9 1.1 fusion.25
  5.1 0.9 reduce-window.14
  6.0 0.2 slice_reduce_fusion.1
  6.2 0.1 fusion.45
  6.3 0.1 reshape.143
  6.5 0.1 copy.32
  6.6 0.9 reduce-window.16
  7.4 0.2 slice_reduce_fusion
  7.7 0.1 fusion.42
  7.8 0.1 reshape.145
  7.9 0.1 copy.38
  8.0 0.2 fusion.20
  8.2 0.2 fusion.21
  8.4 0.7 reduce.1
  9.1 1.3 fusion.24
  10.4 0.9 convolution_convert_fusion.1
  11.3 0.9 convolution_convert_fusion
  12.2 0.5 pad_maximum_fusion
  12.7 65.3 %all_to_all.21 = bf16[16,64,2560]{2,1,0:T(8,128)(2,1)} all-to-all(bf16[16,64,2560]{2,1,0:T(8,128)(2,1)S(1)} %bitcast.112), channel_id=1, replica_groups=mesh['pipe'=16,'expert'=16] {'expert'}, dimensions={0} | all-to-all | bytes 10485760 | tf_op jit(solution)/shard_map/all_to_all | solution.py:60
  78.0 22.5 %fusion.4 = bf16[1024,2560]{1,0:T(8,128)(2,1)} fusion(bf16[1,1,1152,2560]{3,2,1,0:T(8,128)(2,1)} %param.15, bf16[1024,2560]{1,0:T(8,128)(2,1)} %bitcast.116, bf16[1,1,2560,1152]{3,2,1,0:T(8,128)(2,1)} %param.14), kind=kOutput, calls=%fused_computation.4 | convolution fusion | flops 12088115200 | bytes 22282240 | tf_op jit(solution)/shard_map/dot_general | solution.py:49
  100.6 6.7 %all-to-all-start.1 = ((bf16[16,64,2560]{2,1,0:T(8,128)(2,1)}), bf16[16,64,2560]{2,1,0:T(8,128)(2,1)}, u32[]{:S(2)}, u32[]{:S(2)}) async-start(bf16[16,64,2560]{2,1,0:T(8,128)(2,1)} %bitcast.115), calls=%async_computation.1 | async-start | bytes 10485760 | tf_op jit(solution)/shard_map/all_to_all | solution.py:60
  107.3 0.0 copy-done.3
  107.3 0.0 copy-done.4
  107.4 0.2 fusion.28
  107.6 0.2 fusion.30
  107.9 0.2 select_reduce_fusion.1
  108.1 0.2 select_reduce_fusion
  108.3 77.1 %all-to-all-done.1 = bf16[16,64,2560]{2,1,0:T(8,128)(2,1)} async-done(((bf16[16,64,2560]{2,1,0:T(8,128)(2,1)}), bf16[16,64,2560]{2,1,0:T(8,128)(2,1)}, u32[]{:S(2)}, u32[]{:S(2)}) %all-to-all-start.1) | async-done | bytes 5242912 | tf_op jit(solution)/shard_map/all_to_all | solution.py:60
  185.4 2.9 %fusion.49 = (bf16[16,1,32,2560]{3,2,1,0:T(8,128)(2,1)S(1)}, bf16[16,1,32,2560]{3,2,1,0:T(8,128)(2,1)S(1)}) fusion(bf16[16,2,32,2560]{3,2,1,0:T(8,128)(2,1)} %bitcast.19), kind=kLoop, calls=%fused_computation.85 | loop fusion | bytes 10485760 | tf_op jit(solution)/shard_map/slice | solution.py:78
  188.3 0.0 copy-start.2
  188.3 0.6 fusion.38
  188.9 0.6 fusion.17
  189.5 3.3 %collective-permute-start = (bf16[1,64,2560]{2,1,0:T(8,128)(2,1)S(1)}, bf16[1,64,2560]{2,1,0:T(8,128)(2,1)S(1)}, u32[]{:S(2)}, u32[]{:S(2)}) collective-permute-start(bf16[1,64,2560]{2,1,0:T(8,128)(2,1)S(1)} %fusion.17), channel_id=1, source_target_pairs={{240,0},{0,16},{16,32},{32,48},{48,64},{64,80},{80,96},{96,112},{1... | collective-permute-start | bytes 983048 | tf_op jit(solution)/shard_map/ppermute | solution.py:12
  192.8 0.6 fusion.35
  193.4 0.6 fusion.18
  194.0 4.7 %collective-permute-start.1 = (bf16[1,64,2560]{2,1,0:T(8,128)(2,1)S(1)}, bf16[1,64,2560]{2,1,0:T(8,128)(2,1)S(1)}, u32[]{:S(2)}, u32[]{:S(2)}) collective-permute-start(bf16[1,64,2560]{2,1,0:T(8,128)(2,1)S(1)} %fusion.18), channel_id=1, source_target_pairs={{16,0},{32,16},{48,32},{64,48},{80,64},{96,80},{112,96},{128,112},... | collective-permute-start | bytes 983048 | tf_op jit(solution)/shard_map/ppermute | solution.py:12
  198.7 11.0 %collective-permute-done = bf16[1,64,2560]{2,1,0:T(8,128)(2,1)S(1)} collective-permute-done((bf16[1,64,2560]{2,1,0:T(8,128)(2,1)S(1)}, bf16[1,64,2560]{2,1,0:T(8,128)(2,1)S(1)}, u32[]{:S(2)}, u32[]{:S(2)}) %collective-permute-start) | collective-permute-done | bytes 327712 | tf_op jit(solution)/shard_map/ppermute | solution.py:12
  209.7 3.0 %collective-permute-done.1 = bf16[1,64,2560]{2,1,0:T(8,128)(2,1)S(1)} collective-permute-done((bf16[1,64,2560]{2,1,0:T(8,128)(2,1)S(1)}, bf16[1,64,2560]{2,1,0:T(8,128)(2,1)S(1)}, u32[]{:S(2)}, u32[]{:S(2)}) %collective-permute-start.1) | collective-permute-done | bytes 327712 | tf_op jit(solution)/shard_map/ppermute | solution.py:12
  212.7 0.7 copy.54
  213.4 0.7 copy.55
  (21 shorter events, 0.3 us)
Async XLA Ops:
  0.6 106.7 %copy-start = (bf16[1,2560,16]{1,2,0:T(8,128)(2,1)S(1)}, bf16[1,2560,16]{1,2,0:T(8,128)(2,1)}, u32[]{:S(2)}) copy-start(bf16[1,2560,16]{1,2,0:T(8,128)(2,1)} %param.13) | copy-start | bytes 245764
  100.6 6.8 %copy-start.3 = (s32[1,64,6]{1,0,2:T(1,128)S(1)}, s32[1,64,6]{1,0,2:T(1,128)}, u32[]{:S(2)}) copy-start(s32[1,64,6]{1,0,2:T(1,128)} %param.10) | copy-start | bytes 4612
  100.6 6.8 %copy-start.4 = (s32[1,64,6]{1,0,2:T(1,128)S(1)}, s32[1,64,6]{1,0,2:T(1,128)}, u32[]{:S(2)}) copy-start(s32[1,64,6]{1,0,2:T(1,128)} %param.11) | copy-start | bytes 4612
  100.6 84.8 %all-to-all-start.1 = ((bf16[16,64,2560]{2,1,0:T(8,128)(2,1)}), bf16[16,64,2560]{2,1,0:T(8,128)(2,1)}, u32[]{:S(2)}, u32[]{:S(2)}) async-start(bf16[16,64,2560]{2,1,0:T(8,128)(2,1)} %bitcast.115), calls=%async_computation.1 | async-start | bytes 10485760 | tf_op jit(solution)/shard_map/all_to_all | solution.py:60
  185.4 3.5 %copy-start.1 = (bf16[1,64,2560]{2,1,0:T(8,128)(2,1)S(1)}, bf16[1,64,2560]{2,1,0:T(8,128)(2,1)}, u32[]{:S(2)}) copy-start(bf16[1,64,2560]{2,1,0:T(8,128)(2,1)} %param.8) | copy-start | bytes 983044
  188.3 5.1 %copy-start.2 = (bf16[1,64,2560]{2,1,0:T(8,128)(2,1)S(1)}, bf16[1,64,2560]{2,1,0:T(8,128)(2,1)}, u32[]{:S(2)}) copy-start(bf16[1,64,2560]{2,1,0:T(8,128)(2,1)} %param.9) | copy-start | bytes 983044
  189.5 20.2 %collective-permute-start = (bf16[1,64,2560]{2,1,0:T(8,128)(2,1)S(1)}, bf16[1,64,2560]{2,1,0:T(8,128)(2,1)S(1)}, u32[]{:S(2)}, u32[]{:S(2)}) collective-permute-start(bf16[1,64,2560]{2,1,0:T(8,128)(2,1)S(1)} %fusion.17), channel_id=1, source_target_pairs={{240,0},{0,16},{16,32},{32,48},{48,64},{64,80},{80,96},{96,112},{1... | collective-permute-start | bytes 983048 | tf_op jit(solution)/shard_map/ppermute | solution.py:12
  194.0 18.7 %collective-permute-start.1 = (bf16[1,64,2560]{2,1,0:T(8,128)(2,1)S(1)}, bf16[1,64,2560]{2,1,0:T(8,128)(2,1)S(1)}, u32[]{:S(2)}, u32[]{:S(2)}) collective-permute-start(bf16[1,64,2560]{2,1,0:T(8,128)(2,1)S(1)} %fusion.18), channel_id=1, source_target_pairs={{16,0},{32,16},{48,32},{64,48},{80,64},{96,80},{112,96},{128,112},... | collective-permute-start | bytes 983048 | tf_op jit(solution)/shard_map/ppermute | solution.py:12

commit v7 on v1

--- a/solution.py
+++ b/solution.py
@@ -1,9 +1,40 @@
 import jax
 import jax.numpy as jnp
 from jax import lax
+from jax.experimental import pallas as pl
 from jax.sharding import PartitionSpec as P
 
 CAP = 32
+
+def dispatch_kernel(x_ref, gain_ref, ids_ref, send_ref, normed_ref):
+    tokens, width = x_ref.shape
+    rows = send_ref.shape[0]
+    xf = x_ref[...].astype(jnp.float32)
+    ms = jnp.mean(xf * xf, axis=-1, keepdims=True)
+    normed = (xf * lax.rsqrt(ms + 1e-06) * gain_ref[...]).astype(jnp.bfloat16)
+    normed_ref[...] = normed
+    ids = ids_ref[...]
+    owner = lax.broadcasted_iota(jnp.int32, (tokens, rows), 1) // CAP
+    member = ids[:, 0:1] == owner
+    for k in range(1, ids.shape[1]):
+        member = member | (ids[:, k:k + 1] == owner)
+    member = member.astype(jnp.float32)
+    earlier = (lax.broadcasted_iota(jnp.int32, (tokens, tokens), 1)
+               < lax.broadcasted_iota(jnp.int32, (tokens, tokens), 0)).astype(jnp.bfloat16)
+    slot = jnp.dot(earlier, member.astype(jnp.bfloat16), preferred_element_type=jnp.float32)
+    offset = (lax.broadcasted_iota(jnp.int32, (tokens, rows), 1) % CAP).astype(jnp.float32)
+    place = jnp.where(slot == offset, member, 0.0)
+    place_t = place.T.astype(jnp.bfloat16)
+    send_ref[...] = jnp.dot(place_t, normed, preferred_element_type=jnp.float32).astype(jnp.bfloat16)
+
+def dispatch(x, gain, ids, experts):
+    tokens, width = x.shape
+    rows = experts * CAP
+    return pl.pallas_call(
+        dispatch_kernel,
+        out_shape=(jax.ShapeDtypeStruct((rows, width), jnp.bfloat16),
+                   jax.ShapeDtypeStruct((tokens, width), jnp.bfloat16)),
+    )(x, gain.reshape(1, width), ids)
 
 
 def shifted(block, axis, distance):
@@ -16,10 +47,7 @@
     tokens_here = x.shape[0]
     experts = table.shape[1]
     choose = ids.shape[1]
-    xf = x.astype(jnp.float32)
-    normed = (xf * lax.rsqrt(jnp.mean(xf * xf, axis=-1, keepdims=True) + 1e-06) * gain).astype(
-        jnp.bfloat16
-    )
+    send, normed = dispatch(x, gain, ids, experts)
     logits = jnp.dot(normed, table, preferred_element_type=jnp.float32)
     chosen = jnp.take_along_axis(logits, ids, axis=1)
     score = jax.nn.sigmoid(chosen)
@@ -33,10 +61,6 @@
     target = ids * CAP + slot
     rows = jnp.arange(experts * CAP, dtype=jnp.int32)
     hit = target[:, :, None] == rows[None, None, :]
-    place = jnp.any(hit, axis=1).astype(jnp.bfloat16)
-    send = lax.dot_general(
-        place, normed, (((0,), (0,)), ((), ())), preferred_element_type=jnp.float32
-    ).astype(jnp.bfloat16)
     weight = jnp.sum(jnp.where(hit, gates[:, :, None], 0.0), axis=1)
     weight_hi = weight.astype(jnp.bfloat16)
     weight_lo = (weight - weight_hi.astype(jnp.float32)).astype(jnp.bfloat16)

time: 208 us -> 208 us (level)
  Pallas kernels: 0 us -> 7.41 us
  matrix products: 39.8 us -> 33.7 us
  other arithmetic: 5.62 us -> 2.86 us
    pallas_call x0 -> x2, Pallas kernels: none -> 7.41 us  [dispatch(): pl.pallas_call(dispatch_kernel, out_shape=(jax.ShapeDtypeStruct((rows, wi...]
    dot_general x2 -> x0, matrix products: 5.85 us -> none  [layer_route(): lax.dot_general(place, normed, (((0,), (0,)), ((), ())), preferred_elemen...]
    unnamed x18 -> x24, local copies, waits for them, and re-layouts: 3.9 us -> 5.12 us
    gather x10 -> x6, local copies, waits for them, and re-layouts: 6.85 us -> 6.53 us  [layer_route(): chosen = jnp.take_along_axis(logits, ids, axis=1)]
  transfers between devices with their start and end apart: 6 -> 6, of which waited for: 6 -> 5; matrix products, arithmetic and copies ran while one was open for 22% -> 22% of each run, Pallas kernels for 0% -> 2%
where the time goes in v7:
time: 208 us; the launch traced here: 206 us
  waiting for transfers between devices  116 us (56%)
  matrix products  33.7 us (16%)
  starting transfers between devices  32.4 us (16%)
  local copies, waits for them, and re-layouts  13.2 us (6%)
  Pallas kernels  7.41 us (4%)
  other arithmetic  2.86 us (1%)
    all_to_all x4, waiting for transfers between devices, exchange(): lax.all_to_all(block, 'expert', split_axis=0, concat_axis=0, tiled=True)  101 us
    dot_general x2, matrix products, apply_experts(): jnp.dot(hidden, down_w, preferred_element_type=jnp.float32)  28.4 us
    all_to_all x4, starting transfers between devices, exchange(): lax.all_to_all(block, 'expert', split_axis=0, concat_axis=0, tiled=True)  20.9 us
    ppermute x2, waiting for transfers between devices, shifted(): return lax.ppermute(block, axis, route)  14.9 us
    ppermute x2, starting transfers between devices, shifted(): return lax.ppermute(block, axis, route)  11.5 us
    pallas_call x2, Pallas kernels, dispatch(): pl.pallas_call(dispatch_kernel, out_shape=(jax.ShapeDtypeStruct((rows, wi...  7.41 us
    gather x6, local copies, waits for them, and re-layouts, layer_route(): chosen = jnp.take_along_axis(logits, ids, axis=1)  6.53 us
    unnamed x24, local copies, waits for them, and re-layouts  5.12 us
  transfers between devices with their start and end apart: 6, of which 5 were waited for; matrix products, arithmetic and copies ran while one was open for 22% of the time, Pallas kernels for 2%

profile of v7, /device:TPU:6, one launch (start us, length us, event | category | flops | bytes accessed | tf_op | source)
XLA Modules:
  0.0 206.3 jit_solution(5613741962189301489)
XLA Ops:
  0.6 1.4 copy.41
  2.1 3.7 %shard_map.96 = (bf16[512,2560]{1,0:T(8,128)(2,1)}, bf16[64,2560]{1,0:T(8,128)(2,1)}) custom-call(bf16[64,2560]{1,0:T(8,128)(2,1)} %bitcast.126, f32[1,2560]{1,0:T(1,128)} %gain_ref.3, s32[64,6]{1,0:T(8,128)} %bitcast.125), custom_call_target="tpu_custom_call" | custom-call | tf_op jit(solution)/shard_map/pallas_call | solution.py:33
  5.8 6.3 %all-to-all-start.2 = ((bf16[16,32,2560]{2,1,0:T(8,128)(2,1)}), bf16[16,32,2560]{2,1,0:T(8,128)(2,1)S(1)}, u32[]{:S(2)}, u32[]{:S(2)}) async-start(bf16[16,32,2560]{2,1,0:T(8,128)(2,1)} %bitcast.123), calls=%async_computation.2 | async-start | bytes 5242880 | tf_op jit(solution)/shard_map/all_to_all | solution.py:84
  12.1 0.7 copy.32
  12.8 3.7 %shard_map.95 = (bf16[512,2560]{1,0:T(8,128)(2,1)}, bf16[64,2560]{1,0:T(8,128)(2,1)}) custom-call(bf16[64,2560]{1,0:T(8,128)(2,1)} %bitcast.127, f32[1,2560]{1,0:T(1,128)} %gain_ref.3, s32[64,6]{1,0:T(8,128)} %bitcast.124), custom_call_target="tpu_custom_call" | custom-call | tf_op jit(solution)/shard_map/pallas_call | solution.py:33
  16.4 33.2 %all-to-all-done.2 = bf16[16,32,2560]{2,1,0:T(8,128)(2,1)S(1)} async-done(((bf16[16,32,2560]{2,1,0:T(8,128)(2,1)}), bf16[16,32,2560]{2,1,0:T(8,128)(2,1)S(1)}, u32[]{:S(2)}, u32[]{:S(2)}) %all-to-all-start.2) | async-done | bytes 2621472 | tf_op jit(solution)/shard_map/all_to_all | solution.py:84
  49.7 4.9 %all-to-all-start = ((bf16[16,32,2560]{2,1,0:T(8,128)(2,1)}), bf16[16,32,2560]{2,1,0:T(8,128)(2,1)}, u32[]{:S(2)}, u32[]{:S(2)}) async-start(bf16[16,32,2560]{2,1,0:T(8,128)(2,1)} %bitcast.121), calls=%async_computation | async-start | bytes 5242880 | tf_op jit(solution)/shard_map/all_to_all | solution.py:84
  54.5 13.8 %fusion.11 = bf16[512,2560]{1,0:T(8,128)(2,1)} fusion(bf16[1,1,1152,2560]{3,2,1,0:T(8,128)(2,1)} %param.17, bf16[512,2560]{1,0:T(8,128)(2,1)S(1)} %bitcast.120, bf16[1,1,2560,1152]{3,2,1,0:T(8,128)(2,1)} %param.16), kind=kOutput, calls=%fused_computation.11 | convolution fusion | flops 6044057600 | bytes 17039360 | tf_op jit(solution)/shard_map/dot_general | solution.py:73
  68.4 23.9 %all-to-all-done = bf16[16,32,2560]{2,1,0:T(8,128)(2,1)} async-done(((bf16[16,32,2560]{2,1,0:T(8,128)(2,1)}), bf16[16,32,2560]{2,1,0:T(8,128)(2,1)}, u32[]{:S(2)}, u32[]{:S(2)}) %all-to-all-start) | async-done | bytes 2621472 | tf_op jit(solution)/shard_map/all_to_all | solution.py:84
  92.3 4.9 %all-to-all-start.3 = ((bf16[16,32,2560]{2,1,0:T(8,128)(2,1)}), bf16[16,32,2560]{2,1,0:T(8,128)(2,1)S(1)}, u32[]{:S(2)}, u32[]{:S(2)}) async-start(bf16[16,32,2560]{2,1,0:T(8,128)(2,1)} %bitcast.122), calls=%async_computation.3 | async-start | bytes 5242880 | tf_op jit(solution)/shard_map/all_to_all | solution.py:84
  97.1 14.6 %fusion.8 = bf16[512,2560]{1,0:T(8,128)(2,1)} fusion(bf16[1,1,1152,2560]{3,2,1,0:T(8,128)(2,1)} %param.17, bf16[512,2560]{1,0:T(8,128)(2,1)} %bitcast.6, bf16[1,1,2560,1152]{3,2,1,0:T(8,128)(2,1)} %param.16), kind=kOutput, calls=%fused_computation.10 | convolution fusion | flops 6044057600 | bytes 17039360 | tf_op jit(solution)/shard_map/dot_general | solution.py:73
  111.7 23.0 %all-to-all-done.3 = bf16[16,32,2560]{2,1,0:T(8,128)(2,1)S(1)} async-done(((bf16[16,32,2560]{2,1,0:T(8,128)(2,1)}), bf16[16,32,2560]{2,1,0:T(8,128)(2,1)S(1)}, u32[]{:S(2)}, u32[]{:S(2)}) %all-to-all-start.3) | async-done | bytes 2621472 | tf_op jit(solution)/shard_map/all_to_all | solution.py:84
  134.8 1.5 copy-done.1
  136.3 4.9 %all-to-all-start.1 = ((bf16[16,32,2560]{2,1,0:T(8,128)(2,1)}), bf16[16,32,2560]{2,1,0:T(8,128)(2,1)S(1)}, u32[]{:S(2)}, u32[]{:S(2)}) async-start(bf16[16,32,2560]{2,1,0:T(8,128)(2,1)} %bitcast.119), calls=%async_computation.1 | async-start | bytes 5242880 | tf_op jit(solution)/shard_map/all_to_all | solution.py:84
  141.1 0.1 eq.82
  141.3 0.1 eq.78
  141.4 0.1 eq.93
  141.6 0.1 eq.89
  141.7 0.9 reduce-window.14
  142.6 0.2 slice_reduce_fusion.1
  142.9 0.1 fusion.49
  142.9 0.1 reshape.87
  143.2 0.9 reduce-window.16
  144.1 0.2 slice_reduce_fusion
  144.3 0.1 fusion.46
  144.4 0.1 reshape.89
  144.7 0.1 reshape.119
  144.8 0.1 reshape.114
  145.0 0.2 fusion.30
  145.2 3.0 %gather_fusion.1 = f32[384]{0:T(512)S(1)} fusion(f32[64,16]{0,1:T(8,128)S(1)} %fusion.30, s32[384]{0:T(512)S(1)} %reshape.119), kind=kCustom, calls=%fused_computation.1.clone | custom fusion | bytes 6144 | tf_op jit(solution)/shard_map/jit(take_along_axis)/gather | solution.py:52
  148.2 0.1 reshape.122
  148.3 0.1 divide_reduce_fusion
  148.6 0.2 fusion.32
  148.8 3.0 %gather_fusion = f32[384]{0:T(512)S(1)} fusion(f32[64,16]{0,1:T(8,128)S(1)} %fusion.32, s32[384]{0:T(512)S(1)} %reshape.114), kind=kCustom, calls=%fused_computation.clone | custom fusion | bytes 6144 | tf_op jit(solution)/shard_map/jit(take_along_axis)/gather | solution.py:52
  151.8 0.1 reshape.117
  152.0 0.1 divide_reduce_fusion.1
  152.3 0.2 select_reduce_fusion
  152.4 0.2 select_reduce_fusion.1
  152.6 2.5 %fusion.39 = f32[64,2560]{1,0:T(8,128)S(1)} fusion(bf16[512,2560]{1,0:T(8,128)(2,1)} %bitcast.117, f32[64,512]{1,0:T(8,128)S(1)} %select_reduce_fusion), kind=kOutput, calls=%fused_computation.46 | convolution fusion | flops 167804928 | bytes 3407872 | tf_op jit(solution)/shard_map/dot_general | solution.py:77
  155.1 1.3 fusion.21
  156.4 7.9 %collective-permute-start.1 = (bf16[1,64,2560]{2,1,0:T(8,128)(2,1)}, bf16[1,64,2560]{2,1,0:T(8,128)(2,1)S(1)}, u32[]{:S(2)}, u32[]{:S(2)}) collective-permute-start(bf16[1,64,2560]{2,1,0:T(8,128)(2,1)} %fusion.21), channel_id=1, source_target_pairs={{16,0},{32,16},{48,32},{64,48},{80,64},{96,80},{112,96},{128,112},... | collective-permute-start | bytes 983048 | tf_op jit(solution)/shard_map/ppermute | solution.py:43
  164.3 20.8 %all-to-all-done.1 = bf16[16,32,2560]{2,1,0:T(8,128)(2,1)S(1)} async-done(((bf16[16,32,2560]{2,1,0:T(8,128)(2,1)}), bf16[16,32,2560]{2,1,0:T(8,128)(2,1)S(1)}, u32[]{:S(2)}, u32[]{:S(2)}) %all-to-all-start.1) | async-done | bytes 2621472 | tf_op jit(solution)/shard_map/all_to_all | solution.py:84
  185.1 0.6 fusion.42
  185.7 0.6 fusion.20
  186.3 3.7 %collective-permute-start = (bf16[1,64,2560]{2,1,0:T(8,128)(2,1)S(1)}, bf16[1,64,2560]{2,1,0:T(8,128)(2,1)S(1)}, u32[]{:S(2)}, u32[]{:S(2)}) collective-permute-start(bf16[1,64,2560]{2,1,0:T(8,128)(2,1)S(1)} %fusion.20), channel_id=1, source_target_pairs={{240,0},{0,16},{16,32},{32,48},{48,64},{64,80},{80,96},{96,112},{1... | collective-permute-start | bytes 983048 | tf_op jit(solution)/shard_map/ppermute | solution.py:43
  189.9 14.9 %collective-permute-done = bf16[1,64,2560]{2,1,0:T(8,128)(2,1)S(1)} collective-permute-done((bf16[1,64,2560]{2,1,0:T(8,128)(2,1)S(1)}, bf16[1,64,2560]{2,1,0:T(8,128)(2,1)S(1)}, u32[]{:S(2)}, u32[]{:S(2)}) %collective-permute-start) | collective-permute-done | bytes 327712 | tf_op jit(solution)/shard_map/ppermute | solution.py:43
  204.8 0.7 copy.56
  205.6 0.7 copy.57
  (34 shorter events, 0.7 us)
Async XLA Ops:
  0.6 144.3 %copy-start = (bf16[1,2560,16]{1,2,0:T(8,128)(2,1)S(1)}, bf16[1,2560,16]{1,2,0:T(8,128)(2,1)}, u32[]{:S(2)}) copy-start(bf16[1,2560,16]{1,2,0:T(8,128)(2,1)} %param.15) | copy-start | bytes 245764
  5.8 6.3 %copy-start.9 = (s32[1,64,6]{1,0,2:T(1,128)S(1)}, s32[1,64,6]{1,0,2:T(1,128)}, u32[]{:S(2)}) copy-start(s32[1,64,6]{1,0,2:T(1,128)} %param.12) | copy-start | bytes 4612
  5.8 43.9 %all-to-all-start.2 = ((bf16[16,32,2560]{2,1,0:T(8,128)(2,1)}), bf16[16,32,2560]{2,1,0:T(8,128)(2,1)S(1)}, u32[]{:S(2)}, u32[]{:S(2)}) async-start(bf16[16,32,2560]{2,1,0:T(8,128)(2,1)} %bitcast.123), calls=%async_computation.2 | async-start | bytes 5242880 | tf_op jit(solution)/shard_map/all_to_all | solution.py:84
  49.7 42.6 %all-to-all-start = ((bf16[16,32,2560]{2,1,0:T(8,128)(2,1)}), bf16[16,32,2560]{2,1,0:T(8,128)(2,1)}, u32[]{:S(2)}, u32[]{:S(2)}) async-start(bf16[16,32,2560]{2,1,0:T(8,128)(2,1)} %bitcast.121), calls=%async_computation | async-start | bytes 5242880 | tf_op jit(solution)/shard_map/all_to_all | solution.py:84
  92.3 42.5 %all-to-all-start.3 = ((bf16[16,32,2560]{2,1,0:T(8,128)(2,1)}), bf16[16,32,2560]{2,1,0:T(8,128)(2,1)S(1)}, u32[]{:S(2)}, u32[]{:S(2)}) async-start(bf16[16,32,2560]{2,1,0:T(8,128)(2,1)} %bitcast.122), calls=%async_computation.3 | async-start | bytes 5242880 | tf_op jit(solution)/shard_map/all_to_all | solution.py:84
  134.8 1.5 copy-start.1
  134.8 6.4 %copy-start.3 = (s32[1,64,6]{2,1,0:T(8,128)S(1)}, s32[1,64,6]{2,1,0:T(8,128)}, u32[]{:S(2)}) copy-start(s32[1,64,6]{2,1,0:T(8,128)} %copy.32) | copy-start | bytes 4612
  134.8 6.7 %copy-start.4 = (s32[1,64,6]{2,1,0:T(8,128)S(1)}, s32[1,64,6]{2,1,0:T(8,128)}, u32[]{:S(2)}) copy-start(s32[1,64,6]{2,1,0:T(8,128)} %copy.41) | copy-start | bytes 4612
  134.8 10.2 %copy-start.8 = (bf16[64,2560]{1,0:T(8,128)(2,1)S(1)}, bf16[64,2560]{1,0:T(8,128)(2,1)}, u32[]{:S(2)}) copy-start(bf16[64,2560]{1,0:T(8,128)(2,1)} %get-tuple-element.9) | copy-start | bytes 983044
  136.3 48.8 %all-to-all-start.1 = ((bf16[16,32,2560]{2,1,0:T(8,128)(2,1)}), bf16[16,32,2560]{2,1,0:T(8,128)(2,1)S(1)}, u32[]{:S(2)}, u32[]{:S(2)}) async-start(bf16[16,32,2560]{2,1,0:T(8,128)(2,1)} %bitcast.119), calls=%async_computation.1 | async-start | bytes 5242880 | tf_op jit(solution)/shard_map/all_to_all | solution.py:84
  145.2 3.4 %copy-start.7 = (bf16[64,2560]{1,0:T(8,128)(2,1)S(1)}, bf16[64,2560]{1,0:T(8,128)(2,1)}, u32[]{:S(2)}) copy-start(bf16[64,2560]{1,0:T(8,128)(2,1)} %get-tuple-element.7) | copy-start | bytes 983044
  151.8 3.3 %copy-start.5 = (bf16[1,64,2560]{2,1,0:T(8,128)(2,1)S(1)}, bf16[1,64,2560]{2,1,0:T(8,128)(2,1)}, u32[]{:S(2)}) copy-start(bf16[1,64,2560]{2,1,0:T(8,128)(2,1)} %param.11) | copy-start | bytes 983044
  152.3 2.9 %copy-start.2 = (bf16[16,32,2560]{2,1,0:T(8,128)(2,1)S(1)}, bf16[16,32,2560]{2,1,0:T(8,128)(2,1)}, u32[]{:S(2)}) copy-start(bf16[16,32,2560]{2,1,0:T(8,128)(2,1)} %copy-done.1) | copy-start | bytes 7864324
  156.4 29.2 %copy-start.6 = (bf16[1,64,2560]{2,1,0:T(8,128)(2,1)S(1)}, bf16[1,64,2560]{2,1,0:T(8,128)(2,1)}, u32[]{:S(2)}) copy-start(bf16[1,64,2560]{2,1,0:T(8,128)(2,1)} %param.10) | copy-start | bytes 983044
  156.4 33.5 %collective-permute-start.1 = (bf16[1,64,2560]{2,1,0:T(8,128)(2,1)}, bf16[1,64,2560]{2,1,0:T(8,128)(2,1)S(1)}, u32[]{:S(2)}, u32[]{:S(2)}) collective-permute-start(bf16[1,64,2560]{2,1,0:T(8,128)(2,1)} %fusion.21), channel_id=1, source_target_pairs={{16,0},{32,16},{48,32},{64,48},{80,64},{96,80},{112,96},{128,112},... | collective-permute-start | bytes 983048 | tf_op jit(solution)/shard_map/ppermute | solution.py:43
  186.3 18.6 %collective-permute-start = (bf16[1,64,2560]{2,1,0:T(8,128)(2,1)S(1)}, bf16[1,64,2560]{2,1,0:T(8,128)(2,1)S(1)}, u32[]{:S(2)}, u32[]{:S(2)}) collective-permute-start(bf16[1,64,2560]{2,1,0:T(8,128)(2,1)S(1)} %fusion.20), channel_id=1, source_target_pairs={{240,0},{0,16},{16,32},{32,48},{48,64},{64,80},{80,96},{96,112},{1... | collective-permute-start | bytes 983048 | tf_op jit(solution)/shard_map/ppermute | solution.py:43

commit v8 on v7

--- a/solution.py
+++ b/solution.py
@@ -7,14 +7,19 @@
 CAP = 32
 
 def dispatch_kernel(x_ref, gain_ref, ids_ref, send_ref, normed_ref):
-    tokens, width = x_ref.shape
-    rows = send_ref.shape[0]
-    xf = x_ref[...].astype(jnp.float32)
-    ms = jnp.mean(xf * xf, axis=-1, keepdims=True)
-    normed = (xf * lax.rsqrt(ms + 1e-06) * gain_ref[...]).astype(jnp.bfloat16)
-    normed_ref[...] = normed
+    step = pl.program_id(0)
+    tokens = x_ref.shape[0]
+    block = send_ref.shape[0]
+
+    @pl.when(step == 0)
+    def _():
+        xf = x_ref[...].astype(jnp.float32)
+        ms = jnp.mean(xf * xf, axis=-1, keepdims=True)
+        normed_ref[...] = (xf * lax.rsqrt(ms + 1e-06) * gain_ref[...]).astype(jnp.bfloat16)
+
     ids = ids_ref[...]
-    owner = lax.broadcasted_iota(jnp.int32, (tokens, rows), 1) // CAP
+    row = lax.broadcasted_iota(jnp.int32, (tokens, block), 1) + step * block
+    owner = row // CAP
     member = ids[:, 0:1] == owner
     for k in range(1, ids.shape[1]):
         member = member | (ids[:, k:k + 1] == owner)
@@ -22,16 +27,30 @@
     earlier = (lax.broadcasted_iota(jnp.int32, (tokens, tokens), 1)
                < lax.broadcasted_iota(jnp.int32, (tokens, tokens), 0)).astype(jnp.bfloat16)
     slot = jnp.dot(earlier, member.astype(jnp.bfloat16), preferred_element_type=jnp.float32)
-    offset = (lax.broadcasted_iota(jnp.int32, (tokens, rows), 1) % CAP).astype(jnp.float32)
+    offset = (row % CAP).astype(jnp.float32)
     place = jnp.where(slot == offset, member, 0.0)
     place_t = place.T.astype(jnp.bfloat16)
-    send_ref[...] = jnp.dot(place_t, normed, preferred_element_type=jnp.float32).astype(jnp.bfloat16)
+    send_ref[...] = jnp.dot(
+        place_t, normed_ref[...], preferred_element_type=jnp.float32
+    ).astype(jnp.bfloat16)
+
 
 def dispatch(x, gain, ids, experts):
     tokens, width = x.shape
     rows = experts * CAP
+    block = 128
     return pl.pallas_call(
         dispatch_kernel,
+        grid=(rows // block,),
+        in_specs=[
+            pl.BlockSpec((tokens, width), lambda i: (0, 0)),
+            pl.BlockSpec((1, width), lambda i: (0, 0)),
+            pl.BlockSpec((tokens, ids.shape[1]), lambda i: (0, 0)),
+        ],
+        out_specs=(
+            pl.BlockSpec((block, width), lambda i: (i, 0)),
+            pl.BlockSpec((tokens, width), lambda i: (0, 0)),
+        ),
         out_shape=(jax.ShapeDtypeStruct((rows, width), jnp.bfloat16),
                    jax.ShapeDtypeStruct((tokens, width), jnp.bfloat16)),
     )(x, gain.reshape(1, width), ids)

time: 208 us -> 210 us (level)
  Pallas kernels: 7.41 us -> 9.6 us
    pallas_call x2, Pallas kernels: 7.41 us -> 9.6 us  [dispatch(): pl.pallas_call(dispatch_kernel, grid=(rows // block,), in_specs=[pl.Block...]
where the time goes in v8:
time: 210 us; the launch traced here: 207 us
  waiting for transfers between devices  115 us (55%)
  matrix products  33.7 us (16%)
  starting transfers between devices  32.4 us (15%)
  local copies, waits for them, and re-layouts  13.2 us (6%)
  Pallas kernels  9.6 us (5%)
  other arithmetic  2.86 us (1%)
    all_to_all x4, waiting for transfers between devices, exchange(): lax.all_to_all(block, 'expert', split_axis=0, concat_axis=0, tiled=True)  99.9 us
    dot_general x2, matrix products, apply_experts(): jnp.dot(hidden, down_w, preferred_element_type=jnp.float32)  28.4 us
    all_to_all x4, starting transfers between devices, exchange(): lax.all_to_all(block, 'expert', split_axis=0, concat_axis=0, tiled=True)  20.9 us
    ppermute x2, waiting for transfers between devices, shifted(): return lax.ppermute(block, axis, route)  14.9 us
    ppermute x2, starting transfers between devices, shifted(): return lax.ppermute(block, axis, route)  11.5 us
    pallas_call x2, Pallas kernels, dispatch(): pl.pallas_call(dispatch_kernel, grid=(rows // block,), in_specs=[pl.Block...  9.6 us
    gather x6, local copies, waits for them, and re-layouts, layer_route(): chosen = jnp.take_along_axis(logits, ids, axis=1)  6.53 us
    unnamed x24, local copies, waits for them, and re-layouts  5.12 us
  transfers between devices with their start and end apart: 6, of which 5 were waited for; matrix products, arithmetic and copies ran while one was open for 22% of the time, Pallas kernels for 2%

profile of v8, /device:TPU:6, one launch (start us, length us, event | category | flops | bytes accessed | tf_op | source)
XLA Modules:
  0.0 207.4 jit_solution(7402098817354171685)
XLA Ops:
  0.6 1.4 copy.41
  2.1 4.8 %shard_map.96 = (bf16[512,2560]{1,0:T(8,128)(2,1)}, bf16[64,2560]{1,0:T(8,128)(2,1)}) custom-call(bf16[64,2560]{1,0:T(8,128)(2,1)} %bitcast.126, f32[1,2560]{1,0:T(1,128)} %gain_ref.3, s32[64,6]{1,0:T(8,128)} %bitcast.125), custom_call_target="tpu_custom_call" | custom-call | tf_op jit(solution)/shard_map/pallas_call | solution.py:42
  6.9 6.3 %all-to-all-start.2 = ((bf16[16,32,2560]{2,1,0:T(8,128)(2,1)}), bf16[16,32,2560]{2,1,0:T(8,128)(2,1)S(1)}, u32[]{:S(2)}, u32[]{:S(2)}) async-start(bf16[16,32,2560]{2,1,0:T(8,128)(2,1)} %bitcast.123), calls=%async_computation.2 | async-start | bytes 5242880 | tf_op jit(solution)/shard_map/all_to_all | solution.py:103
  13.1 0.7 copy.32
  13.8 4.8 %shard_map.95 = (bf16[512,2560]{1,0:T(8,128)(2,1)}, bf16[64,2560]{1,0:T(8,128)(2,1)}) custom-call(bf16[64,2560]{1,0:T(8,128)(2,1)} %bitcast.127, f32[1,2560]{1,0:T(1,128)} %gain_ref.3, s32[64,6]{1,0:T(8,128)} %bitcast.124), custom_call_target="tpu_custom_call" | custom-call | tf_op jit(solution)/shard_map/pallas_call | solution.py:42
  18.6 32.1 %all-to-all-done.2 = bf16[16,32,2560]{2,1,0:T(8,128)(2,1)S(1)} async-done(((bf16[16,32,2560]{2,1,0:T(8,128)(2,1)}), bf16[16,32,2560]{2,1,0:T(8,128)(2,1)S(1)}, u32[]{:S(2)}, u32[]{:S(2)}) %all-to-all-start.2) | async-done | bytes 2621472 | tf_op jit(solution)/shard_map/all_to_all | solution.py:103
  50.8 4.9 %all-to-all-start = ((bf16[16,32,2560]{2,1,0:T(8,128)(2,1)}), bf16[16,32,2560]{2,1,0:T(8,128)(2,1)}, u32[]{:S(2)}, u32[]{:S(2)}) async-start(bf16[16,32,2560]{2,1,0:T(8,128)(2,1)} %bitcast.121), calls=%async_computation | async-start | bytes 5242880 | tf_op jit(solution)/shard_map/all_to_all | solution.py:103
  55.6 13.8 %fusion.11 = bf16[512,2560]{1,0:T(8,128)(2,1)} fusion(bf16[1,1,1152,2560]{3,2,1,0:T(8,128)(2,1)} %param.17, bf16[512,2560]{1,0:T(8,128)(2,1)S(1)} %bitcast.120, bf16[1,1,2560,1152]{3,2,1,0:T(8,128)(2,1)} %param.16), kind=kOutput, calls=%fused_computation.11 | convolution fusion | flops 6044057600 | bytes 17039360 | tf_op jit(solution)/shard_map/dot_general | solution.py:92
  69.5 23.9 %all-to-all-done = bf16[16,32,2560]{2,1,0:T(8,128)(2,1)} async-done(((bf16[16,32,2560]{2,1,0:T(8,128)(2,1)}), bf16[16,32,2560]{2,1,0:T(8,128)(2,1)}, u32[]{:S(2)}, u32[]{:S(2)}) %all-to-all-start) | async-done | bytes 2621472 | tf_op jit(solution)/shard_map/all_to_all | solution.py:103
  93.4 4.9 %all-to-all-start.3 = ((bf16[16,32,2560]{2,1,0:T(8,128)(2,1)}), bf16[16,32,2560]{2,1,0:T(8,128)(2,1)S(1)}, u32[]{:S(2)}, u32[]{:S(2)}) async-start(bf16[16,32,2560]{2,1,0:T(8,128)(2,1)} %bitcast.122), calls=%async_computation.3 | async-start | bytes 5242880 | tf_op jit(solution)/shard_map/all_to_all | solution.py:103
  98.2 14.6 %fusion.8 = bf16[512,2560]{1,0:T(8,128)(2,1)} fusion(bf16[1,1,1152,2560]{3,2,1,0:T(8,128)(2,1)} %param.17, bf16[512,2560]{1,0:T(8,128)(2,1)} %bitcast.6, bf16[1,1,2560,1152]{3,2,1,0:T(8,128)(2,1)} %param.16), kind=kOutput, calls=%fused_computation.10 | convolution fusion | flops 6044057600 | bytes 17039360 | tf_op jit(solution)/shard_map/dot_general | solution.py:92
  112.8 23.1 %all-to-all-done.3 = bf16[16,32,2560]{2,1,0:T(8,128)(2,1)S(1)} async-done(((bf16[16,32,2560]{2,1,0:T(8,128)(2,1)}), bf16[16,32,2560]{2,1,0:T(8,128)(2,1)S(1)}, u32[]{:S(2)}, u32[]{:S(2)}) %all-to-all-start.3) | async-done | bytes 2621472 | tf_op jit(solution)/shard_map/all_to_all | solution.py:103
  135.9 1.5 copy-done.1
  137.4 4.9 %all-to-all-start.1 = ((bf16[16,32,2560]{2,1,0:T(8,128)(2,1)}), bf16[16,32,2560]{2,1,0:T(8,128)(2,1)S(1)}, u32[]{:S(2)}, u32[]{:S(2)}) async-start(bf16[16,32,2560]{2,1,0:T(8,128)(2,1)} %bitcast.119), calls=%async_computation.1 | async-start | bytes 5242880 | tf_op jit(solution)/shard_map/all_to_all | solution.py:103
  142.2 0.1 eq.82
  142.4 0.1 eq.78
  142.5 0.1 eq.93
  142.7 0.1 eq.89
  142.8 0.9 reduce-window.14
  143.7 0.2 slice_reduce_fusion.1
  143.9 0.1 fusion.49
  144.0 0.1 reshape.87
  144.3 0.9 reduce-window.16
  145.1 0.2 slice_reduce_fusion
  145.4 0.1 fusion.46
  145.5 0.1 reshape.89
  145.8 0.1 reshape.119
  145.9 0.1 reshape.114
  146.1 0.2 fusion.30
  146.3 3.0 %gather_fusion.1 = f32[384]{0:T(512)S(1)} fusion(f32[64,16]{0,1:T(8,128)S(1)} %fusion.30, s32[384]{0:T(512)S(1)} %reshape.119), kind=kCustom, calls=%fused_computation.1.clone | custom fusion | bytes 6144 | tf_op jit(solution)/shard_map/jit(take_along_axis)/gather | solution.py:71
  149.3 0.1 reshape.122
  149.4 0.1 divide_reduce_fusion
  149.7 0.2 fusion.32
  149.9 3.0 %gather_fusion = f32[384]{0:T(512)S(1)} fusion(f32[64,16]{0,1:T(8,128)S(1)} %fusion.32, s32[384]{0:T(512)S(1)} %reshape.114), kind=kCustom, calls=%fused_computation.clone | custom fusion | bytes 6144 | tf_op jit(solution)/shard_map/jit(take_along_axis)/gather | solution.py:71
  152.9 0.1 reshape.117
  153.0 0.1 divide_reduce_fusion.1
  153.3 0.2 select_reduce_fusion
  153.5 0.2 select_reduce_fusion.1
  153.7 2.5 %fusion.39 = f32[64,2560]{1,0:T(8,128)S(1)} fusion(bf16[512,2560]{1,0:T(8,128)(2,1)} %bitcast.117, f32[64,512]{1,0:T(8,128)S(1)} %select_reduce_fusion), kind=kOutput, calls=%fused_computation.46 | convolution fusion | flops 167804928 | bytes 3407872 | tf_op jit(solution)/shard_map/dot_general | solution.py:96
  156.2 1.3 fusion.21
  157.5 7.8 %collective-permute-start.1 = (bf16[1,64,2560]{2,1,0:T(8,128)(2,1)}, bf16[1,64,2560]{2,1,0:T(8,128)(2,1)S(1)}, u32[]{:S(2)}, u32[]{:S(2)}) collective-permute-start(bf16[1,64,2560]{2,1,0:T(8,128)(2,1)} %fusion.21), channel_id=1, source_target_pairs={{16,0},{32,16},{48,32},{64,48},{80,64},{96,80},{112,96},{128,112},... | collective-permute-start | bytes 983048 | tf_op jit(solution)/shard_map/ppermute | solution.py:62
  165.4 20.8 %all-to-all-done.1 = bf16[16,32,2560]{2,1,0:T(8,128)(2,1)S(1)} async-done(((bf16[16,32,2560]{2,1,0:T(8,128)(2,1)}), bf16[16,32,2560]{2,1,0:T(8,128)(2,1)S(1)}, u32[]{:S(2)}, u32[]{:S(2)}) %all-to-all-start.1) | async-done | bytes 2621472 | tf_op jit(solution)/shard_map/all_to_all | solution.py:103
  186.2 0.6 fusion.42
  186.8 0.6 fusion.20
  187.3 3.7 %collective-permute-start = (bf16[1,64,2560]{2,1,0:T(8,128)(2,1)S(1)}, bf16[1,64,2560]{2,1,0:T(8,128)(2,1)S(1)}, u32[]{:S(2)}, u32[]{:S(2)}) collective-permute-start(bf16[1,64,2560]{2,1,0:T(8,128)(2,1)S(1)} %fusion.20), channel_id=1, source_target_pairs={{240,0},{0,16},{16,32},{32,48},{48,64},{64,80},{80,96},{96,112},{1... | collective-permute-start | bytes 983048 | tf_op jit(solution)/shard_map/ppermute | solution.py:62
  191.0 14.9 %collective-permute-done = bf16[1,64,2560]{2,1,0:T(8,128)(2,1)S(1)} collective-permute-done((bf16[1,64,2560]{2,1,0:T(8,128)(2,1)S(1)}, bf16[1,64,2560]{2,1,0:T(8,128)(2,1)S(1)}, u32[]{:S(2)}, u32[]{:S(2)}) %collective-permute-start) | collective-permute-done | bytes 327712 | tf_op jit(solution)/shard_map/ppermute | solution.py:62
  205.9 0.7 copy.56
  206.7 0.7 copy.57
  (34 shorter events, 0.7 us)
Async XLA Ops:
  0.6 145.4 %copy-start = (bf16[1,2560,16]{1,2,0:T(8,128)(2,1)S(1)}, bf16[1,2560,16]{1,2,0:T(8,128)(2,1)}, u32[]{:S(2)}) copy-start(bf16[1,2560,16]{1,2,0:T(8,128)(2,1)} %param.15) | copy-start | bytes 245764
  6.9 6.3 %copy-start.9 = (s32[1,64,6]{1,0,2:T(1,128)S(1)}, s32[1,64,6]{1,0,2:T(1,128)}, u32[]{:S(2)}) copy-start(s32[1,64,6]{1,0,2:T(1,128)} %param.12) | copy-start | bytes 4612
  6.9 43.9 %all-to-all-start.2 = ((bf16[16,32,2560]{2,1,0:T(8,128)(2,1)}), bf16[16,32,2560]{2,1,0:T(8,128)(2,1)S(1)}, u32[]{:S(2)}, u32[]{:S(2)}) async-start(bf16[16,32,2560]{2,1,0:T(8,128)(2,1)} %bitcast.123), calls=%async_computation.2 | async-start | bytes 5242880 | tf_op jit(solution)/shard_map/all_to_all | solution.py:103
  50.8 42.6 %all-to-all-start = ((bf16[16,32,2560]{2,1,0:T(8,128)(2,1)}), bf16[16,32,2560]{2,1,0:T(8,128)(2,1)}, u32[]{:S(2)}, u32[]{:S(2)}) async-start(bf16[16,32,2560]{2,1,0:T(8,128)(2,1)} %bitcast.121), calls=%async_computation | async-start | bytes 5242880 | tf_op jit(solution)/shard_map/all_to_all | solution.py:103
  93.4 42.5 %all-to-all-start.3 = ((bf16[16,32,2560]{2,1,0:T(8,128)(2,1)}), bf16[16,32,2560]{2,1,0:T(8,128)(2,1)S(1)}, u32[]{:S(2)}, u32[]{:S(2)}) async-start(bf16[16,32,2560]{2,1,0:T(8,128)(2,1)} %bitcast.122), calls=%async_computation.3 | async-start | bytes 5242880 | tf_op jit(solution)/shard_map/all_to_all | solution.py:103
  135.8 1.5 copy-start.1
  135.8 6.4 %copy-start.3 = (s32[1,64,6]{2,1,0:T(8,128)S(1)}, s32[1,64,6]{2,1,0:T(8,128)}, u32[]{:S(2)}) copy-start(s32[1,64,6]{2,1,0:T(8,128)} %copy.32) | copy-start | bytes 4612
  135.8 6.7 %copy-start.4 = (s32[1,64,6]{2,1,0:T(8,128)S(1)}, s32[1,64,6]{2,1,0:T(8,128)}, u32[]{:S(2)}) copy-start(s32[1,64,6]{2,1,0:T(8,128)} %copy.41) | copy-start | bytes 4612
  135.8 10.2 %copy-start.8 = (bf16[64,2560]{1,0:T(8,128)(2,1)S(1)}, bf16[64,2560]{1,0:T(8,128)(2,1)}, u32[]{:S(2)}) copy-start(bf16[64,2560]{1,0:T(8,128)(2,1)} %get-tuple-element.9) | copy-start | bytes 983044
  137.4 48.8 %all-to-all-start.1 = ((bf16[16,32,2560]{2,1,0:T(8,128)(2,1)}), bf16[16,32,2560]{2,1,0:T(8,128)(2,1)S(1)}, u32[]{:S(2)}, u32[]{:S(2)}) async-start(bf16[16,32,2560]{2,1,0:T(8,128)(2,1)} %bitcast.119), calls=%async_computation.1 | async-start | bytes 5242880 | tf_op jit(solution)/shard_map/all_to_all | solution.py:103
  146.3 3.4 %copy-start.7 = (bf16[64,2560]{1,0:T(8,128)(2,1)S(1)}, bf16[64,2560]{1,0:T(8,128)(2,1)}, u32[]{:S(2)}) copy-start(bf16[64,2560]{1,0:T(8,128)(2,1)} %get-tuple-element.7) | copy-start | bytes 983044
  152.9 3.3 %copy-start.5 = (bf16[1,64,2560]{2,1,0:T(8,128)(2,1)S(1)}, bf16[1,64,2560]{2,1,0:T(8,128)(2,1)}, u32[]{:S(2)}) copy-start(bf16[1,64,2560]{2,1,0:T(8,128)(2,1)} %param.11) | copy-start | bytes 983044
  153.3 2.9 %copy-start.2 = (bf16[16,32,2560]{2,1,0:T(8,128)(2,1)S(1)}, bf16[16,32,2560]{2,1,0:T(8,128)(2,1)}, u32[]{:S(2)}) copy-start(bf16[16,32,2560]{2,1,0:T(8,128)(2,1)} %copy-done.1) | copy-start | bytes 7864324
  157.5 29.2 %copy-start.6 = (bf16[1,64,2560]{2,1,0:T(8,128)(2,1)S(1)}, bf16[1,64,2560]{2,1,0:T(8,128)(2,1)}, u32[]{:S(2)}) copy-start(bf16[1,64,2560]{2,1,0:T(8,128)(2,1)} %param.10) | copy-start | bytes 983044
  157.5 33.5 %collective-permute-start.1 = (bf16[1,64,2560]{2,1,0:T(8,128)(2,1)}, bf16[1,64,2560]{2,1,0:T(8,128)(2,1)S(1)}, u32[]{:S(2)}, u32[]{:S(2)}) collective-permute-start(bf16[1,64,2560]{2,1,0:T(8,128)(2,1)} %fusion.21), channel_id=1, source_target_pairs={{16,0},{32,16},{48,32},{64,48},{80,64},{96,80},{112,96},{128,112},... | collective-permute-start | bytes 983048 | tf_op jit(solution)/shard_map/ppermute | solution.py:62
  187.3 18.6 %collective-permute-start = (bf16[1,64,2560]{2,1,0:T(8,128)(2,1)S(1)}, bf16[1,64,2560]{2,1,0:T(8,128)(2,1)S(1)}, u32[]{:S(2)}, u32[]{:S(2)}) collective-permute-start(bf16[1,64,2560]{2,1,0:T(8,128)(2,1)S(1)} %fusion.20), channel_id=1, source_target_pairs={{240,0},{0,16},{16,32},{32,48},{48,64},{64,80},{80,96},{96,112},{1... | collective-permute-start | bytes 983048 | tf_op jit(solution)/shard_map/ppermute | solution.py:62

commit v9 on v7

--- a/solution.py
+++ b/solution.py
@@ -7,25 +7,26 @@
 CAP = 32
 
 def dispatch_kernel(x_ref, gain_ref, ids_ref, send_ref, normed_ref):
-    tokens, width = x_ref.shape
+    tokens = x_ref.shape[0]
     rows = send_ref.shape[0]
     xf = x_ref[...].astype(jnp.float32)
     ms = jnp.mean(xf * xf, axis=-1, keepdims=True)
     normed = (xf * lax.rsqrt(ms + 1e-06) * gain_ref[...]).astype(jnp.bfloat16)
     normed_ref[...] = normed
     ids = ids_ref[...]
-    owner = lax.broadcasted_iota(jnp.int32, (tokens, rows), 1) // CAP
-    member = ids[:, 0:1] == owner
-    for k in range(1, ids.shape[1]):
-        member = member | (ids[:, k:k + 1] == owner)
-    member = member.astype(jnp.float32)
-    earlier = (lax.broadcasted_iota(jnp.int32, (tokens, tokens), 1)
-               < lax.broadcasted_iota(jnp.int32, (tokens, tokens), 0)).astype(jnp.bfloat16)
-    slot = jnp.dot(earlier, member.astype(jnp.bfloat16), preferred_element_type=jnp.float32)
-    offset = (lax.broadcasted_iota(jnp.int32, (tokens, rows), 1) % CAP).astype(jnp.float32)
-    place = jnp.where(slot == offset, member, 0.0)
-    place_t = place.T.astype(jnp.bfloat16)
-    send_ref[...] = jnp.dot(place_t, normed, preferred_element_type=jnp.float32).astype(jnp.bfloat16)
+    row = lax.broadcasted_iota(jnp.int32, (rows, tokens), 0)
+    owner = row // CAP
+    member = ids[0:1, :] == owner
+    for k in range(1, ids.shape[0]):
+        member = member | (ids[k:k + 1, :] == owner)
+    member = member.astype(jnp.bfloat16)
+    later = (lax.broadcasted_iota(jnp.int32, (tokens, tokens), 0)
+             < lax.broadcasted_iota(jnp.int32, (tokens, tokens), 1)).astype(jnp.bfloat16)
+    slot = jnp.dot(member, later, preferred_element_type=jnp.float32)
+    offset = (row % CAP).astype(jnp.float32)
+    place = jnp.where(slot == offset, member, jnp.zeros_like(member))
+    send_ref[...] = jnp.dot(place, normed, preferred_element_type=jnp.float32).astype(jnp.bfloat16)
+
 
 def dispatch(x, gain, ids, experts):
     tokens, width = x.shape
@@ -34,7 +35,7 @@
         dispatch_kernel,
         out_shape=(jax.ShapeDtypeStruct((rows, width), jnp.bfloat16),
                    jax.ShapeDtypeStruct((tokens, width), jnp.bfloat16)),
-    )(x, gain.reshape(1, width), ids)
+    )(x, gain.reshape(1, width), ids.T)
 
 
 def shifted(block, axis, distance):

time: 208 us -> 208 us (level)
    gather x6 -> x10, local copies, waits for them, and re-layouts: 6.53 us -> 6.87 us  [layer_route(): chosen = jnp.take_along_axis(logits, ids, axis=1)]
where the time goes in v9:
time: 208 us; the launch traced here: 206 us
  waiting for transfers between devices  116 us (56%)
  matrix products  33.8 us (16%)
  starting transfers between devices  32.4 us (16%)
  local copies, waits for them, and re-layouts  13.4 us (6%)
  Pallas kernels  7.12 us (3%)
  other arithmetic  2.5 us (1%)
    all_to_all x4, waiting for transfers between devices, exchange(): lax.all_to_all(block, 'expert', split_axis=0, concat_axis=0, tiled=True)  101 us
    dot_general x2, matrix products, apply_experts(): jnp.dot(hidden, down_w, preferred_element_type=jnp.float32)  28.4 us
    all_to_all x4, starting transfers between devices, exchange(): lax.all_to_all(block, 'expert', split_axis=0, concat_axis=0, tiled=True)  20.9 us
    ppermute x2, waiting for transfers between devices, shifted(): return lax.ppermute(block, axis, route)  14.9 us
    ppermute x2, starting transfers between devices, shifted(): return lax.ppermute(block, axis, route)  11.5 us
    pallas_call x2, Pallas kernels, dispatch(): pl.pallas_call(dispatch_kernel, out_shape=(jax.ShapeDtypeStruct((rows, wi...  7.12 us
    gather x10, local copies, waits for them, and re-layouts, layer_route(): chosen = jnp.take_along_axis(logits, ids, axis=1)  6.87 us
    unnamed x24, local copies, waits for them, and re-layouts  5.1 us
  transfers between devices with their start and end apart: 6, of which 5 were waited for; matrix products, arithmetic and copies ran while one was open for 22% of the time, Pallas kernels for 2%

profile of v9, /device:TPU:6, one launch (start us, length us, event | category | flops | bytes accessed | tf_op | source)
XLA Modules:
  0.0 206.1 jit_solution(3825673063030617129)
XLA Ops:
  0.6 1.3 copy.80
  2.0 3.6 %shard_map.96 = (bf16[512,2560]{1,0:T(8,128)(2,1)}, bf16[64,2560]{1,0:T(8,128)(2,1)}) custom-call(bf16[64,2560]{1,0:T(8,128)(2,1)} %bitcast.148, f32[1,2560]{1,0:T(1,128)} %gain_ref.3, s32[6,64]{1,0:T(8,128)} %bitcast.150), custom_call_target="tpu_custom_call" | custom-call | tf_op jit(solution)/shard_map/pallas_call | solution.py:34
  5.5 6.3 %all-to-all-start.2 = ((bf16[16,32,2560]{2,1,0:T(8,128)(2,1)}), bf16[16,32,2560]{2,1,0:T(8,128)(2,1)S(1)}, u32[]{:S(2)}, u32[]{:S(2)}) async-start(bf16[16,32,2560]{2,1,0:T(8,128)(2,1)} %bitcast.146), calls=%async_computation.2 | async-start | bytes 5242880 | tf_op jit(solution)/shard_map/all_to_all | solution.py:85
  11.8 0.6 copy.81
  12.4 3.5 %shard_map.95 = (bf16[512,2560]{1,0:T(8,128)(2,1)}, bf16[64,2560]{1,0:T(8,128)(2,1)}) custom-call(bf16[64,2560]{1,0:T(8,128)(2,1)} %bitcast.149, f32[1,2560]{1,0:T(1,128)} %gain_ref.3, s32[6,64]{1,0:T(8,128)} %bitcast.151), custom_call_target="tpu_custom_call" | custom-call | tf_op jit(solution)/shard_map/pallas_call | solution.py:34
  15.9 33.5 %all-to-all-done.2 = bf16[16,32,2560]{2,1,0:T(8,128)(2,1)S(1)} async-done(((bf16[16,32,2560]{2,1,0:T(8,128)(2,1)}), bf16[16,32,2560]{2,1,0:T(8,128)(2,1)S(1)}, u32[]{:S(2)}, u32[]{:S(2)}) %all-to-all-start.2) | async-done | bytes 2621472 | tf_op jit(solution)/shard_map/all_to_all | solution.py:85
  49.4 4.9 %all-to-all-start = ((bf16[16,32,2560]{2,1,0:T(8,128)(2,1)}), bf16[16,32,2560]{2,1,0:T(8,128)(2,1)}, u32[]{:S(2)}, u32[]{:S(2)}) async-start(bf16[16,32,2560]{2,1,0:T(8,128)(2,1)} %bitcast.145), calls=%async_computation | async-start | bytes 5242880 | tf_op jit(solution)/shard_map/all_to_all | solution.py:85
  54.3 13.8 %fusion.11 = bf16[512,2560]{1,0:T(8,128)(2,1)} fusion(bf16[1,1,1152,2560]{3,2,1,0:T(8,128)(2,1)} %param.17, bf16[512,2560]{1,0:T(8,128)(2,1)S(1)} %bitcast.144, bf16[1,1,2560,1152]{3,2,1,0:T(8,128)(2,1)} %param.16), kind=kOutput, calls=%fused_computation.11 | convolution fusion | flops 6044057600 | bytes 17039360 | tf_op jit(solution)/shard_map/dot_general | solution.py:74
  68.1 23.9 %all-to-all-done = bf16[16,32,2560]{2,1,0:T(8,128)(2,1)} async-done(((bf16[16,32,2560]{2,1,0:T(8,128)(2,1)}), bf16[16,32,2560]{2,1,0:T(8,128)(2,1)}, u32[]{:S(2)}, u32[]{:S(2)}) %all-to-all-start) | async-done | bytes 2621472 | tf_op jit(solution)/shard_map/all_to_all | solution.py:85
  92.0 4.9 %all-to-all-start.3 = ((bf16[16,32,2560]{2,1,0:T(8,128)(2,1)}), bf16[16,32,2560]{2,1,0:T(8,128)(2,1)S(1)}, u32[]{:S(2)}, u32[]{:S(2)}) async-start(bf16[16,32,2560]{2,1,0:T(8,128)(2,1)} %bitcast.147), calls=%async_computation.3 | async-start | bytes 5242880 | tf_op jit(solution)/shard_map/all_to_all | solution.py:85
  96.9 14.6 %fusion.8 = bf16[512,2560]{1,0:T(8,128)(2,1)} fusion(bf16[1,1,1152,2560]{3,2,1,0:T(8,128)(2,1)} %param.17, bf16[512,2560]{1,0:T(8,128)(2,1)} %bitcast.6, bf16[1,1,2560,1152]{3,2,1,0:T(8,128)(2,1)} %param.16), kind=kOutput, calls=%fused_computation.10 | convolution fusion | flops 6044057600 | bytes 17039360 | tf_op jit(solution)/shard_map/dot_general | solution.py:74
  111.5 23.0 %all-to-all-done.3 = bf16[16,32,2560]{2,1,0:T(8,128)(2,1)S(1)} async-done(((bf16[16,32,2560]{2,1,0:T(8,128)(2,1)}), bf16[16,32,2560]{2,1,0:T(8,128)(2,1)S(1)}, u32[]{:S(2)}, u32[]{:S(2)}) %all-to-all-start.3) | async-done | bytes 2621472 | tf_op jit(solution)/shard_map/all_to_all | solution.py:85
  134.5 1.5 copy-done.1
  136.0 4.9 %all-to-all-start.1 = ((bf16[16,32,2560]{2,1,0:T(8,128)(2,1)}), bf16[16,32,2560]{2,1,0:T(8,128)(2,1)S(1)}, u32[]{:S(2)}, u32[]{:S(2)}) async-start(bf16[16,32,2560]{2,1,0:T(8,128)(2,1)} %bitcast.143), calls=%async_computation.1 | async-start | bytes 5242880 | tf_op jit(solution)/shard_map/all_to_all | solution.py:85
  140.9 0.1 copy.30
  141.0 0.1 eq.82
  141.1 0.1 eq.78
  141.3 0.1 copy.36
  141.4 0.1 eq.93
  141.5 0.1 eq.89
  141.7 0.1 copy.40
  141.8 0.1 reshape.119
  141.9 0.1 copy.34
  142.0 0.1 reshape.114
  142.2 0.9 reduce-window.14
  143.1 0.2 slice_reduce_fusion.1
  143.4 0.1 reshape.87
  143.6 0.9 reduce-window.16
  144.5 0.2 slice_reduce_fusion
  144.9 0.1 reshape.89
  145.1 0.2 fusion.30
  145.3 3.0 %gather_fusion.1 = f32[384]{0:T(512)S(1)} fusion(f32[64,16]{0,1:T(8,128)S(1)} %fusion.30, s32[384]{0:T(512)S(1)} %reshape.119), kind=kCustom, calls=%fused_computation.1.clone | custom fusion | bytes 6144 | tf_op jit(solution)/shard_map/jit(take_along_axis)/gather | solution.py:53
  148.3 0.1 reshape.122
  148.5 0.2 fusion.32
  148.7 3.0 %gather_fusion = f32[384]{0:T(512)S(1)} fusion(f32[64,16]{0,1:T(8,128)S(1)} %fusion.32, s32[384]{0:T(512)S(1)} %reshape.114), kind=kCustom, calls=%fused_computation.clone | custom fusion | bytes 6144 | tf_op jit(solution)/shard_map/jit(take_along_axis)/gather | solution.py:53
  151.7 0.1 reshape.117
  152.0 0.2 select_reduce_fusion
  152.2 0.2 select_reduce_fusion.1
  152.4 2.5 %fusion.35 = f32[64,2560]{1,0:T(8,128)S(1)} fusion(bf16[512,2560]{1,0:T(8,128)(2,1)} %bitcast.141, f32[64,512]{1,0:T(8,128)S(1)} %select_reduce_fusion), kind=kOutput, calls=%fused_computation.35 | convolution fusion | flops 167804928 | bytes 3407872 | tf_op jit(solution)/shard_map/dot_general | solution.py:78
  155.0 1.3 fusion.21
  156.3 7.9 %collective-permute-start.1 = (bf16[1,64,2560]{2,1,0:T(8,128)(2,1)}, bf16[1,64,2560]{2,1,0:T(8,128)(2,1)S(1)}, u32[]{:S(2)}, u32[]{:S(2)}) collective-permute-start(bf16[1,64,2560]{2,1,0:T(8,128)(2,1)} %fusion.21), channel_id=1, source_target_pairs={{16,0},{32,16},{48,32},{64,48},{80,64},{96,80},{112,96},{128,112},... | collective-permute-start | bytes 983048 | tf_op jit(solution)/shard_map/ppermute | solution.py:44
  164.1 20.7 %all-to-all-done.1 = bf16[16,32,2560]{2,1,0:T(8,128)(2,1)S(1)} async-done(((bf16[16,32,2560]{2,1,0:T(8,128)(2,1)}), bf16[16,32,2560]{2,1,0:T(8,128)(2,1)S(1)}, u32[]{:S(2)}, u32[]{:S(2)}) %all-to-all-start.1) | async-done | bytes 2621472 | tf_op jit(solution)/shard_map/all_to_all | solution.py:85
  184.9 0.6 fusion.38
  185.5 0.6 fusion.20
  186.1 3.7 %collective-permute-start = (bf16[1,64,2560]{2,1,0:T(8,128)(2,1)S(1)}, bf16[1,64,2560]{2,1,0:T(8,128)(2,1)S(1)}, u32[]{:S(2)}, u32[]{:S(2)}) collective-permute-start(bf16[1,64,2560]{2,1,0:T(8,128)(2,1)S(1)} %fusion.20), channel_id=1, source_target_pairs={{240,0},{0,16},{16,32},{32,48},{48,64},{64,80},{80,96},{96,112},{1... | collective-permute-start | bytes 983048 | tf_op jit(solution)/shard_map/ppermute | solution.py:44
  189.7 14.9 %collective-permute-done = bf16[1,64,2560]{2,1,0:T(8,128)(2,1)S(1)} collective-permute-done((bf16[1,64,2560]{2,1,0:T(8,128)(2,1)S(1)}, bf16[1,64,2560]{2,1,0:T(8,128)(2,1)S(1)}, u32[]{:S(2)}, u32[]{:S(2)}) %collective-permute-start) | collective-permute-done | bytes 327712 | tf_op jit(solution)/shard_map/ppermute | solution.py:44
  204.6 0.7 copy.84
  205.3 0.7 copy.85
  (36 shorter events, 0.7 us)
Async XLA Ops:
  0.6 144.4 %copy-start = (bf16[1,2560,16]{1,2,0:T(8,128)(2,1)S(1)}, bf16[1,2560,16]{1,2,0:T(8,128)(2,1)}, u32[]{:S(2)}) copy-start(bf16[1,2560,16]{1,2,0:T(8,128)(2,1)} %param.15) | copy-start | bytes 245764
  5.5 6.3 %copy-start.8 = (s32[1,64,6]{1,0,2:T(1,128)S(1)}, s32[1,64,6]{1,0,2:T(1,128)}, u32[]{:S(2)}) copy-start(s32[1,64,6]{1,0,2:T(1,128)} %param.12) | copy-start | bytes 4612
  5.5 43.9 %all-to-all-start.2 = ((bf16[16,32,2560]{2,1,0:T(8,128)(2,1)}), bf16[16,32,2560]{2,1,0:T(8,128)(2,1)S(1)}, u32[]{:S(2)}, u32[]{:S(2)}) async-start(bf16[16,32,2560]{2,1,0:T(8,128)(2,1)} %bitcast.146), calls=%async_computation.2 | async-start | bytes 5242880 | tf_op jit(solution)/shard_map/all_to_all | solution.py:85
  49.4 42.6 %all-to-all-start = ((bf16[16,32,2560]{2,1,0:T(8,128)(2,1)}), bf16[16,32,2560]{2,1,0:T(8,128)(2,1)}, u32[]{:S(2)}, u32[]{:S(2)}) async-start(bf16[16,32,2560]{2,1,0:T(8,128)(2,1)} %bitcast.145), calls=%async_computation | async-start | bytes 5242880 | tf_op jit(solution)/shard_map/all_to_all | solution.py:85
  92.0 42.5 %all-to-all-start.3 = ((bf16[16,32,2560]{2,1,0:T(8,128)(2,1)}), bf16[16,32,2560]{2,1,0:T(8,128)(2,1)S(1)}, u32[]{:S(2)}, u32[]{:S(2)}) async-start(bf16[16,32,2560]{2,1,0:T(8,128)(2,1)} %bitcast.147), calls=%async_computation.3 | async-start | bytes 5242880 | tf_op jit(solution)/shard_map/all_to_all | solution.py:85
  134.5 1.5 copy-start.1
  134.5 6.8 %copy-start.7 = (s32[1,64,6]{1,0,2:T(1,128)S(1)}, s32[1,64,6]{1,0,2:T(1,128)}, u32[]{:S(2)}) copy-start(s32[1,64,6]{1,0,2:T(1,128)} %param.13) | copy-start | bytes 4612
  134.5 10.6 %copy-start.5 = (bf16[64,2560]{1,0:T(8,128)(2,1)S(1)}, bf16[64,2560]{1,0:T(8,128)(2,1)}, u32[]{:S(2)}) copy-start(bf16[64,2560]{1,0:T(8,128)(2,1)} %get-tuple-element.9) | copy-start | bytes 983044
  136.0 48.8 %all-to-all-start.1 = ((bf16[16,32,2560]{2,1,0:T(8,128)(2,1)}), bf16[16,32,2560]{2,1,0:T(8,128)(2,1)S(1)}, u32[]{:S(2)}, u32[]{:S(2)}) async-start(bf16[16,32,2560]{2,1,0:T(8,128)(2,1)} %bitcast.143), calls=%async_computation.1 | async-start | bytes 5242880 | tf_op jit(solution)/shard_map/all_to_all | solution.py:85
  145.3 3.2 %copy-start.6 = (bf16[64,2560]{1,0:T(8,128)(2,1)S(1)}, bf16[64,2560]{1,0:T(8,128)(2,1)}, u32[]{:S(2)}) copy-start(bf16[64,2560]{1,0:T(8,128)(2,1)} %get-tuple-element.7) | copy-start | bytes 983044
  151.7 3.3 %copy-start.3 = (bf16[1,64,2560]{2,1,0:T(8,128)(2,1)S(1)}, bf16[1,64,2560]{2,1,0:T(8,128)(2,1)}, u32[]{:S(2)}) copy-start(bf16[1,64,2560]{2,1,0:T(8,128)(2,1)} %param.11) | copy-start | bytes 983044
  151.9 3.1 %copy-start.2 = (bf16[16,32,2560]{2,1,0:T(8,128)(2,1)S(1)}, bf16[16,32,2560]{2,1,0:T(8,128)(2,1)}, u32[]{:S(2)}) copy-start(bf16[16,32,2560]{2,1,0:T(8,128)(2,1)} %copy-done.1) | copy-start | bytes 7864324
  156.3 29.2 %copy-start.4 = (bf16[1,64,2560]{2,1,0:T(8,128)(2,1)S(1)}, bf16[1,64,2560]{2,1,0:T(8,128)(2,1)}, u32[]{:S(2)}) copy-start(bf16[1,64,2560]{2,1,0:T(8,128)(2,1)} %param.10) | copy-start | bytes 983044
  156.3 33.4 %collective-permute-start.1 = (bf16[1,64,2560]{2,1,0:T(8,128)(2,1)}, bf16[1,64,2560]{2,1,0:T(8,128)(2,1)S(1)}, u32[]{:S(2)}, u32[]{:S(2)}) collective-permute-start(bf16[1,64,2560]{2,1,0:T(8,128)(2,1)} %fusion.21), channel_id=1, source_target_pairs={{16,0},{32,16},{48,32},{64,48},{80,64},{96,80},{112,96},{128,112},... | collective-permute-start | bytes 983048 | tf_op jit(solution)/shard_map/ppermute | solution.py:44
  186.1 18.6 %collective-permute-start = (bf16[1,64,2560]{2,1,0:T(8,128)(2,1)S(1)}, bf16[1,64,2560]{2,1,0:T(8,128)(2,1)S(1)}, u32[]{:S(2)}, u32[]{:S(2)}) collective-permute-start(bf16[1,64,2560]{2,1,0:T(8,128)(2,1)S(1)} %fusion.20), channel_id=1, source_target_pairs={{240,0},{0,16},{16,32},{32,48},{48,64},{64,80},{80,96},{96,112},{1... | collective-permute-start | bytes 983048 | tf_op jit(solution)/shard_map/ppermute | solution.py:44

commit v10 on v9

--- a/solution.py
+++ b/solution.py
@@ -13,12 +13,11 @@
     ms = jnp.mean(xf * xf, axis=-1, keepdims=True)
     normed = (xf * lax.rsqrt(ms + 1e-06) * gain_ref[...]).astype(jnp.bfloat16)
     normed_ref[...] = normed
-    ids = ids_ref[...]
     row = lax.broadcasted_iota(jnp.int32, (rows, tokens), 0)
     owner = row // CAP
-    member = ids[0:1, :] == owner
-    for k in range(1, ids.shape[0]):
-        member = member | (ids[k:k + 1, :] == owner)
+    member = ids_ref[0] == owner
+    for k in range(1, ids_ref.shape[0]):
+        member = member | (ids_ref[k] == owner)
     member = member.astype(jnp.bfloat16)
     later = (lax.broadcasted_iota(jnp.int32, (tokens, tokens), 0)
              < lax.broadcasted_iota(jnp.int32, (tokens, tokens), 1)).astype(jnp.bfloat16)
@@ -35,7 +34,7 @@
         dispatch_kernel,
         out_shape=(jax.ShapeDtypeStruct((rows, width), jnp.bfloat16),
                    jax.ShapeDtypeStruct((tokens, width), jnp.bfloat16)),
-    )(x, gain.reshape(1, width), ids.T)
+    )(x, gain.reshape(1, width), jnp.transpose(ids, (2, 0, 1)))
 
 
 def shifted(block, axis, distance):
@@ -44,11 +43,12 @@
     return lax.ppermute(block, axis, route)
 
 
-def layer_route(x, ids, gain, table):
+def layer_route(x, ids_block, gain, table):
+    ids = ids_block[0]
     tokens_here = x.shape[0]
     experts = table.shape[1]
     choose = ids.shape[1]
-    send, normed = dispatch(x, gain, ids, experts)
+    send, normed = dispatch(x, gain, ids_block, experts)
     logits = jnp.dot(normed, table, preferred_element_type=jnp.float32)
     chosen = jnp.take_along_axis(logits, ids, axis=1)
     score = jax.nn.sigmoid(chosen)
@@ -90,8 +90,8 @@
     table = router[0]
     up_w = w_up[0, 0]
     down_w = w_down[0, 0]
-    send_up, hi_up, lo_up = layer_route(up_in[0], up_ids[0], gain, table)
-    send_down, hi_down, lo_down = layer_route(down_in[0], down_ids[0], gain, table)
+    send_up, hi_up, lo_up = layer_route(up_in[0], up_ids, gain, table)
+    send_down, hi_down, lo_down = layer_route(down_in[0], down_ids, gain, table)
     rows_up = exchange(send_up)
     rows_down = exchange(send_down)
     back_up = exchange(apply_experts(rows_up, up_w, down_w))

time: 208 us -> 207 us (level)
    unnamed x24 -> x22, local copies, waits for them, and re-layouts: 5.1 us -> 3.2 us
where the time goes in v10:
time: 207 us; the launch traced here: 205 us
  waiting for transfers between devices  117 us (57%)
  matrix products  33.8 us (16%)
  starting transfers between devices  32.3 us (16%)
  local copies, waits for them, and re-layouts  11.5 us (6%)
  Pallas kernels  7.15 us (3%)
  other arithmetic  2.5 us (1%)
    all_to_all x4, waiting for transfers between devices, exchange(): lax.all_to_all(block, 'expert', split_axis=0, concat_axis=0, tiled=True)  102 us
    dot_general x2, matrix products, apply_experts(): jnp.dot(hidden, down_w, preferred_element_type=jnp.float32)  28.4 us
    all_to_all x4, starting transfers between devices, exchange(): lax.all_to_all(block, 'expert', split_axis=0, concat_axis=0, tiled=True)  20.7 us
    ppermute x2, waiting for transfers between devices, shifted(): return lax.ppermute(block, axis, route)  14.9 us
    ppermute x2, starting transfers between devices, shifted(): return lax.ppermute(block, axis, route)  11.5 us
    pallas_call x2, Pallas kernels, dispatch(): pl.pallas_call(dispatch_kernel, out_shape=(jax.ShapeDtypeStruct((rows, wi...  7.15 us
    gather x10, local copies, waits for them, and re-layouts, layer_route(): chosen = jnp.take_along_axis(logits, ids, axis=1)  6.87 us
  transfers between devices with their start and end apart: 6, of which 5 were waited for; matrix products, arithmetic and copies ran while one was open for 22% of the time, Pallas kernels for 2%

profile of v10, /device:TPU:6, one launch (start us, length us, event | category | flops | bytes accessed | tf_op | source)
XLA Modules:
  0.0 204.6 jit_solution(13165858845657320701)
XLA Ops:
  0.6 3.6 %shard_map.96 = (bf16[512,2560]{1,0:T(8,128)(2,1)}, bf16[64,2560]{1,0:T(8,128)(2,1)}) custom-call(bf16[64,2560]{1,0:T(8,128)(2,1)} %bitcast.136, f32[1,2560]{1,0:T(1,128)} %gain_ref.3, s32[6,1,64]{2,1,0:T(1,128)} %bitcast.138), custom_call_target="tpu_custom_call" | custom-call | tf_op jit(solution)/shard_map/pallas_call | solution.py:33
  4.3 6.1 %all-to-all-start.2 = ((bf16[16,32,2560]{2,1,0:T(8,128)(2,1)}), bf16[16,32,2560]{2,1,0:T(8,128)(2,1)S(1)}, u32[]{:S(2)}, u32[]{:S(2)}) async-start(bf16[16,32,2560]{2,1,0:T(8,128)(2,1)} %bitcast.135), calls=%async_computation.2 | async-start | bytes 5242880 | tf_op jit(solution)/shard_map/all_to_all | solution.py:85
  10.4 3.5 %shard_map.95 = (bf16[512,2560]{1,0:T(8,128)(2,1)}, bf16[64,2560]{1,0:T(8,128)(2,1)}) custom-call(bf16[64,2560]{1,0:T(8,128)(2,1)} %bitcast.137, f32[1,2560]{1,0:T(1,128)} %gain_ref.3, s32[6,1,64]{2,1,0:T(1,128)} %bitcast.139), custom_call_target="tpu_custom_call" | custom-call | tf_op jit(solution)/shard_map/pallas_call | solution.py:33
  13.9 34.1 %all-to-all-done.2 = bf16[16,32,2560]{2,1,0:T(8,128)(2,1)S(1)} async-done(((bf16[16,32,2560]{2,1,0:T(8,128)(2,1)}), bf16[16,32,2560]{2,1,0:T(8,128)(2,1)S(1)}, u32[]{:S(2)}, u32[]{:S(2)}) %all-to-all-start.2) | async-done | bytes 2621472 | tf_op jit(solution)/shard_map/all_to_all | solution.py:85
  48.0 4.9 %all-to-all-start = ((bf16[16,32,2560]{2,1,0:T(8,128)(2,1)}), bf16[16,32,2560]{2,1,0:T(8,128)(2,1)}, u32[]{:S(2)}, u32[]{:S(2)}) async-start(bf16[16,32,2560]{2,1,0:T(8,128)(2,1)} %bitcast.133), calls=%async_computation | async-start | bytes 5242880 | tf_op jit(solution)/shard_map/all_to_all | solution.py:85
  52.9 13.8 %fusion.11 = bf16[512,2560]{1,0:T(8,128)(2,1)} fusion(bf16[1,1,1152,2560]{3,2,1,0:T(8,128)(2,1)} %param.17, bf16[512,2560]{1,0:T(8,128)(2,1)S(1)} %bitcast.132, bf16[1,1,2560,1152]{3,2,1,0:T(8,128)(2,1)} %param.16), kind=kOutput, calls=%fused_computation.11 | convolution fusion | flops 6044057600 | bytes 17039360 | tf_op jit(solution)/shard_map/dot_general | solution.py:74
  66.7 23.9 %all-to-all-done = bf16[16,32,2560]{2,1,0:T(8,128)(2,1)} async-done(((bf16[16,32,2560]{2,1,0:T(8,128)(2,1)}), bf16[16,32,2560]{2,1,0:T(8,128)(2,1)}, u32[]{:S(2)}, u32[]{:S(2)}) %all-to-all-start) | async-done | bytes 2621472 | tf_op jit(solution)/shard_map/all_to_all | solution.py:85
  90.6 4.9 %all-to-all-start.3 = ((bf16[16,32,2560]{2,1,0:T(8,128)(2,1)}), bf16[16,32,2560]{2,1,0:T(8,128)(2,1)S(1)}, u32[]{:S(2)}, u32[]{:S(2)}) async-start(bf16[16,32,2560]{2,1,0:T(8,128)(2,1)} %bitcast.134), calls=%async_computation.3 | async-start | bytes 5242880 | tf_op jit(solution)/shard_map/all_to_all | solution.py:85
  95.5 14.6 %fusion.8 = bf16[512,2560]{1,0:T(8,128)(2,1)} fusion(bf16[1,1,1152,2560]{3,2,1,0:T(8,128)(2,1)} %param.17, bf16[512,2560]{1,0:T(8,128)(2,1)} %bitcast.6, bf16[1,1,2560,1152]{3,2,1,0:T(8,128)(2,1)} %param.16), kind=kOutput, calls=%fused_computation.10 | convolution fusion | flops 6044057600 | bytes 17039360 | tf_op jit(solution)/shard_map/dot_general | solution.py:74
  110.1 23.1 %all-to-all-done.3 = bf16[16,32,2560]{2,1,0:T(8,128)(2,1)S(1)} async-done(((bf16[16,32,2560]{2,1,0:T(8,128)(2,1)}), bf16[16,32,2560]{2,1,0:T(8,128)(2,1)S(1)}, u32[]{:S(2)}, u32[]{:S(2)}) %all-to-all-start.3) | async-done | bytes 2621472 | tf_op jit(solution)/shard_map/all_to_all | solution.py:85
  133.1 1.5 copy-done.1
  134.6 4.9 %all-to-all-start.1 = ((bf16[16,32,2560]{2,1,0:T(8,128)(2,1)}), bf16[16,32,2560]{2,1,0:T(8,128)(2,1)S(1)}, u32[]{:S(2)}, u32[]{:S(2)}) async-start(bf16[16,32,2560]{2,1,0:T(8,128)(2,1)} %bitcast.131), calls=%async_computation.1 | async-start | bytes 5242880 | tf_op jit(solution)/shard_map/all_to_all | solution.py:85
  139.5 0.1 copy.34
  139.6 0.1 eq.82
  139.7 0.1 eq.78
  139.9 0.1 copy.40
  140.0 0.1 eq.93
  140.1 0.1 eq.89
  140.3 0.1 copy.44
  140.4 0.1 reshape.119
  140.5 0.1 copy.38
  140.6 0.1 reshape.114
  140.8 0.9 reduce-window.14
  141.7 0.2 slice_reduce_fusion.1
  141.9 0.1 fusion.45
  142.0 0.1 reshape.87
  142.2 0.9 reduce-window.16
  143.1 0.2 slice_reduce_fusion
  143.4 0.1 fusion.42
  143.5 0.1 reshape.89
  143.7 0.2 fusion.30
  143.9 3.0 %gather_fusion.1 = f32[384]{0:T(512)S(1)} fusion(f32[64,16]{0,1:T(8,128)S(1)} %fusion.30, s32[384]{0:T(512)S(1)} %reshape.119), kind=kCustom, calls=%fused_computation.1.clone | custom fusion | bytes 6144 | tf_op jit(solution)/shard_map/jit(take_along_axis)/gather | solution.py:53
  146.9 0.1 reshape.122
  147.1 0.2 fusion.32
  147.3 3.0 %gather_fusion = f32[384]{0:T(512)S(1)} fusion(f32[64,16]{0,1:T(8,128)S(1)} %fusion.32, s32[384]{0:T(512)S(1)} %reshape.114), kind=kCustom, calls=%fused_computation.clone | custom fusion | bytes 6144 | tf_op jit(solution)/shard_map/jit(take_along_axis)/gather | solution.py:53
  150.3 0.1 reshape.117
  150.6 0.2 select_reduce_fusion
  150.8 0.2 select_reduce_fusion.1
  151.0 2.5 %fusion.35 = f32[64,2560]{1,0:T(8,128)S(1)} fusion(bf16[512,2560]{1,0:T(8,128)(2,1)} %bitcast.129, f32[64,512]{1,0:T(8,128)S(1)} %select_reduce_fusion), kind=kOutput, calls=%fused_computation.35 | convolution fusion | flops 167804928 | bytes 3407872 | tf_op jit(solution)/shard_map/dot_general | solution.py:78
  153.6 1.3 fusion.21
  154.9 7.9 %collective-permute-start.1 = (bf16[1,64,2560]{2,1,0:T(8,128)(2,1)}, bf16[1,64,2560]{2,1,0:T(8,128)(2,1)S(1)}, u32[]{:S(2)}, u32[]{:S(2)}) collective-permute-start(bf16[1,64,2560]{2,1,0:T(8,128)(2,1)} %fusion.21), channel_id=1, source_target_pairs={{16,0},{32,16},{48,32},{64,48},{80,64},{96,80},{112,96},{128,112},... | collective-permute-start | bytes 983048 | tf_op jit(solution)/shard_map/ppermute | solution.py:43
  162.7 20.7 %all-to-all-done.1 = bf16[16,32,2560]{2,1,0:T(8,128)(2,1)S(1)} async-done(((bf16[16,32,2560]{2,1,0:T(8,128)(2,1)}), bf16[16,32,2560]{2,1,0:T(8,128)(2,1)S(1)}, u32[]{:S(2)}, u32[]{:S(2)}) %all-to-all-start.1) | async-done | bytes 2621472 | tf_op jit(solution)/shard_map/all_to_all | solution.py:85
  183.5 0.6 fusion.38
  184.1 0.6 fusion.20
  184.6 3.7 %collective-permute-start = (bf16[1,64,2560]{2,1,0:T(8,128)(2,1)S(1)}, bf16[1,64,2560]{2,1,0:T(8,128)(2,1)S(1)}, u32[]{:S(2)}, u32[]{:S(2)}) collective-permute-start(bf16[1,64,2560]{2,1,0:T(8,128)(2,1)S(1)} %fusion.20), channel_id=1, source_target_pairs={{240,0},{0,16},{16,32},{32,48},{48,64},{64,80},{80,96},{96,112},{1... | collective-permute-start | bytes 983048 | tf_op jit(solution)/shard_map/ppermute | solution.py:43
  188.3 14.9 %collective-permute-done = bf16[1,64,2560]{2,1,0:T(8,128)(2,1)S(1)} collective-permute-done((bf16[1,64,2560]{2,1,0:T(8,128)(2,1)S(1)}, bf16[1,64,2560]{2,1,0:T(8,128)(2,1)S(1)}, u32[]{:S(2)}, u32[]{:S(2)}) %collective-permute-start) | collective-permute-done | bytes 327712 | tf_op jit(solution)/shard_map/ppermute | solution.py:43
  203.2 0.7 copy.78
  203.9 0.7 copy.79
  (34 shorter events, 0.5 us)
Async XLA Ops:
  0.6 143.0 %copy-start = (bf16[1,2560,16]{1,2,0:T(8,128)(2,1)S(1)}, bf16[1,2560,16]{1,2,0:T(8,128)(2,1)}, u32[]{:S(2)}) copy-start(bf16[1,2560,16]{1,2,0:T(8,128)(2,1)} %param.15) | copy-start | bytes 245764
  4.3 43.8 %all-to-all-start.2 = ((bf16[16,32,2560]{2,1,0:T(8,128)(2,1)}), bf16[16,32,2560]{2,1,0:T(8,128)(2,1)S(1)}, u32[]{:S(2)}, u32[]{:S(2)}) async-start(bf16[16,32,2560]{2,1,0:T(8,128)(2,1)} %bitcast.135), calls=%async_computation.2 | async-start | bytes 5242880 | tf_op jit(solution)/shard_map/all_to_all | solution.py:85
  48.0 42.6 %all-to-all-start = ((bf16[16,32,2560]{2,1,0:T(8,128)(2,1)}), bf16[16,32,2560]{2,1,0:T(8,128)(2,1)}, u32[]{:S(2)}, u32[]{:S(2)}) async-start(bf16[16,32,2560]{2,1,0:T(8,128)(2,1)} %bitcast.133), calls=%async_computation | async-start | bytes 5242880 | tf_op jit(solution)/shard_map/all_to_all | solution.py:85
  90.6 42.5 %all-to-all-start.3 = ((bf16[16,32,2560]{2,1,0:T(8,128)(2,1)}), bf16[16,32,2560]{2,1,0:T(8,128)(2,1)S(1)}, u32[]{:S(2)}, u32[]{:S(2)}) async-start(bf16[16,32,2560]{2,1,0:T(8,128)(2,1)} %bitcast.134), calls=%async_computation.3 | async-start | bytes 5242880 | tf_op jit(solution)/shard_map/all_to_all | solution.py:85
  133.1 1.5 copy-start.1
  133.1 6.4 %copy-start.8 = (s32[1,64,6]{1,0,2:T(1,128)S(1)}, s32[1,64,6]{1,0,2:T(1,128)}, u32[]{:S(2)}) copy-start(s32[1,64,6]{1,0,2:T(1,128)} %param.12) | copy-start | bytes 4612
  133.1 6.8 %copy-start.7 = (s32[1,64,6]{1,0,2:T(1,128)S(1)}, s32[1,64,6]{1,0,2:T(1,128)}, u32[]{:S(2)}) copy-start(s32[1,64,6]{1,0,2:T(1,128)} %param.13) | copy-start | bytes 4612
  133.1 10.6 %copy-start.6 = (bf16[64,2560]{1,0:T(8,128)(2,1)S(1)}, bf16[64,2560]{1,0:T(8,128)(2,1)}, u32[]{:S(2)}) copy-start(bf16[64,2560]{1,0:T(8,128)(2,1)} %get-tuple-element.9) | copy-start | bytes 983044
  134.6 48.8 %all-to-all-start.1 = ((bf16[16,32,2560]{2,1,0:T(8,128)(2,1)}), bf16[16,32,2560]{2,1,0:T(8,128)(2,1)S(1)}, u32[]{:S(2)}, u32[]{:S(2)}) async-start(bf16[16,32,2560]{2,1,0:T(8,128)(2,1)} %bitcast.131), calls=%async_computation.1 | async-start | bytes 5242880 | tf_op jit(solution)/shard_map/all_to_all | solution.py:85
  143.9 3.2 %copy-start.5 = (bf16[64,2560]{1,0:T(8,128)(2,1)S(1)}, bf16[64,2560]{1,0:T(8,128)(2,1)}, u32[]{:S(2)}) copy-start(bf16[64,2560]{1,0:T(8,128)(2,1)} %get-tuple-element.7) | copy-start | bytes 983044
  150.3 3.3 %copy-start.3 = (bf16[1,64,2560]{2,1,0:T(8,128)(2,1)S(1)}, bf16[1,64,2560]{2,1,0:T(8,128)(2,1)}, u32[]{:S(2)}) copy-start(bf16[1,64,2560]{2,1,0:T(8,128)(2,1)} %param.11) | copy-start | bytes 983044
  150.5 3.1 %copy-start.2 = (bf16[16,32,2560]{2,1,0:T(8,128)(2,1)S(1)}, bf16[16,32,2560]{2,1,0:T(8,128)(2,1)}, u32[]{:S(2)}) copy-start(bf16[16,32,2560]{2,1,0:T(8,128)(2,1)} %copy-done.1) | copy-start | bytes 7864324
  154.9 29.2 %copy-start.4 = (bf16[1,64,2560]{2,1,0:T(8,128)(2,1)S(1)}, bf16[1,64,2560]{2,1,0:T(8,128)(2,1)}, u32[]{:S(2)}) copy-start(bf16[1,64,2560]{2,1,0:T(8,128)(2,1)} %param.10) | copy-start | bytes 983044
  154.9 33.4 %collective-permute-start.1 = (bf16[1,64,2560]{2,1,0:T(8,128)(2,1)}, bf16[1,64,2560]{2,1,0:T(8,128)(2,1)S(1)}, u32[]{:S(2)}, u32[]{:S(2)}) collective-permute-start(bf16[1,64,2560]{2,1,0:T(8,128)(2,1)} %fusion.21), channel_id=1, source_target_pairs={{16,0},{32,16},{48,32},{64,48},{80,64},{96,80},{112,96},{128,112},... | collective-permute-start | bytes 983048 | tf_op jit(solution)/shard_map/ppermute | solution.py:43
  184.6 18.6 %collective-permute-start = (bf16[1,64,2560]{2,1,0:T(8,128)(2,1)S(1)}, bf16[1,64,2560]{2,1,0:T(8,128)(2,1)S(1)}, u32[]{:S(2)}, u32[]{:S(2)}) collective-permute-start(bf16[1,64,2560]{2,1,0:T(8,128)(2,1)S(1)} %fusion.20), channel_id=1, source_target_pairs={{240,0},{0,16},{16,32},{32,48},{48,64},{64,80},{80,96},{96,112},{1... | collective-permute-start | bytes 983048 | tf_op jit(solution)/shard_map/ppermute | solution.py:43

commit v11 on v10

--- a/solution.py
+++ b/solution.py
@@ -75,9 +75,12 @@
 
 
 def finish(x, weight_hi, weight_lo, returned):
-    combined = jnp.dot(weight_hi, returned, preferred_element_type=jnp.float32) + jnp.dot(
-        weight_lo, returned, preferred_element_type=jnp.float32
+    tokens_here = weight_hi.shape[0]
+    both = jnp.dot(
+        jnp.concatenate([weight_hi, weight_lo], axis=0), returned,
+        preferred_element_type=jnp.float32,
     )
+    combined = both[:tokens_here] + both[tokens_here:]
     return (x.astype(jnp.float32) + 2.5 * combined).astype(jnp.bfloat16)
 
 

time: 207 us -> 206 us (level)
  matrix products: 33.8 us -> 31.6 us
    dot_general x4 -> x2, matrix products: 4.98 us -> 2.76 us  [finish(): jnp.dot(jnp.concatenate([weight_hi, weight_lo], axis=0), returned, prefer...]
  transfers between devices with their start and end apart: 6 -> 6, of which waited for: 5 -> 5; matrix products, arithmetic and copies ran while one was open for 22% -> 21% of each run, Pallas kernels for 2% -> 2%
where the time goes in v11:
time: 206 us; the launch traced here: 204 us
  waiting for transfers between devices  118 us (57%)
  starting transfers between devices  32.1 us (16%)
  matrix products  31.6 us (15%)
  local copies, waits for them, and re-layouts  11.5 us (6%)
  Pallas kernels  7.15 us (3%)
  other arithmetic  3.46 us (2%)
    all_to_all x4, waiting for transfers between devices, exchange(): lax.all_to_all(block, 'expert', split_axis=0, concat_axis=0, tiled=True)  102 us
    dot_general x2, matrix products, apply_experts(): jnp.dot(hidden, down_w, preferred_element_type=jnp.float32)  28.4 us
    all_to_all x4, starting transfers between devices, exchange(): lax.all_to_all(block, 'expert', split_axis=0, concat_axis=0, tiled=True)  20.7 us
    ppermute x2, waiting for transfers between devices, shifted(): return lax.ppermute(block, axis, route)  15.3 us
    ppermute x2, starting transfers between devices, shifted(): return lax.ppermute(block, axis, route)  11.4 us
    pallas_call x2, Pallas kernels, dispatch(): pl.pallas_call(dispatch_kernel, out_shape=(jax.ShapeDtypeStruct((rows, wi...  7.15 us
    gather x10, local copies, waits for them, and re-layouts, layer_route(): chosen = jnp.take_along_axis(logits, ids, axis=1)  6.87 us
  transfers between devices with their start and end apart: 6, of which 5 were waited for; matrix products, arithmetic and copies ran while one was open for 21% of the time, Pallas kernels for 2%

profile of v11, /device:TPU:6, one launch (start us, length us, event | category | flops | bytes accessed | tf_op | source)
XLA Modules:
  0.0 204.1 jit_solution(4983326240892780793)
XLA Ops:
  0.6 3.6 %shard_map.96 = (bf16[512,2560]{1,0:T(8,128)(2,1)}, bf16[64,2560]{1,0:T(8,128)(2,1)}) custom-call(bf16[64,2560]{1,0:T(8,128)(2,1)} %bitcast.132, f32[1,2560]{1,0:T(1,128)} %gain_ref.3, s32[6,1,64]{2,1,0:T(1,128)} %bitcast.134), custom_call_target="tpu_custom_call" | custom-call | tf_op jit(solution)/shard_map/pallas_call | solution.py:33
  4.3 6.1 %all-to-all-start.2 = ((bf16[16,32,2560]{2,1,0:T(8,128)(2,1)}), bf16[16,32,2560]{2,1,0:T(8,128)(2,1)S(1)}, u32[]{:S(2)}, u32[]{:S(2)}) async-start(bf16[16,32,2560]{2,1,0:T(8,128)(2,1)} %bitcast.131), calls=%async_computation.2 | async-start | bytes 5242880 | tf_op jit(solution)/shard_map/all_to_all | solution.py:88
  10.4 3.5 %shard_map.95 = (bf16[512,2560]{1,0:T(8,128)(2,1)}, bf16[64,2560]{1,0:T(8,128)(2,1)}) custom-call(bf16[64,2560]{1,0:T(8,128)(2,1)} %bitcast.133, f32[1,2560]{1,0:T(1,128)} %gain_ref.3, s32[6,1,64]{2,1,0:T(1,128)} %bitcast.135), custom_call_target="tpu_custom_call" | custom-call | tf_op jit(solution)/shard_map/pallas_call | solution.py:33
  13.9 34.1 %all-to-all-done.2 = bf16[16,32,2560]{2,1,0:T(8,128)(2,1)S(1)} async-done(((bf16[16,32,2560]{2,1,0:T(8,128)(2,1)}), bf16[16,32,2560]{2,1,0:T(8,128)(2,1)S(1)}, u32[]{:S(2)}, u32[]{:S(2)}) %all-to-all-start.2) | async-done | bytes 2621472 | tf_op jit(solution)/shard_map/all_to_all | solution.py:88
  48.0 4.9 %all-to-all-start = ((bf16[16,32,2560]{2,1,0:T(8,128)(2,1)}), bf16[16,32,2560]{2,1,0:T(8,128)(2,1)}, u32[]{:S(2)}, u32[]{:S(2)}) async-start(bf16[16,32,2560]{2,1,0:T(8,128)(2,1)} %bitcast.129), calls=%async_computation | async-start | bytes 5242880 | tf_op jit(solution)/shard_map/all_to_all | solution.py:88
  52.9 13.8 %fusion.11 = bf16[512,2560]{1,0:T(8,128)(2,1)} fusion(bf16[1,1,1152,2560]{3,2,1,0:T(8,128)(2,1)} %param.17, bf16[512,2560]{1,0:T(8,128)(2,1)S(1)} %bitcast.128, bf16[1,1,2560,1152]{3,2,1,0:T(8,128)(2,1)} %param.16), kind=kOutput, calls=%fused_computation.11 | convolution fusion | flops 6044057600 | bytes 17039360 | tf_op jit(solution)/shard_map/dot_general | solution.py:74
  66.7 23.9 %all-to-all-done = bf16[16,32,2560]{2,1,0:T(8,128)(2,1)} async-done(((bf16[16,32,2560]{2,1,0:T(8,128)(2,1)}), bf16[16,32,2560]{2,1,0:T(8,128)(2,1)}, u32[]{:S(2)}, u32[]{:S(2)}) %all-to-all-start) | async-done | bytes 2621472 | tf_op jit(solution)/shard_map/all_to_all | solution.py:88
  90.6 4.9 %all-to-all-start.3 = ((bf16[16,32,2560]{2,1,0:T(8,128)(2,1)}), bf16[16,32,2560]{2,1,0:T(8,128)(2,1)S(1)}, u32[]{:S(2)}, u32[]{:S(2)}) async-start(bf16[16,32,2560]{2,1,0:T(8,128)(2,1)} %bitcast.130), calls=%async_computation.3 | async-start | bytes 5242880 | tf_op jit(solution)/shard_map/all_to_all | solution.py:88
  95.5 14.6 %fusion.8 = bf16[512,2560]{1,0:T(8,128)(2,1)} fusion(bf16[1,1,1152,2560]{3,2,1,0:T(8,128)(2,1)} %param.17, bf16[512,2560]{1,0:T(8,128)(2,1)} %bitcast.6, bf16[1,1,2560,1152]{3,2,1,0:T(8,128)(2,1)} %param.16), kind=kOutput, calls=%fused_computation.10 | convolution fusion | flops 6044057600 | bytes 17039360 | tf_op jit(solution)/shard_map/dot_general | solution.py:74
  110.1 23.1 %all-to-all-done.3 = bf16[16,32,2560]{2,1,0:T(8,128)(2,1)S(1)} async-done(((bf16[16,32,2560]{2,1,0:T(8,128)(2,1)}), bf16[16,32,2560]{2,1,0:T(8,128)(2,1)S(1)}, u32[]{:S(2)}, u32[]{:S(2)}) %all-to-all-start.3) | async-done | bytes 2621472 | tf_op jit(solution)/shard_map/all_to_all | solution.py:88
  133.1 1.5 copy-done.1
  134.6 4.9 %all-to-all-start.1 = ((bf16[16,32,2560]{2,1,0:T(8,128)(2,1)}), bf16[16,32,2560]{2,1,0:T(8,128)(2,1)S(1)}, u32[]{:S(2)}, u32[]{:S(2)}) async-start(bf16[16,32,2560]{2,1,0:T(8,128)(2,1)} %bitcast.127), calls=%async_computation.1 | async-start | bytes 5242880 | tf_op jit(solution)/shard_map/all_to_all | solution.py:88
  139.5 0.1 copy.34
  139.6 0.1 eq.82
  139.7 0.1 eq.78
  139.9 0.1 copy.40
  140.0 0.1 eq.93
  140.1 0.1 eq.89
  140.3 0.1 copy.44
  140.4 0.1 reshape.119
  140.5 0.1 copy.38
  140.6 0.1 reshape.114
  140.8 0.9 reduce-window.14
  141.7 0.2 slice_reduce_fusion.1
  141.9 0.1 fusion.47
  142.0 0.1 reshape.87
  142.2 0.9 reduce-window.16
  143.1 0.2 slice_reduce_fusion
  143.4 0.1 fusion.44
  143.5 0.1 reshape.89
  143.7 0.2 fusion.38
  143.9 3.0 %gather_fusion.1 = f32[384]{0:T(512)S(1)} fusion(f32[64,16]{0,1:T(8,128)S(1)} %fusion.38, s32[384]{0:T(512)S(1)} %reshape.119), kind=kCustom, calls=%fused_computation.1.clone | custom fusion | bytes 6144 | tf_op jit(solution)/shard_map/jit(take_along_axis)/gather | solution.py:53
  146.9 0.1 reshape.122
  147.1 0.2 fusion.40
  147.3 3.0 %gather_fusion = f32[384]{0:T(512)S(1)} fusion(f32[64,16]{0,1:T(8,128)S(1)} %fusion.40, s32[384]{0:T(512)S(1)} %reshape.114), kind=kCustom, calls=%fused_computation.clone | custom fusion | bytes 6144 | tf_op jit(solution)/shard_map/jit(take_along_axis)/gather | solution.py:53
  150.3 0.1 reshape.117
  150.6 0.2 select_reduce_fusion
  150.8 0.2 select_reduce_fusion.1
  151.1 2.2 %fusion.34 = f32[128,2560]{1,0:T(8,128)S(1)} fusion(bf16[512,2560]{1,0:T(8,128)(2,1)} %bitcast.126, bf16[64,512]{1,0:T(8,128)(2,1)S(1)} %get-tuple-element.11, bf16[64,512]{1,0:T(8,128)(2,1)S(1)} %get-tuple-element.12), kind=kOutput, calls=%fused_computation.32 | convolution fusion | flops 335806464 | bytes 4063232 | tf_op jit(solution)/shard_map/dot_general | solution.py:79
  153.3 0.8 fusion.29
  154.2 7.9 %collective-permute-start.1 = (bf16[1,64,2560]{2,1,0:T(8,128)(2,1)}, bf16[1,64,2560]{2,1,0:T(8,128)(2,1)S(1)}, u32[]{:S(2)}, u32[]{:S(2)}) collective-permute-start(bf16[1,64,2560]{2,1,0:T(8,128)(2,1)} %fusion.29), channel_id=1, source_target_pairs={{16,0},{32,16},{48,32},{64,48},{80,64},{96,80},{112,96},{128,112},... | collective-permute-start | bytes 983048 | tf_op jit(solution)/shard_map/ppermute | solution.py:43
  162.0 21.2 %all-to-all-done.1 = bf16[16,32,2560]{2,1,0:T(8,128)(2,1)S(1)} async-done(((bf16[16,32,2560]{2,1,0:T(8,128)(2,1)}), bf16[16,32,2560]{2,1,0:T(8,128)(2,1)S(1)}, u32[]{:S(2)}, u32[]{:S(2)}) %all-to-all-start.1) | async-done | bytes 2621472 | tf_op jit(solution)/shard_map/all_to_all | solution.py:88
  183.2 0.5 fusion.30
  183.8 0.1 fusion.28
  183.9 3.5 %collective-permute-start = (bf16[1,64,2560]{2,1,0:T(8,128)(2,1)S(1)}, bf16[1,64,2560]{2,1,0:T(8,128)(2,1)S(1)}, u32[]{:S(2)}, u32[]{:S(2)}) collective-permute-start(bf16[1,64,2560]{2,1,0:T(8,128)(2,1)S(1)} %fusion.28), channel_id=1, source_target_pairs={{240,0},{0,16},{16,32},{32,48},{48,64},{64,80},{80,96},{96,112},{1... | collective-permute-start | bytes 983048 | tf_op jit(solution)/shard_map/ppermute | solution.py:43
  187.4 15.3 %collective-permute-done = bf16[1,64,2560]{2,1,0:T(8,128)(2,1)S(1)} collective-permute-done((bf16[1,64,2560]{2,1,0:T(8,128)(2,1)S(1)}, bf16[1,64,2560]{2,1,0:T(8,128)(2,1)S(1)}, u32[]{:S(2)}, u32[]{:S(2)}) %collective-permute-start) | collective-permute-done | bytes 327712 | tf_op jit(solution)/shard_map/ppermute | solution.py:43
  202.7 0.7 copy.78
  203.4 0.7 copy.79
  (34 shorter events, 0.6 us)
Async XLA Ops:
  0.6 143.0 %copy-start = (bf16[1,2560,16]{1,2,0:T(8,128)(2,1)S(1)}, bf16[1,2560,16]{1,2,0:T(8,128)(2,1)}, u32[]{:S(2)}) copy-start(bf16[1,2560,16]{1,2,0:T(8,128)(2,1)} %param.15) | copy-start | bytes 245764
  4.3 43.8 %all-to-all-start.2 = ((bf16[16,32,2560]{2,1,0:T(8,128)(2,1)}), bf16[16,32,2560]{2,1,0:T(8,128)(2,1)S(1)}, u32[]{:S(2)}, u32[]{:S(2)}) async-start(bf16[16,32,2560]{2,1,0:T(8,128)(2,1)} %bitcast.131), calls=%async_computation.2 | async-start | bytes 5242880 | tf_op jit(solution)/shard_map/all_to_all | solution.py:88
  48.0 42.6 %all-to-all-start = ((bf16[16,32,2560]{2,1,0:T(8,128)(2,1)}), bf16[16,32,2560]{2,1,0:T(8,128)(2,1)}, u32[]{:S(2)}, u32[]{:S(2)}) async-start(bf16[16,32,2560]{2,1,0:T(8,128)(2,1)} %bitcast.129), calls=%async_computation | async-start | bytes 5242880 | tf_op jit(solution)/shard_map/all_to_all | solution.py:88
  90.6 42.5 %all-to-all-start.3 = ((bf16[16,32,2560]{2,1,0:T(8,128)(2,1)}), bf16[16,32,2560]{2,1,0:T(8,128)(2,1)S(1)}, u32[]{:S(2)}, u32[]{:S(2)}) async-start(bf16[16,32,2560]{2,1,0:T(8,128)(2,1)} %bitcast.130), calls=%async_computation.3 | async-start | bytes 5242880 | tf_op jit(solution)/shard_map/all_to_all | solution.py:88
  133.1 1.5 copy-start.1
  133.1 6.4 %copy-start.7 = (s32[1,64,6]{1,0,2:T(1,128)S(1)}, s32[1,64,6]{1,0,2:T(1,128)}, u32[]{:S(2)}) copy-start(s32[1,64,6]{1,0,2:T(1,128)} %param.12) | copy-start | bytes 4612
  133.1 6.8 %copy-start.6 = (s32[1,64,6]{1,0,2:T(1,128)S(1)}, s32[1,64,6]{1,0,2:T(1,128)}, u32[]{:S(2)}) copy-start(s32[1,64,6]{1,0,2:T(1,128)} %param.13) | copy-start | bytes 4612
  133.1 10.6 %copy-start.5 = (bf16[64,2560]{1,0:T(8,128)(2,1)S(1)}, bf16[64,2560]{1,0:T(8,128)(2,1)}, u32[]{:S(2)}) copy-start(bf16[64,2560]{1,0:T(8,128)(2,1)} %get-tuple-element.9) | copy-start | bytes 983044
  134.6 48.6 %all-to-all-start.1 = ((bf16[16,32,2560]{2,1,0:T(8,128)(2,1)}), bf16[16,32,2560]{2,1,0:T(8,128)(2,1)S(1)}, u32[]{:S(2)}, u32[]{:S(2)}) async-start(bf16[16,32,2560]{2,1,0:T(8,128)(2,1)} %bitcast.127), calls=%async_computation.1 | async-start | bytes 5242880 | tf_op jit(solution)/shard_map/all_to_all | solution.py:88
  143.9 3.2 %copy-start.4 = (bf16[64,2560]{1,0:T(8,128)(2,1)S(1)}, bf16[64,2560]{1,0:T(8,128)(2,1)}, u32[]{:S(2)}) copy-start(bf16[64,2560]{1,0:T(8,128)(2,1)} %get-tuple-element.7) | copy-start | bytes 983044
  150.3 3.0 %copy-start.2 = (bf16[1,64,2560]{2,1,0:T(8,128)(2,1)S(1)}, bf16[1,64,2560]{2,1,0:T(8,128)(2,1)}, u32[]{:S(2)}) copy-start(bf16[1,64,2560]{2,1,0:T(8,128)(2,1)} %param.11) | copy-start | bytes 983044
  153.3 30.4 %copy-start.3 = (bf16[1,64,2560]{2,1,0:T(8,128)(2,1)S(1)}, bf16[1,64,2560]{2,1,0:T(8,128)(2,1)}, u32[]{:S(2)}) copy-start(bf16[1,64,2560]{2,1,0:T(8,128)(2,1)} %param.10) | copy-start | bytes 983044
  154.2 33.3 %collective-permute-start.1 = (bf16[1,64,2560]{2,1,0:T(8,128)(2,1)}, bf16[1,64,2560]{2,1,0:T(8,128)(2,1)S(1)}, u32[]{:S(2)}, u32[]{:S(2)}) collective-permute-start(bf16[1,64,2560]{2,1,0:T(8,128)(2,1)} %fusion.29), channel_id=1, source_target_pairs={{16,0},{32,16},{48,32},{64,48},{80,64},{96,80},{112,96},{128,112},... | collective-permute-start | bytes 983048 | tf_op jit(solution)/shard_map/ppermute | solution.py:43
  183.9 18.8 %collective-permute-start = (bf16[1,64,2560]{2,1,0:T(8,128)(2,1)S(1)}, bf16[1,64,2560]{2,1,0:T(8,128)(2,1)S(1)}, u32[]{:S(2)}, u32[]{:S(2)}) collective-permute-start(bf16[1,64,2560]{2,1,0:T(8,128)(2,1)S(1)} %fusion.28), channel_id=1, source_target_pairs={{240,0},{0,16},{16,32},{32,48},{48,64},{64,80},{80,96},{96,112},{1... | collective-permute-start | bytes 983048 | tf_op jit(solution)/shard_map/ppermute | solution.py:43
